TPU v7x, 32 devices: a whole 2x2x4 slice. The times are simulated.
32 devices in a mesh: ind: 8 (over z, x), var: 4 (over y, core).
Axes of the slice: x: 2, y: 2, z: 4, core: 2. Of those that a mesh axis runs over, the one named last changes fastest.
Arguments:
- genotypes: float32 [256, 16384], P('var', 'ind'), may hold values from -30 to 30
- variance_comp: float32 [2], replicated, may hold values from 0.5 to 1.5
- grm_tiles: bfloat16 [80, 512, 512], P('ind'), may hold values from -1 to 6, as said below
- tile_rows: int32 [80], P('ind'), may hold values from 0 to 3, as said below
- tile_cols: int32 [80], P('ind'), may hold values from 0 to 31, as said below
- tile_live: int32 [8], P('ind'), may hold values from 5 to 10, as said below
Outputs:
- solution: float32 [256, 16384], P('var', 'ind')
- gene_gram: float32 [256, 4], P('var')
Inputs may be any that keep to these rules, and one draw needn't show every extreme that they name: `grm_tiles`: every diagonal tile is symmetric, and the tiles of two live slots that form a transposed pair are transposes of each other, so K is symmetric. Slots r < 4 of each index i of ind hold its diagonal tiles: tile_rows = r and tile_cols = i * 4 + r. `tile_cols`: every other slot of index i names a column tile j * 4 + ((i + t) mod 4) of another index j != i, with t < 2. Live off slots come in transposed pairs: a live slot of i at row tile r naming column tile j * 4 + u goes with a live slot of j at row tile u naming column tile i * 4 + r. Some index uses 2 distinct column tiles of one other index. `tile_live`: some index of ind uses all 10 slots.
All inputs are finite; a program needn't handle non-finite values.
Results may differ from a plain program's by a relative error of at most 0.0003.
Values sent between devices are 32-bit elements; how exact they have to be, the bound alone decides.
No kernel may reach another device: no remote copies, remote signals or barrier semaphores. Data moves between devices by JAX's collectives and lax.ppermute only.
A program may use at most 192 MiB of HBM per device.

v0:
```python
import jax
import jax.numpy as jnp
from jax import lax
from jax.sharding import PartitionSpec as P

VARS_GENE = 4
GENES = 64
ITERS = 2
NEED = 2


def local(genotypes, variance_comp, grm_tiles, tile_rows, tile_cols, tile_live):
    cols_here, rows_here = genotypes.shape
    tile_size = grm_tiles.shape[1]
    slot_count = grm_tiles.shape[0]
    row_tiles = rows_here // tile_size
    my_index = lax.axis_index("ind")
    peer_count = lax.axis_size("ind")
    tau_noise = variance_comp[0]
    tau_kin = variance_comp[1]
    live_count = tile_live[0]
    diag_tiles = grm_tiles[:row_tiles]
    off_tiles = grm_tiles[row_tiles:]
    diag_values = jnp.diagonal(diag_tiles, axis1=1, axis2=2).astype(jnp.float32).reshape(rows_here)
    precond = tau_noise + tau_kin * diag_values
    off_rows = tile_rows[row_tiles:]
    off_cols = tile_cols[row_tiles:]
    live_mask = (jnp.arange(row_tiles, slot_count, dtype=jnp.int32) < live_count).astype(
        jnp.float32
    )
    onehot = (off_rows[:, None] == jnp.arange(row_tiles, dtype=jnp.int32)[None, :]).astype(
        jnp.float32
    )
    onehot = onehot * live_mask[:, None]
    solution = jnp.zeros_like(genotypes)
    resid = genotypes
    scaled = resid / precond[None, :]
    direction = scaled
    rz_now = lax.psum(jnp.sum(resid * scaled, axis=1), "ind")
    for rounds in range(ITERS):
        pieces = direction.reshape(cols_here, row_tiles, tile_size)
        table = (
            jnp.arange(peer_count, dtype=jnp.int32)[:, None]
            + jnp.arange(NEED, dtype=jnp.int32)[None, :]
        ) % row_tiles
        outgoing = pieces[:, table]
        arrived = lax.all_to_all(outgoing, "ind", split_axis=1, concat_axis=1, tiled=True)
        flat = arrived.reshape(cols_here, peer_count * NEED, tile_size)
        position = off_cols // row_tiles * NEED + (off_cols % row_tiles - my_index) % row_tiles
        position = jnp.clip(position, 0, peer_count * NEED - 1)
        picked = jnp.take(flat, position, axis=1)
        apply_pieces = direction.reshape(cols_here, row_tiles, tile_size)
        near = jnp.einsum(
            "crk,rqk->crq",
            apply_pieces,
            diag_tiles,
            precision=lax.Precision.HIGHEST,
            preferred_element_type=jnp.float32,
        )
        far = jnp.einsum(
            "csk,sqk->csq",
            picked,
            off_tiles,
            precision=lax.Precision.HIGHEST,
            preferred_element_type=jnp.float32,
        )
        far = jnp.einsum("csq,sr->crq", far, onehot, precision=lax.Precision.HIGHEST)
        image = tau_noise * direction + tau_kin * (near + far).reshape(cols_here, rows_here)
        alpha = rz_now / lax.psum(jnp.sum(direction * image, axis=1), "ind")
        solution = solution + alpha[:, None] * direction
        resid = resid - alpha[:, None] * image
        if rounds + 1 < ITERS:
            scaled = resid / precond[None, :]
            rz_next = lax.psum(jnp.sum(resid * scaled, axis=1), "ind")
            direction = scaled + (rz_next / rz_now)[:, None] * direction
            rz_now = rz_next
    var_index = lax.axis_index("var")
    gathered = lax.all_gather(solution, "var", axis=0, tiled=True)
    split_cols = gathered.reshape(VARS_GENE, GENES, rows_here)
    first_gene = var_index * cols_here % GENES
    matching = lax.dynamic_slice_in_dim(split_cols, first_gene, cols_here, 1)
    partial_gram = jnp.einsum("jn,bjn->jb", genotypes, matching, precision=lax.Precision.HIGHEST)
    total_gram = lax.psum(partial_gram, "ind")
    gene_gram = total_gram / (peer_count * rows_here)
    return (solution, gene_gram)


def solution(mesh):
    placed = (P("var", "ind"), P(), P("ind", None, None), P("ind"), P("ind"), P("ind"))
    return jax.shard_map(
        local,
        mesh=mesh,
        in_specs=placed,
        out_specs=(P("var", "ind"), P("var", None)),
        check_vma=False,
    )
```

profile of v0, /device:TPU:0, one launch (start us, length us, event | category | flops | bytes accessed | tf_op | source)
XLA Modules:
  0.0 310.4 jit_solution(10890623376764823809)
XLA Ops:
  7.2 1.6 slice-done
  8.8 41.5 %copy.31 = bf16[4,512,512]{0,2,1:T(8,128)(2,1)} copy(bf16[4,512,512]{2,1,0:T(8,128)(2,1)S(1)} %slice-done) | data formatting | bytes 4194304 | tf_op jit(solution)/shard_map/slice | solution.py:22
  50.9 6.5 %gather_fusion = bf16[512,4]{1,0:T(8,128)(2,1)S(1)} fusion(bf16[4,512,512]{0,2,1:T(8,128)(2,1)} %copy.31, s32[512]{0:T(512)S(1)} %bitcast.54), kind=kCustom, calls=%fused_computation.2 | custom fusion | bytes 12288 | tf_op jit(solution)/shard_map/jit(diagonal)/gather | solution.py:24
  57.4 1.3 multiply_add_fusion.3
  59.0 2.0 gather_fusion.1
  61.1 7.4 %all-to-all-start = ((f32[64,8,2,512]{3,0,2,1:T(8,128)}), f32[64,8,2,512]{3,0,2,1:T(8,128)S(1)}, u32[]{:S(2)}, u32[]{:S(2)}) async-start(f32[64,8,2,512]{3,0,2,1:T(8,128)} %bitcast.60), calls=%async_computation | async-start | bytes 4194304 | tf_op jit(solution)/shard_map/all_to_all | solution.py:47
  69.4 47.3 %all-to-all-done = f32[64,8,2,512]{3,0,2,1:T(8,128)S(1)} async-done(((f32[64,8,2,512]{3,0,2,1:T(8,128)}), f32[64,8,2,512]{3,0,2,1:T(8,128)S(1)}, u32[]{:S(2)}, u32[]{:S(2)}) %all-to-all-start) | async-done | bytes 2097184 | tf_op jit(solution)/shard_map/all_to_all | solution.py:47
  116.7 1.5 gather_fusion.3
  118.2 5.1 %fusion.6 = f32[64,6,512]{2,0,1:T(8,128)S(1)} fusion(bf16[10,512,512]{2,1,0:T(8,128)(2,1)} %param.10, f32[6,64,512]{2,1,0:T(8,128)} %gather_fusion.3, pred[6]{0:T(512)(128)(4,1)S(1)} %get-tuple-element.7), kind=kOutput, calls=%fused_computation.11 | convolution fusion | flops 1208156160 | bytes 4718598 | tf_op jit(solution)/shard_map/csk,sqk->csq/dot_general | solution.py:60
  123.3 1.4 fusion.18
  124.7 4.3 %fusion.15 = f32[4,8,8,512]{3,2,1,0:T(8,128)S(1)} fusion(f32[4,64,512]{2,0,1:T(4,128)S(1)} %fusion.18, f32[]{:T(128)} %bitcast.1, f32[8,4,8,512]{3,2,1,0:T(8,128)S(1)} %bitcast.68, bf16[10,512,512]{2,1,0:T(8,128)(2,1)} %param.10), kind=kOutput, calls=%fused_computation.18 | convolution fusion | flops 805568512 | bytes 3670528 | tf_op jit(solution)/shard_map/crk,rqk->crq/dot_general | solution.py:53
  129.9 19.5 %all-reduce = (f32[64]{0:T(128)S(1)}, f32[64]{0:T(128)S(1)}) all-reduce(f32[64]{0:T(128)S(1)} %get-tuple-element.4, f32[64]{0:T(128)S(1)} %get-tuple-element.3), channel_id=1, replica_groups=mesh['ind'=8,'var'=4] {'ind'}, use_global_device_ids=true, to_apply=%region_1.2 | all-reduce | flops 128 | bytes 1024 | tf_op jit(solution)/shard_map/psum | solution.py:39
  149.4 0.9 multiply_reduce_fusion.1
  150.3 17.1 %psum.37 = f32[64]{0:T(128)S(1)} all-reduce(f32[64]{0:T(128)S(1)} %multiply_reduce_fusion.1), channel_id=1, replica_groups=mesh['ind'=8,'var'=4] {'ind'}, use_global_device_ids=true, to_apply=%region_5.7 | all-reduce | flops 64 | bytes 512 | tf_op jit(solution)/shard_map/psum | solution.py:74
  168.4 2.0 gather_fusion.2
  170.4 45.8 %all_to_all.10 = f32[64,8,2,512]{3,0,2,1:T(8,128)} all-to-all(f32[64,8,2,512]{3,0,2,1:T(8,128)} %bitcast.61), channel_id=1, replica_groups=mesh['ind'=8,'var'=4] {'ind'}, dimensions={1} | all-to-all | bytes 4194304 | tf_op jit(solution)/shard_map/all_to_all | solution.py:47
  216.2 2.2 gather_fusion.4
  218.4 4.9 %fusion.9 = f32[64,6,512]{2,0,1:T(8,128)S(1)} fusion(bf16[10,512,512]{2,1,0:T(8,128)(2,1)} %param.10, f32[6,64,512]{2,1,0:T(8,128)S(1)} %gather_fusion.4, pred[6]{0:T(512)(128)(4,1)S(1)} %get-tuple-element.7), kind=kOutput, calls=%fused_computation.12 | convolution fusion | flops 1208156160 | bytes 4718598 | tf_op jit(solution)/shard_map/csk,sqk->csq/dot_general | solution.py:60
  223.3 1.4 fusion.16
  224.7 4.3 %fusion.13 = f32[4,8,8,512]{3,2,1,0:T(8,128)S(1)} fusion(f32[4,64,512]{2,0,1:T(4,128)S(1)} %fusion.16, f32[]{:T(128)} %bitcast.1, f32[8,4,8,512]{3,2,1,0:T(8,128)S(1)} %bitcast.57, bf16[10,512,512]{2,1,0:T(8,128)(2,1)} %param.10), kind=kOutput, calls=%fused_computation.15 | convolution fusion | flops 805568512 | bytes 3670528 | tf_op jit(solution)/shard_map/crk,rqk->crq/dot_general | solution.py:53
  229.8 19.4 %psum.38 = f32[64]{0:T(128)S(1)} all-reduce(f32[64]{0:T(128)S(1)} %multiply_reduce_fusion), channel_id=1, replica_groups=mesh['ind'=8,'var'=4] {'ind'}, use_global_device_ids=true, to_apply=%region_7.9 | all-reduce | flops 64 | bytes 512 | tf_op jit(solution)/shard_map/psum | solution.py:69
  250.2 20.1 %all-gather.2.cloned.1.call-done = f32[256,2048]{1,0:T(8,128)} async-done(((f32[64,2048]{1,0:T(8,128)}), f32[256,2048]{1,0:T(8,128)}) %all-gather.2.cloned.1.call-update) | async-done | bytes 2097168 | tf_op jit(solution)/shard_map/all_gather | solution.py:78
  270.3 11.3 %fusion.4 = f32[64,1,4]{2,1,0:T(1,128)S(1)} fusion(f32[4,64,2048]{2,1,0:T(8,128)} %bitcast.77, f32[64,2048,1]{1,0,2:T(8,128)S(1)} %bitcast.55), kind=kOutput, calls=%fused_computation.9 | convolution fusion | flops 6291456 | bytes 2622464 | tf_op jit(solution)/shard_map/jn,bjn->jb/dot_general | solution.py:82
  281.6 21.4 %psum.39 = f32[64,4]{0,1:T(4,128)S(1)} all-reduce(f32[64,4]{0,1:T(4,128)S(1)} %bitcast.76), channel_id=1, replica_groups=mesh['ind'=8,'var'=4] {'ind'}, use_global_device_ids=true, to_apply=%region_8.10 | all-reduce | flops 256 | bytes 2048 | tf_op jit(solution)/shard_map/psum | solution.py:83
  (36 shorter events, 5.4 us)
Async XLA Ops:
  7.2 1.6 slice-start
  8.8 41.5 %copy-start.1 = (f32[2]{0:T(128)S(1)}, f32[2]{0:T(128)}, u32[]{:S(2)}) copy-start(f32[2]{0:T(128)} %param.9) | copy-start | bytes 28
  8.8 50.0 %copy-start = (f32[64,2048]{1,0:T(8,128)S(1)}, f32[64,2048]{1,0:T(8,128)}, u32[]{:S(2)}) copy-start(f32[64,2048]{1,0:T(8,128)} %param.8) | copy-start | bytes 1572868
  61.1 8.1 %copy-start.3 = (s32[10]{0:T(128)S(1)}, s32[10]{0:T(128)}, u32[]{:S(2)}) copy-start(s32[10]{0:T(128)} %param.11) | copy-start | bytes 124
  61.1 8.2 %copy-start.2 = (s32[10]{0:T(128)S(1)}, s32[10]{0:T(128)}, u32[]{:S(2)}) copy-start(s32[10]{0:T(128)} %param.12) | copy-start | bytes 124
  61.1 55.7 %all-to-all-start = ((f32[64,8,2,512]{3,0,2,1:T(8,128)}), f32[64,8,2,512]{3,0,2,1:T(8,128)S(1)}, u32[]{:S(2)}, u32[]{:S(2)}) async-start(f32[64,8,2,512]{3,0,2,1:T(8,128)} %bitcast.60), calls=%async_computation | async-start | bytes 4194304 | tf_op jit(solution)/shard_map/all_to_all | solution.py:47
  68.5 201.8 %all-gather.2.cloned.1.call-start = ((), (), s32[]{:S(2)}) async-start(), calls=%async_computation.2 | async-start | bytes 2621440 | tf_op jit(solution)/shard_map/all_gather | solution.py:78
Sparse Core Ops, SparseCore 0:
  250.3 19.8 all-gather.1
where the time goes:
time: 311 us; the launch traced here: 310 us
  blocking collectives  123 us (40%)
  waiting for transfers between devices  67.4 us (22%)
  local copies, waits for them, and re-layouts  58.4 us (19%)
  matrix products  32.6 us (10%)
  between operations  14.8 us (5%)
  starting transfers between devices  7.45 us (2%)
  other arithmetic  6.54 us (2%)
    all_to_all x1, waiting for transfers between devices, local(): lax.all_to_all(outgoing, 'ind', split_axis=1, concat_axis=1, tiled=True)  47.3 us
    all_to_all x1, blocking collectives, local(): lax.all_to_all(outgoing, 'ind', split_axis=1, concat_axis=1, tiled=True)  45.8 us
    slice x3, local copies, waits for them, and re-layouts, local(): diag_tiles = grm_tiles[:row_tiles]  43.1 us
    psum x1, blocking collectives, local(): total_gram = lax.psum(partial_gram, 'ind')  21.4 us
    all_gather x1, waiting for transfers between devices, local(): gathered = lax.all_gather(solution, 'var', axis=0, tiled=True)  20.1 us
    psum x1, blocking collectives, local(): rz_now = lax.psum(jnp.sum(resid * scaled, axis=1), 'ind')  19.5 us
    psum x1, blocking collectives, local(): alpha = rz_now / lax.psum(jnp.sum(direction * image, axis=1), 'ind')  19.4 us
    psum x1, blocking collectives, local(): rz_next = lax.psum(jnp.sum(resid * scaled, axis=1), 'ind')  17.1 us
  transfers between devices with their start and end apart: 2, of which 2 were waited for; matrix products, arithmetic and copies ran while one was open for 0% of the time, Pallas kernels for 0%

commit v1 on v0

v1 whole, which is shorter than its diff:
```python
import jax
import jax.numpy as jnp
from jax import lax
from jax.sharding import PartitionSpec as P

VARS_GENE = 4
NEED = 2
HI = lax.Precision.HIGHEST


def tile_dot(x, tile):
    return lax.dot_general(
        x, tile.astype(jnp.float32), (((1,), (1,)), ((), ())),
        precision=HI, preferred_element_type=jnp.float32,
    )


def local(genotypes, variance_comp, grm_tiles, tile_rows, tile_cols, tile_live):
    cols_here, rows_here = genotypes.shape
    tile_size = grm_tiles.shape[1]
    slot_count = grm_tiles.shape[0]
    row_tiles = rows_here // tile_size
    off_count = slot_count - row_tiles
    me = lax.axis_index("ind")
    peers = lax.axis_size("ind")
    v = lax.axis_index("var")
    nvar = lax.axis_size("var")
    ncol = cols_here * nvar
    genes = ncol // VARS_GENE
    total_ind = peers * rows_here
    tau0 = variance_comp[0]
    tau1 = variance_comp[1]
    live = tile_live[0]

    diag_tiles = grm_tiles[:row_tiles]
    off_tiles = grm_tiles[row_tiles:]
    diag_values = jnp.diagonal(diag_tiles, axis1=1, axis2=2).astype(jnp.float32).reshape(rows_here)
    precond = tau0 + tau1 * diag_values
    off_rows = tile_rows[row_tiles:]
    off_cols = tile_cols[row_tiles:]
    live_mask = (jnp.arange(row_tiles, slot_count, dtype=jnp.int32) < live).astype(jnp.float32)
    weight = (off_rows[:, None] == jnp.arange(row_tiles, dtype=jnp.int32)[None, :]).astype(jnp.float32)
    weight = weight * live_mask[:, None]
    position = off_cols // row_tiles * NEED + (off_cols % row_tiles - me) % row_tiles
    position = jnp.clip(position, 0, peers * NEED - 1)

    table = [(p + t) % row_tiles for p in range(peers) for t in range(NEED)]

    def exchange(x):
        pieces = jnp.stack([x[:, k * tile_size:(k + 1) * tile_size] for k in table])
        return lax.all_to_all(pieces, "ind", split_axis=0, concat_axis=0, tiled=True)

    def kprod(x, arrived):
        far = []
        for s in range(off_count):
            picked = lax.dynamic_index_in_dim(arrived, position[s], 0, keepdims=False)
            far.append(tile_dot(picked, off_tiles[s]))
        out = []
        for r in range(row_tiles):
            acc = tile_dot(x[:, r * tile_size:(r + 1) * tile_size], diag_tiles[r])
            for s in range(off_count):
                acc = acc + weight[s, r] * far[s]
            out.append(acc)
        return jnp.concatenate(out, axis=1)

    geno_all = lax.all_gather(genotypes, "var", axis=0, tiled=True)
    first = v * cols_here
    a_out = first // genes
    g0 = first % genes
    geno_sub = jnp.stack(
        [lax.dynamic_slice_in_dim(geno_all, a * genes + g0, cols_here, 0) for a in range(VARS_GENE)]
    )

    z0 = genotypes / precond[None, :]
    arrived0 = exchange(z0)
    kz0 = kprod(z0, arrived0)
    image0 = tau0 * z0 + tau1 * kz0
    w = image0 / precond[None, :]
    arrived1 = exchange(w)

    red1 = lax.psum(jnp.stack([jnp.sum(genotypes * z0, axis=1), jnp.sum(z0 * image0, axis=1)]), "ind")
    rz0 = red1[0]
    alpha0 = rz0 / red1[1]
    resid1 = genotypes - alpha0[:, None] * image0
    z1 = resid1 / precond[None, :]
    rz1 = lax.psum(jnp.sum(resid1 * z1, axis=1), "ind")
    beta = rz1 / rz0
    p0 = jnp.sum(geno_sub * z0[None], axis=2)

    kw = kprod(w, arrived1)
    dir1 = z1 + beta[:, None] * z0
    kdir1 = (kz0 - alpha0[:, None] * kw) + beta[:, None] * kz0
    image1 = tau0 * dir1 + tau1 * kdir1
    dad1 = jnp.sum(dir1 * image1, axis=1)
    pd1 = jnp.sum(geno_sub * dir1[None], axis=2)

    lead = (me == 0).astype(jnp.float32)
    block = jnp.concatenate(
        [dad1[None], (rz1 * lead)[None], alpha0[None] * p0, pd1], axis=0
    )
    nrow = block.shape[0]
    full = jnp.zeros((nrow, nvar, cols_here), jnp.float32)
    full = lax.dynamic_update_slice(full, block[:, None, :], (0, v, 0))
    full = lax.psum(full.reshape(nrow, ncol), ("ind", "var"))
    alpha1_all = full[1] / full[0]
    alpha1 = lax.dynamic_slice_in_dim(alpha1_all, first, cols_here, 0)
    solution = alpha0[:, None] * z0 + alpha1[:, None] * dir1

    a0p0 = lax.dynamic_index_in_dim(full[2:2 + VARS_GENE], a_out, 0, keepdims=False)
    pd1_all = lax.dynamic_index_in_dim(full[2 + VARS_GENE:], a_out, 0, keepdims=False)
    gram_cols = a0p0 + alpha1_all * pd1_all
    gram_cols = lax.dynamic_slice_in_dim(gram_cols.reshape(VARS_GENE, genes), g0, cols_here, 1)
    gene_gram = jnp.transpose(gram_cols) / total_ind
    return (solution, gene_gram)


def solution(mesh):
    placed = (P("var", "ind"), P(), P("ind", None, None), P("ind"), P("ind"), P("ind"))
    return jax.shard_map(
        local,
        mesh=mesh,
        in_specs=placed,
        out_specs=(P("var", "ind"), P("var", None)),
        check_vma=False,
    )
```

time: 311 us -> 335 us (1.077)
  waiting for transfers between devices: 67.4 us -> 34.3 us
  matrix products: 32.6 us -> 63.6 us
  local copies, waits for them, and re-layouts: 58.4 us -> 78.9 us
  blocking collectives: 123 us -> 109 us
  between operations: 14.8 us -> 26.2 us
  starting transfers between devices: 7.45 us -> 11.8 us
    all_to_all x1 -> x0, blocking collectives: 45.8 us -> none  [local(): lax.all_to_all(outgoing, 'ind', split_axis=1, concat_axis=1, tiled=True)]
    psum x4 -> x3, blocking collectives: 77.4 us -> 109 us  [the longest x1 46.8 us: local(): full = lax.psum(full.reshape(nrow, ncol), ('ind', 'var'))]
    dot_general x7 -> x20, matrix products: 32.6 us -> 63.6 us  [tile_dot(): lax.dot_general(x, tile.astype(jnp.float32), (((1,), (1,)), ((), ())), pr...]
    unnamed x10 -> x58, local copies, waits for them, and re-layouts: 0.13 us -> 20.5 us
    all_gather x1, waiting for transfers between devices: 20.1 us -> 0.02 us  [local(): geno_all = lax.all_gather(genotypes, 'var', axis=0, tiled=True)]
    all_to_all x1 -> x2, waiting for transfers between devices: 47.3 us -> 33.6 us  [exchange(): lax.all_to_all(pieces, 'ind', split_axis=0, concat_axis=0, tiled=True)]
    gather x4 -> x0, local copies, waits for them, and re-layouts: 7.73 us -> none  [the longest x2 4.07 us: local(): outgoing = pieces[:, table]]
    all_to_all x1 -> x2, starting transfers between devices: 7.41 us -> 11.8 us  [exchange(): lax.all_to_all(pieces, 'ind', split_axis=0, concat_axis=0, tiled=True)]
  transfers between devices with their start and end apart: 2 -> 3, of which waited for: 2 -> 1; matrix products, arithmetic and copies ran while one was open for 0% -> 15% of each run, Pallas kernels for 0% -> 0%
where the time goes in v1:
time: 335 us; the launch traced here: 333 us
  blocking collectives  109 us (33%)
  local copies, waits for them, and re-layouts  78.9 us (24%)
  matrix products  63.6 us (19%)
  waiting for transfers between devices  34.3 us (10%)
  between operations  26.2 us (8%)
  starting transfers between devices  11.8 us (4%)
  other arithmetic  8.66 us (3%)
    dot_general x20, matrix products, tile_dot(): lax.dot_general(x, tile.astype(jnp.float32), (((1,), (1,)), ((), ())), pr...  63.6 us
    psum x1, blocking collectives, local(): full = lax.psum(full.reshape(nrow, ncol), ('ind', 'var'))  46.8 us
    slice x3, local copies, waits for them, and re-layouts, local(): diag_tiles = grm_tiles[:row_tiles]  44.5 us
    psum x1, blocking collectives, local(): rz1 = lax.psum(jnp.sum(resid1 * z1, axis=1), 'ind')  43.2 us
    all_to_all x2, waiting for transfers between devices, exchange(): lax.all_to_all(pieces, 'ind', split_axis=0, concat_axis=0, tiled=True)  33.6 us
    unnamed x58, local copies, waits for them, and re-layouts  20.5 us
    psum x1, blocking collectives, local(): lax.psum(jnp.stack([jnp.sum(genotypes * z0, axis=1), jnp.sum(z0 * image0,...  19.5 us
    all_to_all x2, starting transfers between devices, exchange(): lax.all_to_all(pieces, 'ind', split_axis=0, concat_axis=0, tiled=True)  11.8 us
  transfers between devices with their start and end apart: 3, of which 1 were waited for; matrix products, arithmetic and copies ran while one was open for 15% of the time, Pallas kernels for 0%

profile of v1, /device:TPU:0, one launch (start us, length us, event | category | flops | bytes accessed | tf_op | source)
XLA Modules:
  0.0 332.8 jit_solution(7097121847370197725)
XLA Ops:
  8.8 42.9 %copy.11 = bf16[4,512,512]{0,2,1:T(8,128)(2,1)} copy(bf16[4,512,512]{2,1,0:T(8,128)(2,1)S(1)} %slice-done.2) | data formatting | bytes 4194304 | tf_op jit(solution)/shard_map/slice | solution.py:35
  52.2 6.5 %gather_fusion = bf16[512,4]{1,0:T(8,128)(2,1)S(1)} fusion(bf16[4,512,512]{0,2,1:T(8,128)(2,1)} %copy.11, s32[512]{0:T(512)S(1)} %bitcast.187), kind=kCustom, calls=%fused_computation | custom fusion | bytes 12288 | tf_op jit(solution)/shard_map/jit(diagonal)/gather | solution.py:37
  70.9 7.4 %all-to-all-start = ((f32[16,64,512]{2,1,0:T(8,128)}), f32[16,64,512]{2,1,0:T(8,128)}, u32[]{:S(2)}, u32[]{:S(2)}) async-start(f32[16,64,512]{2,1,0:T(8,128)} %bitcast_dynamic-update-slice_fusion.31), calls=%async_computation | async-start | bytes 4194304 | tf_op jit(solution)/shard_map/all_to_all | solution.py:51
  93.0 33.6 %all-to-all-done = f32[16,64,512]{2,1,0:T(8,128)} async-done(((f32[16,64,512]{2,1,0:T(8,128)}), f32[16,64,512]{2,1,0:T(8,128)}, u32[]{:S(2)}, u32[]{:S(2)}) %all-to-all-start) | async-done | bytes 2097184 | tf_op jit(solution)/shard_map/all_to_all | solution.py:51
  128.3 1.7 fusion.58
  130.1 1.9 fusion.62
  131.9 1.7 fusion.66
  133.6 1.7 fusion.70
  135.3 1.7 fusion.74
  137.1 5.5 %fusion.36 = f32[64,512]{1,0:T(8,128)S(1)} fusion(bf16[10,512,512]{2,1,0:T(8,128)(2,1)} %param.8, f32[64,512]{1,0:T(8,128)S(1)} %fusion.54, f32[64,512]{1,0:T(8,128)S(1)} %fusion.58, f32[64,512]{1,0:T(8,128)S(1)} %fusion.62, f32[64,512]{1,0:T(8,128)S(1)} %fusion.66, f32[64,512]{1,0:T(8,128)S(1)} %fusion.70, f32[64,512]{1,0:T(8,128)S(1)} %fusion.74, ...), kind=kOutput, calls=%fused_computation.48 | convolution fusion | flops 201719808 | bytes 1575936 | tf_op jit(solution)/shard_map/dot_general | solution.py:12
  142.6 5.5 %fusion.37 = f32[64,512]{1,0:T(8,128)S(1)} fusion(bf16[10,512,512]{2,1,0:T(8,128)(2,1)} %param.8, f32[64,512]{1,0:T(8,128)S(1)} %fusion.54, f32[64,512]{1,0:T(8,128)S(1)} %fusion.58, f32[64,512]{1,0:T(8,128)S(1)} %fusion.62, f32[64,512]{1,0:T(8,128)S(1)} %fusion.66, f32[64,512]{1,0:T(8,128)S(1)} %fusion.70, f32[64,512]{1,0:T(8,128)S(1)} %fusion.74, ...), kind=kOutput, calls=%fused_computation.49 | convolution fusion | flops 201719808 | bytes 1575936 | tf_op jit(solution)/shard_map/dot_general | solution.py:12
  148.0 5.4 %fusion.38 = f32[64,512]{1,0:T(8,128)S(1)} fusion(bf16[10,512,512]{2,1,0:T(8,128)(2,1)} %param.8, f32[64,512]{1,0:T(8,128)S(1)} %fusion.54, f32[64,512]{1,0:T(8,128)S(1)} %fusion.58, f32[64,512]{1,0:T(8,128)S(1)} %fusion.62, f32[64,512]{1,0:T(8,128)S(1)} %fusion.66, f32[64,512]{1,0:T(8,128)S(1)} %fusion.70, f32[64,512]{1,0:T(8,128)S(1)} %fusion.74, ...), kind=kOutput, calls=%fused_computation.50 | convolution fusion | flops 201719808 | bytes 1575936 | tf_op jit(solution)/shard_map/dot_general | solution.py:12
  153.5 4.5 %fusion.39 = f32[64,512]{1,0:T(8,128)S(1)} fusion(bf16[10,512,512]{2,1,0:T(8,128)(2,1)S(1)} %bitcast.189, f32[64,512]{1,0:T(8,128)S(1)} %fusion.54, f32[64,512]{1,0:T(8,128)S(1)} %fusion.58, f32[64,512]{1,0:T(8,128)S(1)} %fusion.62, f32[64,512]{1,0:T(8,128)S(1)} %fusion.66, f32[64,512]{1,0:T(8,128)S(1)} %fusion.70, f32[64,512]{1,0:T(8,128)S(1)} %fusion.74, ...), kind=kOutput, calls=%fused_computation.51 | convolution fusion | flops 201719808 | bytes 1572888 | tf_op jit(solution)/shard_map/dot_general | solution.py:12
  159.5 19.5 %psum.21 = f32[2,64]{1,0:T(2,128)S(1)} all-reduce(f32[2,64]{1,0:T(2,128)S(1)} %pad_maximum_fusion.3), channel_id=1, replica_groups=mesh['ind'=8,'var'=4] {'ind'}, use_global_device_ids=true, to_apply=%region_2.3 | all-reduce | flops 128 | bytes 1024 | tf_op jit(solution)/shard_map/psum | solution.py:81
  191.2 4.3 %all-to-all-start.1 = ((f32[16,64,512]{2,1,0:T(8,128)}), f32[16,64,512]{2,1,0:T(8,128)}, u32[]{:S(2)}, u32[]{:S(2)}) async-start(f32[16,64,512]{2,1,0:T(8,128)} %bitcast_dynamic-update-slice_fusion.15), calls=%async_computation.1 | async-start | bytes 4194304 | tf_op jit(solution)/shard_map/all_to_all | solution.py:51
  195.6 2.7 dynamic-slice_bitcast_fusion.3
  198.3 43.2 %psum.22 = f32[64]{0:T(128)S(1)} all-reduce(f32[64]{0:T(128)S(1)} %get-tuple-element.14), channel_id=1, replica_groups=mesh['ind'=8,'var'=4] {'ind'}, use_global_device_ids=true, to_apply=%region_4.5 | all-reduce | flops 64 | bytes 512 | tf_op jit(solution)/shard_map/psum | solution.py:86
  244.3 1.7 fusion.56
  247.8 1.7 fusion.64
  252.9 5.5 %fusion.32 = f32[64,512]{1,0:T(8,128)S(1)} fusion(bf16[10,512,512]{2,1,0:T(8,128)(2,1)} %param.8, f32[64,512]{1,0:T(8,128)S(1)} %fusion.52, f32[64,512]{1,0:T(8,128)S(1)} %fusion.56, f32[64,512]{1,0:T(8,128)S(1)} %fusion.60, f32[64,512]{1,0:T(8,128)S(1)} %fusion.64, f32[64,512]{1,0:T(8,128)S(1)} %fusion.68, f32[64,512]{1,0:T(8,128)S(1)} %fusion.72, ...), kind=kOutput, calls=%fused_computation.44 | convolution fusion | flops 201719808 | bytes 1575936 | tf_op jit(solution)/shard_map/dot_general | solution.py:12
  258.4 5.5 %fusion.33 = f32[64,512]{1,0:T(8,128)S(1)} fusion(bf16[10,512,512]{2,1,0:T(8,128)(2,1)} %param.8, f32[64,512]{1,0:T(8,128)S(1)} %fusion.52, f32[64,512]{1,0:T(8,128)S(1)} %fusion.56, f32[64,512]{1,0:T(8,128)S(1)} %fusion.60, f32[64,512]{1,0:T(8,128)S(1)} %fusion.64, f32[64,512]{1,0:T(8,128)S(1)} %fusion.68, f32[64,512]{1,0:T(8,128)S(1)} %fusion.72, ...), kind=kOutput, calls=%fused_computation.45 | convolution fusion | flops 201719808 | bytes 1575936 | tf_op jit(solution)/shard_map/dot_general | solution.py:12
  263.9 5.4 %fusion.34 = f32[64,512]{1,0:T(8,128)S(1)} fusion(bf16[10,512,512]{2,1,0:T(8,128)(2,1)} %param.8, f32[64,512]{1,0:T(8,128)S(1)} %fusion.52, f32[64,512]{1,0:T(8,128)S(1)} %fusion.56, f32[64,512]{1,0:T(8,128)S(1)} %fusion.60, f32[64,512]{1,0:T(8,128)S(1)} %fusion.64, f32[64,512]{1,0:T(8,128)S(1)} %fusion.68, f32[64,512]{1,0:T(8,128)S(1)} %fusion.72, ...), kind=kOutput, calls=%fused_computation.46 | convolution fusion | flops 201719808 | bytes 1575936 | tf_op jit(solution)/shard_map/dot_general | solution.py:12
  269.3 5.6 %fusion.35 = f32[64,512]{1,0:T(8,128)S(1)} fusion(bf16[10,512,512]{2,1,0:T(8,128)(2,1)} %param.8, f32[64,512]{1,0:T(8,128)S(1)} %fusion.52, f32[64,512]{1,0:T(8,128)S(1)} %fusion.56, f32[64,512]{1,0:T(8,128)S(1)} %fusion.60, f32[64,512]{1,0:T(8,128)S(1)} %fusion.64, f32[64,512]{1,0:T(8,128)S(1)} %fusion.68, f32[64,512]{1,0:T(8,128)S(1)} %fusion.72, ...), kind=kOutput, calls=%fused_computation.47 | convolution fusion | flops 201719808 | bytes 1575936 | tf_op jit(solution)/shard_map/dot_general | solution.py:12
  277.5 46.8 %psum.23 = f32[10,256]{1,0:T(8,128)S(1)} all-reduce(f32[10,256]{1,0:T(8,128)S(1)} %reshape.53), channel_id=1, replica_groups=mesh['ind'=8,'var'=4] {'ind','var'}, use_global_device_ids=true, to_apply=%region_8.9 | all-reduce | flops 2560 | bytes 20480 | tf_op jit(solution)/shard_map/psum | solution.py:104
  (102 shorter events, 44.8 us)
Async XLA Ops:
  7.2 1.6 slice-start.2
  8.8 42.9 %copy-start.6 = (f32[2]{0:T(128)S(1)}, f32[2]{0:T(128)}, u32[]{:S(2)}) copy-start(f32[2]{0:T(128)} %param.7) | copy-start | bytes 28
  8.8 51.3 %copy-start = (f32[64,2048]{1,0:T(8,128)S(1)}, f32[64,2048]{1,0:T(8,128)}, u32[]{:S(2)}) copy-start(f32[64,2048]{1,0:T(8,128)} %param.6) | copy-start | bytes 1572868
  70.9 8.2 %copy-start.9 = (s32[10]{0:T(128)S(1)}, s32[10]{0:T(128)}, u32[]{:S(2)}) copy-start(s32[10]{0:T(128)} %param.10) | copy-start | bytes 124
  70.9 17.0 %copy-start.10 = (s32[10]{0:T(128)S(1)}, s32[10]{0:T(128)}, u32[]{:S(2)}) copy-start(s32[10]{0:T(128)} %param.9) | copy-start | bytes 124
  70.9 82.6 %slice-start = ((s8[5242880]{0:T(1024)(128)(4,1)}), s8[1048576]{0:T(1024)(128)(4,1)S(1)}, s32[]{:S(2)}) async-start(s8[5242880]{0:T(1024)(128)(4,1)} %bitcast.188), calls=%async_computation.3 | async-start | bytes 2097152
  70.9 55.8 %all-to-all-start = ((f32[16,64,512]{2,1,0:T(8,128)}), f32[16,64,512]{2,1,0:T(8,128)}, u32[]{:S(2)}, u32[]{:S(2)}) async-start(f32[16,64,512]{2,1,0:T(8,128)} %bitcast_dynamic-update-slice_fusion.31), calls=%async_computation | async-start | bytes 4194304 | tf_op jit(solution)/shard_map/all_to_all | solution.py:51
  78.3 117.3 %all-gather.2.cloned.1.call-start = ((), (), s32[]{:S(2)}) async-start(), calls=%async_computation.2 | async-start | bytes 2621440 | tf_op jit(solution)/shard_map/all_gather | solution.py:66
  130.0 23.4 %slice-start.1 = ((s8[5242880]{0:T(1024)(128)(4,1)}), s8[4194304]{0:T(1024)(128)(4,1)S(1)}, s32[]{:S(2)}) async-start(s8[5242880]{0:T(1024)(128)(4,1)} %bitcast.188), calls=%async_computation.4 | async-start | bytes 8388608
  142.5 15.4 %copy-start.1 = (f32[64,2048]{1,0:T(8,128)S(1)}, f32[64,2048]{1,0:T(8,128)}, u32[]{:S(2)}) copy-start(f32[64,2048]{1,0:T(8,128)} %param.6) | copy-start | bytes 1572868
  158.0 26.5 %copy-start.4 = (f32[64,512]{1,0:T(8,128)}, f32[64,512]{1,0:T(8,128)S(1)}, u32[]{:S(2)}) copy-start(f32[64,512]{1,0:T(8,128)S(1)} %fusion.39) | copy-start | bytes 393220
  191.2 51.4 %all-to-all-start.1 = ((f32[16,64,512]{2,1,0:T(8,128)}), f32[16,64,512]{2,1,0:T(8,128)}, u32[]{:S(2)}, u32[]{:S(2)}) async-start(f32[16,64,512]{2,1,0:T(8,128)} %bitcast_dynamic-update-slice_fusion.15), calls=%async_computation.1 | async-start | bytes 4194304 | tf_op jit(solution)/shard_map/all_to_all | solution.py:51
  258.4 16.6 %copy-start.5 = (f32[64,512]{1,0:T(8,128)S(1)}, f32[64,512]{1,0:T(8,128)}, u32[]{:S(2)}) copy-start(f32[64,512]{1,0:T(8,128)} %copy-done.4) | copy-start | bytes 393220
  258.4 16.6 %copy-start.7 = (f32[64]{0:T(128)S(1)}, f32[64]{0:T(128)}, u32[]{:S(2)}) copy-start(f32[64]{0:T(128)} %get-tuple-element.43) | copy-start | bytes 772
  269.3 7.4 %copy-start.2 = (f32[1,64,2048]{2,1,0:T(8,128)S(1)}, f32[1,64,2048]{2,1,0:T(8,128)}, u32[]{:S(2)}) copy-start(f32[1,64,2048]{2,1,0:T(8,128)} %get-tuple-element.12) | copy-start | bytes 1572868
  269.3 7.3 %copy-start.3 = (f32[1,64,2048]{2,1,0:T(8,128)S(1)}, f32[1,64,2048]{2,1,0:T(8,128)}, u32[]{:S(2)}) copy-start(f32[1,64,2048]{2,1,0:T(8,128)} %get-tuple-element.13) | copy-start | bytes 1572868
  276.6 0.7 copy-start.8
Sparse Core Ops, SparseCore 0:
  80.6 23.9 all-gather.1

commit v2 on v1

v2 whole, which is shorter than its diff:
```python
import jax
import jax.numpy as jnp
from jax import lax
from jax.sharding import PartitionSpec as P

VARS_GENE = 4
NEED = 2
PAD_ROWS = 8


def split3(x):
    hi = lax.reduce_precision(x, exponent_bits=8, mantissa_bits=7)
    rest = x - hi
    mid = lax.reduce_precision(rest, exponent_bits=8, mantissa_bits=7)
    lo = rest - mid
    return hi.astype(jnp.bfloat16), mid.astype(jnp.bfloat16), lo.astype(jnp.bfloat16)


def batched_tile_dot(lhs, tiles):
    cols = lhs.shape[1]
    parts = jnp.concatenate(split3(lhs), axis=1)
    prod = lax.dot_general(
        parts, tiles, (((2,), (2,)), ((0,), (0,))), preferred_element_type=jnp.float32
    )
    return (prod[:, :cols] + prod[:, cols:2 * cols]) + prod[:, 2 * cols:]


def local(genotypes, variance_comp, grm_tiles, tile_rows, tile_cols, tile_live):
    cols_here, rows_here = genotypes.shape
    tile_size = grm_tiles.shape[1]
    slot_count = grm_tiles.shape[0]
    row_tiles = rows_here // tile_size
    off_count = slot_count - row_tiles
    me = lax.axis_index("ind")
    peers = lax.axis_size("ind")
    v = lax.axis_index("var")
    nvar = lax.axis_size("var")
    ncol = cols_here * nvar
    genes = ncol // VARS_GENE
    total_ind = peers * rows_here
    tau0 = variance_comp[0]
    tau1 = variance_comp[1]
    live = tile_live[0]

    eye = jnp.arange(tile_size)[:, None] == jnp.arange(tile_size)[None, :]
    diag_values = jnp.sum(
        jnp.where(eye[None], grm_tiles[:row_tiles].astype(jnp.float32), 0.0), axis=2
    )
    precond = (tau0 + tau1 * diag_values)[:, None, :]
    off_rows = tile_rows[row_tiles:]
    off_cols = tile_cols[row_tiles:]
    live_mask = (jnp.arange(row_tiles, slot_count, dtype=jnp.int32) < live).astype(jnp.float32)
    weight = (off_rows[:, None] == jnp.arange(row_tiles, dtype=jnp.int32)[None, :]).astype(jnp.float32)
    weight = weight * live_mask[:, None]
    position = off_cols // row_tiles * NEED + (off_cols % row_tiles - me) % row_tiles
    position = jnp.clip(position, 0, peers * NEED - 1)

    def to_tiles(x):
        return jnp.transpose(x.reshape(cols_here, row_tiles, tile_size), (1, 0, 2))

    def from_tiles(x):
        return jnp.transpose(x, (1, 0, 2)).reshape(cols_here, rows_here)

    def exchange(x, extra):
        rolled = jnp.stack([jnp.roll(x, -t, axis=0) for t in range(NEED)], axis=1)
        rolled = rolled.reshape(row_tiles, NEED * cols_here, tile_size)
        pieces = jnp.tile(rolled, (peers // row_tiles, 1, 1))
        flat = extra.reshape(-1)
        flat = jnp.pad(flat, (0, PAD_ROWS * tile_size - flat.shape[0]))
        side = jnp.broadcast_to(flat.reshape(1, PAD_ROWS, tile_size), (peers, PAD_ROWS, tile_size))
        pieces = jnp.concatenate([pieces, side], axis=1)
        arrived = lax.all_to_all(pieces, "ind", split_axis=0, concat_axis=0, tiled=True)
        tiles_in = arrived[:, :NEED * cols_here].reshape(peers * NEED, cols_here, tile_size)
        sums = jnp.sum(arrived[:, NEED * cols_here:].reshape(peers, -1)[:, :extra.size], axis=0)
        return tiles_in, sums.reshape(extra.shape)

    def kprod(x, tiles_in):
        picked = jnp.stack([lax.dynamic_index_in_dim(tiles_in, position[s], 0, keepdims=False)
                            for s in range(off_count)])
        prod = batched_tile_dot(jnp.concatenate([x, picked], axis=0), grm_tiles)
        far = prod[row_tiles:]
        return prod[:row_tiles] + jnp.sum(weight[:, :, None, None] * far[:, None], axis=0)

    def colsum(x):
        return jnp.sum(x, axis=(0, 2))

    geno_all = lax.all_gather(genotypes, "var", axis=0, tiled=True)
    first = v * cols_here
    a_out = first // genes
    g0 = first % genes
    geno_sub = jnp.stack(
        [to_tiles(lax.dynamic_slice_in_dim(geno_all, a * genes + g0, cols_here, 0))
         for a in range(VARS_GENE)]
    )

    g = to_tiles(genotypes)
    z0 = g / precond
    tiles0, sums0 = exchange(z0, colsum(g * z0)[None])
    rz0 = sums0[0]
    kz0 = kprod(z0, tiles0)
    image0 = tau0 * z0 + tau1 * kz0
    w = image0 / precond
    p0_local = jnp.sum(geno_sub * z0[None], axis=(1, 3))
    extra1 = jnp.concatenate([colsum(z0 * image0)[None], p0_local], axis=0)
    tiles1, sums1 = exchange(w, extra1)
    dad0 = sums1[0]
    p0 = sums1[1:]
    alpha0 = rz0 / dad0
    resid1 = g - alpha0[None, :, None] * image0
    z1 = resid1 / precond
    kw = kprod(w, tiles1)
    kz1 = kz0 - alpha0[None, :, None] * kw
    az1 = tau0 * z1 + tau1 * kz1
    red_local = jnp.concatenate(
        [colsum(resid1 * z1)[None], colsum(z1 * az1)[None],
         colsum(z1 * image0 + z0 * az1)[None], jnp.sum(geno_sub * z1[None], axis=(1, 3))],
        axis=0,
    )
    red = jnp.sum(lax.all_gather(red_local, "ind", axis=0, tiled=False), axis=0)
    rz1 = red[0]
    beta = rz1 / rz0
    dad1 = red[1] + beta * (red[2] + beta * dad0)
    alpha1 = rz1 / dad1
    dir1 = z1 + beta[None, :, None] * z0
    solution = alpha0[None, :, None] * z0 + alpha1[None, :, None] * dir1
    p1 = red[3:]
    gram_part = alpha0[None] * p0 + alpha1[None] * (p1 + beta[None] * p0)
    gathered = lax.all_gather(gram_part, "var", axis=0, tiled=False)
    full = jnp.transpose(gathered, (1, 0, 2)).reshape(VARS_GENE, ncol)
    gram_cols = lax.dynamic_index_in_dim(full, a_out, 0, keepdims=False)
    gram_cols = lax.dynamic_slice_in_dim(gram_cols.reshape(VARS_GENE, genes), g0, cols_here, 1)
    gene_gram = jnp.transpose(gram_cols) / total_ind
    return (from_tiles(solution), gene_gram)


def solution(mesh):
    placed = (P("var", "ind"), P(), P("ind", None, None), P("ind"), P("ind"), P("ind"))
    return jax.shard_map(
        local,
        mesh=mesh,
        in_specs=placed,
        out_specs=(P("var", "ind"), P("var", None)),
        check_vma=False,
    )
```

time: 335 us -> 205 us (0.61)
  blocking collectives: 109 us -> 35.8 us
  local copies, waits for them, and re-layouts: 78.9 us -> 23.4 us
  matrix products: 63.6 us -> 8.67 us
  waiting for transfers between devices: 34.3 us -> 75.6 us
  other arithmetic: 8.66 us -> 22.1 us
    psum x3 -> x0, blocking collectives: 109 us -> none  [the longest x1 46.8 us: local(): full = lax.psum(full.reshape(nrow, ncol), ('ind', 'var'))]
    dot_general x20 -> x2, matrix products: 63.6 us -> 8.67 us  [batched_tile_dot(): lax.dot_general(parts, tiles, (((2,), (2,)), ((0,), (0,))), preferred_ele...]
    slice x8 -> x12, local copies, waits for them, and re-layouts: 47 us -> 5.27 us  [the longest x2 2.03 us: exchange(): arrived[:, :NEED * cols_here].reshape(peers * NEED, cols_here, tile_size)]
    all_gather x0 -> x2, blocking collectives: none -> 35.8 us  [the longest x1 30.6 us: local(): red = jnp.sum(lax.all_gather(red_local, 'ind', axis=0, tiled=False), axis=0)]
    all_to_all x2, waiting for transfers between devices: 33.6 us -> 63.5 us  [exchange(): lax.all_to_all(pieces, 'ind', split_axis=0, concat_axis=0, tiled=True)]
    unnamed x58 -> x46, local copies, waits for them, and re-layouts: 20.5 us -> 4.91 us
    all_gather x1, waiting for transfers between devices: 0.02 us -> 11.5 us  [local(): geno_all = lax.all_gather(genotypes, 'var', axis=0, tiled=True)]
    reshape x1 -> x7, local copies, waits for them, and re-layouts: 0.08 us -> 7.53 us  [the longest x4 6.53 us: to_tiles(): return jnp.transpose(x.reshape(cols_here, row_tiles, tile_size), (1, 0, 2))]
  transfers between devices with their start and end apart: 3 -> 3, of which waited for: 1 -> 3; matrix products, arithmetic and copies ran while one was open for 15% -> 7% of each run, Pallas kernels for 0% -> 0%
where the time goes in v2:
time: 205 us; the launch traced here: 204 us
  waiting for transfers between devices  75.6 us (37%)
  blocking collectives  35.8 us (17%)
  between operations  26.7 us (13%)
  local copies, waits for them, and re-layouts  23.4 us (11%)
  other arithmetic  22.1 us (11%)
  starting transfers between devices  12 us (6%)
  matrix products  8.67 us (4%)
    all_to_all x2, waiting for transfers between devices, exchange(): lax.all_to_all(pieces, 'ind', split_axis=0, concat_axis=0, tiled=True)  63.5 us
    all_gather x1, blocking collectives, local(): red = jnp.sum(lax.all_gather(red_local, 'ind', axis=0, tiled=False), axis=0)  30.6 us
    all_to_all x2, starting transfers between devices, exchange(): lax.all_to_all(pieces, 'ind', split_axis=0, concat_axis=0, tiled=True)  11.9 us
    all_gather x1, waiting for transfers between devices, local(): geno_all = lax.all_gather(genotypes, 'var', axis=0, tiled=True)  11.5 us
    dot_general x2, matrix products, batched_tile_dot(): lax.dot_general(parts, tiles, (((2,), (2,)), ((0,), (0,))), preferred_ele...  8.67 us
    reshape x4, local copies, waits for them, and re-layouts, to_tiles(): return jnp.transpose(x.reshape(cols_here, row_tiles, tile_size), (1, 0, 2))  6.53 us
    all_gather x1, blocking collectives, local(): gathered = lax.all_gather(gram_part, 'var', axis=0, tiled=False)  5.18 us
    unnamed x46, local copies, waits for them, and re-layouts  4.91 us
  transfers between devices with their start and end apart: 3, of which 3 were waited for; matrix products, arithmetic and copies ran while one was open for 7% of the time, Pallas kernels for 0%

profile of v2, /device:TPU:0, one launch (start us, length us, event | category | flops | bytes accessed | tf_op | source)
XLA Modules:
  0.0 204.3 jit_solution(7713018969594389198)
XLA Ops:
  7.3 1.4 fusion.37
  8.7 2.4 %select_reduce_fusion = f32[4,512]{1,0:T(4,128)S(1)} fusion(bf16[10,512,512]{2,1,0:T(8,128)(2,1)} %param.8, pred[512,512]{1,0:T(8,128)(4,1)S(1)} %iota_compare_fusion), kind=kLoop, calls=%fused_computation | loop fusion | flops 3143680 | bytes 2367488 | tf_op jit(solution)/shard_map/reduce_sum | solution.py:46
  11.1 1.3 multiply_add_fusion.1
  14.1 1.6 pad_maximum_fusion
  15.8 7.4 %all-to-all-start = ((f32[8,136,512]{2,1,0:T(8,128)}), f32[8,136,512]{2,1,0:T(8,128)S(1)}, u32[]{:S(2)}, u32[]{:S(2)}) async-start(f32[8,136,512]{2,1,0:T(8,128)} %pad_maximum_fusion), calls=%async_computation | async-start | bytes 4456448 | tf_op jit(solution)/shard_map/all_to_all | solution.py:72
  32.3 1.1 copy.27
  38.1 11.5 %all-gather.6.cloned.1.call-done = f32[256,2048]{1,0:T(8,128)} async-done(((f32[64,2048]{1,0:T(8,128)}), f32[256,2048]{1,0:T(8,128)}) %all-gather.6.cloned.1.call-update) | async-done | bytes 2097168 | tf_op jit(solution)/shard_map/all_gather | solution.py:87
  49.6 2.7 %constant_dynamic-slice_fusion.4 = (f32[64,2048]{1,0:T(8,128)S(1)}, f32[64,2048]{1,0:T(8,128)}, f32[64,2048]{1,0:T(8,128)}, f32[64,2048]{1,0:T(8,128)}) fusion(f32[256,2048]{1,0:T(8,128)} %all-gather.6.cloned.1.call-done, s32[]{:T(128)S(6)} %select_n.83, s32[]{:T(128)S(6)} %select_n.86, s32[]{:T(128)S(6)} %select_n.85, s32[]{:T(128)S(6)} %select_n.84), kind=kLoop, calls=%fused_computation.80 | loop fusion | bytes 4194320 | tf_op jit(solution)/shard_map/dynamic_slice | solution.py:92
  52.6 1.6 reshape.148
  54.2 2.4 %reshape.147 = f32[64,4,512]{2,1,0:T(4,128)} reshape(f32[64,2048]{1,0:T(8,128)} %get-tuple-element.14) | data formatting | bytes 1048576 | tf_op jit(solution)/shard_map/reshape | solution.py:59
  56.6 2.2 %reshape.146 = f32[64,4,512]{2,1,0:T(4,128)} reshape(f32[64,2048]{1,0:T(8,128)} %get-tuple-element.15) | data formatting | bytes 1048576 | tf_op jit(solution)/shard_map/reshape | solution.py:59
  58.8 2.2 %multiply_reduce_fusion.3 = f32[4,64]{1,0:T(4,128)S(1)} fusion(f32[4,64,512]{2,0,1:T(4,128)} %copy.27, f32[1,4,64,512]{3,1,2,0:T(4,128)S(1)} %bitcast.148, f32[1,4,64,512]{3,1,2,0:T(4,128)} %bitcast.150, f32[1,4,64,512]{3,1,2,0:T(4,128)} %bitcast.152, f32[1,4,64,512]{3,1,2,0:T(4,128)S(1)} %bitcast.146), kind=kLoop, calls=%fused_computation.7 | loop fusion | flops 2621184 | bytes 2622464 | tf_op jit(solution)/shard_map/reduce_sum | solution.py:103
  61.1 13.1 %all-to-all-done = f32[8,136,512]{2,1,0:T(8,128)S(1)} async-done(((f32[8,136,512]{2,1,0:T(8,128)}), f32[8,136,512]{2,1,0:T(8,128)S(1)}, u32[]{:S(2)}, u32[]{:S(2)}) %all-to-all-start) | async-done | bytes 2228256 | tf_op jit(solution)/shard_map/all_to_all | solution.py:72
  76.1 4.3 %fusion = f32[10,192,512]{2,1,0:T(8,128)S(1)} fusion(bf16[10,512,512]{2,1,0:T(8,128)(2,1)} %param.8, bf16[10,64,512]{2,1,0:T(8,128)(2,1)S(1)} %get-tuple-element.20, bf16[10,64,512]{2,1,0:T(8,128)(2,1)S(1)} %get-tuple-element.21, bf16[10,64,512]{2,1,0:T(8,128)(2,1)S(1)} %get-tuple-element.19), kind=kOutput, calls=%fused_computation.8 | convolution fusion | flops 1012531200 | bytes 11141120 | tf_op jit(solution)/shard_map/dot_general | solution.py:22
  82.3 2.4 %constant_dynamic-update-slice_fusion.1 = (f32[10,64,512]{2,1,0:T(8,128)}, f32[4,64,512]{2,1,0:T(8,128)S(1)}, f32[4,64,512]{2,1,0:T(8,128)S(1)}) fusion(f32[4,512]{1,0:T(4,128)S(1)} %multiply_add_fusion.1, f32[4,64,512]{2,1,0:T(8,128)S(1)} %multiply_reduce_fusion.1, f32[10,64,512]{2,1,0:T(8,128)S(1)} %slice_add_fusion.2, f32[]{:T(128)} %bitcast.2, ...), kind=kLoop, calls=%fused_computation.73 | loop fusion | flops 786431 | bytes 3153928
  86.9 1.1 pad_maximum_fusion.4
  88.4 1.6 pad_maximum_fusion.1
  90.0 4.5 %all-to-all-start.1 = ((f32[8,136,512]{2,1,0:T(8,128)}), f32[8,136,512]{2,1,0:T(8,128)}, u32[]{:S(2)}, u32[]{:S(2)}) async-start(f32[8,136,512]{2,1,0:T(8,128)} %pad_maximum_fusion.1), calls=%async_computation.1 | async-start | bytes 4456448 | tf_op jit(solution)/shard_map/all_to_all | solution.py:72
  94.7 50.4 %all-to-all-done.1 = f32[8,136,512]{2,1,0:T(8,128)} async-done(((f32[8,136,512]{2,1,0:T(8,128)}), f32[8,136,512]{2,1,0:T(8,128)}, u32[]{:S(2)}, u32[]{:S(2)}) %all-to-all-start.1) | async-done | bytes 2228256 | tf_op jit(solution)/shard_map/all_to_all | solution.py:72
  145.1 1.8 slice.183
  148.5 4.3 %fusion.6 = f32[10,192,512]{2,1,0:T(8,128)S(1)} fusion(bf16[10,512,512]{2,1,0:T(8,128)(2,1)} %param.8, bf16[10,64,512]{2,1,0:T(8,128)(2,1)S(1)} %get-tuple-element.17, bf16[10,64,512]{2,1,0:T(8,128)(2,1)S(1)} %get-tuple-element.18, bf16[10,64,512]{2,1,0:T(8,128)(2,1)S(1)} %get-tuple-element.16), kind=kOutput, calls=%fused_computation.14 | convolution fusion | flops 1012531200 | bytes 11141120 | tf_op jit(solution)/shard_map/dot_general | solution.py:22
  154.5 2.8 %fusion.21 = (f32[4,64,512]{2,1,0:T(8,128)S(1)}, f32[4,64,512]{2,1,0:T(8,128)S(1)}) fusion(f32[4,64,512]{2,1,0:T(8,128)S(1)} %multiply_reduce_fusion, f32[10,64,512]{2,1,0:T(8,128)S(1)} %slice_add_fusion, f32[64]{0:T(128)S(1)} %slice_divide_fusion, f32[]{:T(128)} %bitcast.2, f32[]{:T(128)} %bitcast.1, f32[4,64,512]{2,1,0:T(8,128)S(1)} %copy-done.4, ...), kind=kLoop, calls=%fused_computation.46 | loop fusion | flops 1310720 | bytes 4202760 | tf_op jit(solution)/shard_map/add | solution.py:113
  159.7 30.6 %all-gather.2 = f32[8,7,64]{2,1,0:T(8,128)S(1)} all-gather(f32[1,7,64]{2,1,0:T(8,128)S(1)} %maximum_bitcast_fusion.2), channel_id=2, replica_groups=mesh['ind'=8,'var'=4] {'ind'}, dimensions={0}, use_global_device_ids=true | all-gather | bytes 16128 | tf_op jit(solution)/shard_map/all_gather | solution.py:119
  191.5 5.2 %all-gather.3 = f32[4,4,64]{2,1,0:T(4,128)S(1)} all-gather(f32[1,4,64]{2,1,0:T(4,128)S(1)} %add_bitcast_fusion.1), channel_id=3, replica_groups=mesh['ind'=8,'var'=4] {'var'}, dimensions={0}, use_global_device_ids=true | all-gather | bytes 5120 | tf_op jit(solution)/shard_map/all_gather | solution.py:128
  (106 shorter events, 17.5 us)
Async XLA Ops:
  7.2 5.3 %copy-start = (f32[64,2048]{1,0:T(8,128)S(1)}, f32[64,2048]{1,0:T(8,128)}, u32[]{:S(2)}) copy-start(f32[64,2048]{1,0:T(8,128)} %param.6) | copy-start | bytes 1572868
  15.7 8.2 %copy-start.14 = (s32[10]{0:T(128)S(1)}, s32[10]{0:T(128)}, u32[]{:S(2)}) copy-start(s32[10]{0:T(128)} %param.10) | copy-start | bytes 124
  15.8 18.4 %copy-start.15 = (s32[10]{0:T(128)S(1)}, s32[10]{0:T(128)}, u32[]{:S(2)}) copy-start(s32[10]{0:T(128)} %param.9) | copy-start | bytes 124
  15.8 58.5 %all-to-all-start = ((f32[8,136,512]{2,1,0:T(8,128)}), f32[8,136,512]{2,1,0:T(8,128)S(1)}, u32[]{:S(2)}, u32[]{:S(2)}) async-start(f32[8,136,512]{2,1,0:T(8,128)} %pad_maximum_fusion), calls=%async_computation | async-start | bytes 4456448 | tf_op jit(solution)/shard_map/all_to_all | solution.py:72
  23.2 26.4 %all-gather.6.cloned.1.call-start = ((), (), s32[]{:S(2)}) async-start(), calls=%async_computation.2 | async-start | bytes 2621440 | tf_op jit(solution)/shard_map/all_gather | solution.py:87
  52.6 8.5 %copy-start.5 = (f32[64,4,512]{2,1,0:T(4,128)}, f32[64,4,512]{2,1,0:T(4,128)S(1)}, u32[]{:S(2)}) copy-start(f32[64,4,512]{2,1,0:T(4,128)S(1)} %reshape.145) | copy-start | bytes 1572868
  54.2 6.9 %copy-start.7 = (f32[64,4,512]{2,1,0:T(4,128)}, f32[64,4,512]{2,1,0:T(4,128)S(1)}, u32[]{:S(2)}) copy-start(f32[64,4,512]{2,1,0:T(4,128)S(1)} %reshape.148) | copy-start | bytes 1572868
  74.2 1.3 copy-start.12
  80.9 3.8 %copy-start.2 = (f32[10,64,512]{2,1,0:T(8,128)}, f32[10,64,512]{2,1,0:T(8,128)S(1)}, u32[]{:S(2)}) copy-start(f32[10,64,512]{2,1,0:T(8,128)S(1)} %slice_add_fusion.2) | copy-start | bytes 3932164
  80.9 1.4 copy-start.1
  82.3 3.2 %copy-start.3 = (f32[4,64,512]{2,1,0:T(8,128)}, f32[4,64,512]{2,1,0:T(8,128)S(1)}, u32[]{:S(2)}) copy-start(f32[4,64,512]{2,1,0:T(8,128)S(1)} %multiply_reduce_fusion.1) | copy-start | bytes 1572868
  84.6 0.9 copy-start.11
  90.0 55.1 %all-to-all-start.1 = ((f32[8,136,512]{2,1,0:T(8,128)}), f32[8,136,512]{2,1,0:T(8,128)}, u32[]{:S(2)}, u32[]{:S(2)}) async-start(f32[8,136,512]{2,1,0:T(8,128)} %pad_maximum_fusion.1), calls=%async_computation.1 | async-start | bytes 4456448 | tf_op jit(solution)/shard_map/all_to_all | solution.py:72
  94.7 52.2 %copy-start.13 = (f32[10,64,512]{2,1,0:T(8,128)S(1)}, f32[10,64,512]{2,1,0:T(8,128)}, u32[]{:S(2)}) copy-start(f32[10,64,512]{2,1,0:T(8,128)} %get-tuple-element.9) | copy-start | bytes 3932164
  153.5 1.0 copy-start.4
  157.3 1.0 copy-start.6
  157.3 1.2 copy-start.8
  157.3 1.3 copy-start.9
  157.3 1.5 copy-start.10
Sparse Core Ops, SparseCore 0:
  25.5 23.9 all-gather.5

commit v3 on v2

--- a/solution.py
+++ b/solution.py
@@ -6,6 +6,7 @@
 VARS_GENE = 4
 NEED = 2
 PAD_ROWS = 8
+CHUNKS = 2
 
 
 def split3(x):
@@ -63,15 +64,16 @@
 
     def exchange(x, extra):
         rolled = jnp.stack([jnp.roll(x, -t, axis=0) for t in range(NEED)], axis=1)
-        rolled = rolled.reshape(row_tiles, NEED * cols_here, tile_size)
+        width = x.shape[1]
+        rolled = rolled.reshape(row_tiles, NEED * width, tile_size)
         pieces = jnp.tile(rolled, (peers // row_tiles, 1, 1))
         flat = extra.reshape(-1)
         flat = jnp.pad(flat, (0, PAD_ROWS * tile_size - flat.shape[0]))
         side = jnp.broadcast_to(flat.reshape(1, PAD_ROWS, tile_size), (peers, PAD_ROWS, tile_size))
         pieces = jnp.concatenate([pieces, side], axis=1)
         arrived = lax.all_to_all(pieces, "ind", split_axis=0, concat_axis=0, tiled=True)
-        tiles_in = arrived[:, :NEED * cols_here].reshape(peers * NEED, cols_here, tile_size)
-        sums = jnp.sum(arrived[:, NEED * cols_here:].reshape(peers, -1)[:, :extra.size], axis=0)
+        tiles_in = arrived[:, :NEED * width].reshape(peers * NEED, width, tile_size)
+        sums = jnp.sum(arrived[:, NEED * width:].reshape(peers, -1)[:, :extra.size], axis=0)
         return tiles_in, sums.reshape(extra.shape)
 
     def kprod(x, tiles_in):
@@ -93,38 +95,50 @@
          for a in range(VARS_GENE)]
     )
 
-    g = to_tiles(genotypes)
-    z0 = g / precond
-    tiles0, sums0 = exchange(z0, colsum(g * z0)[None])
-    rz0 = sums0[0]
-    kz0 = kprod(z0, tiles0)
-    image0 = tau0 * z0 + tau1 * kz0
-    w = image0 / precond
-    p0_local = jnp.sum(geno_sub * z0[None], axis=(1, 3))
-    extra1 = jnp.concatenate([colsum(z0 * image0)[None], p0_local], axis=0)
-    tiles1, sums1 = exchange(w, extra1)
-    dad0 = sums1[0]
-    p0 = sums1[1:]
-    alpha0 = rz0 / dad0
-    resid1 = g - alpha0[None, :, None] * image0
-    z1 = resid1 / precond
-    kw = kprod(w, tiles1)
-    kz1 = kz0 - alpha0[None, :, None] * kw
-    az1 = tau0 * z1 + tau1 * kz1
-    red_local = jnp.concatenate(
-        [colsum(resid1 * z1)[None], colsum(z1 * az1)[None],
-         colsum(z1 * image0 + z0 * az1)[None], jnp.sum(geno_sub * z1[None], axis=(1, 3))],
-        axis=0,
-    )
-    red = jnp.sum(lax.all_gather(red_local, "ind", axis=0, tiled=False), axis=0)
-    rz1 = red[0]
-    beta = rz1 / rz0
-    dad1 = red[1] + beta * (red[2] + beta * dad0)
-    alpha1 = rz1 / dad1
-    dir1 = z1 + beta[None, :, None] * z0
-    solution = alpha0[None, :, None] * z0 + alpha1[None, :, None] * dir1
-    p1 = red[3:]
-    gram_part = alpha0[None] * p0 + alpha1[None] * (p1 + beta[None] * p0)
+    def reduce_ind(x):
+        spread = jnp.broadcast_to(x[None], (peers,) + x.shape)
+        return jnp.sum(lax.all_to_all(spread, "ind", split_axis=0, concat_axis=0, tiled=True), axis=0)
+
+    def chunk(g, geno_sub):
+        z0 = g / precond
+        tiles0, sums0 = exchange(z0, colsum(g * z0)[None])
+        rz0 = sums0[0]
+        kz0 = kprod(z0, tiles0)
+        image0 = tau0 * z0 + tau1 * kz0
+        w = image0 / precond
+        p0_local = jnp.sum(geno_sub * z0[None], axis=(1, 3))
+        extra1 = jnp.concatenate([colsum(z0 * image0)[None], p0_local], axis=0)
+        tiles1, sums1 = exchange(w, extra1)
+        dad0 = sums1[0]
+        p0 = sums1[1:]
+        alpha0 = rz0 / dad0
+        resid1 = g - alpha0[None, :, None] * image0
+        z1 = resid1 / precond
+        kw = kprod(w, tiles1)
+        kz1 = kz0 - alpha0[None, :, None] * kw
+        az1 = tau0 * z1 + tau1 * kz1
+        red_local = jnp.concatenate(
+            [colsum(resid1 * z1)[None], colsum(z1 * az1)[None],
+             colsum(z1 * image0 + z0 * az1)[None], jnp.sum(geno_sub * z1[None], axis=(1, 3))],
+            axis=0,
+        )
+        red = reduce_ind(red_local)
+        rz1 = red[0]
+        beta = rz1 / rz0
+        dad1 = red[1] + beta * (red[2] + beta * dad0)
+        alpha1 = rz1 / dad1
+        dir1 = z1 + beta[None, :, None] * z0
+        sol = alpha0[None, :, None] * z0 + alpha1[None, :, None] * dir1
+        p1 = red[3:]
+        part = alpha0[None] * p0 + alpha1[None] * (p1 + beta[None] * p0)
+        return sol, part
+
+    g_all = to_tiles(genotypes)
+    width = cols_here // CHUNKS
+    outs = [chunk(g_all[:, k * width:(k + 1) * width], geno_sub[:, :, k * width:(k + 1) * width])
+            for k in range(CHUNKS)]
+    solution = jnp.concatenate([o[0] for o in outs], axis=1)
+    gram_part = jnp.concatenate([o[1] for o in outs], axis=1)
     gathered = lax.all_gather(gram_part, "var", axis=0, tiled=False)
     full = jnp.transpose(gathered, (1, 0, 2)).reshape(VARS_GENE, ncol)
     gram_cols = lax.dynamic_index_in_dim(full, a_out, 0, keepdims=False)

time: 205 us -> 223 us (1.088)
  blocking collectives: 35.8 us -> 5.18 us
  starting transfers between devices: 12 us -> 27.1 us
  local copies, waits for them, and re-layouts: 23.4 us -> 35.5 us
  other arithmetic: 22.1 us -> 29.8 us
  waiting for transfers between devices: 75.6 us -> 82.4 us
  matrix products: 8.67 us -> 14.4 us
    all_gather x1 -> x0, blocking collectives: 30.6 us -> none  [local(): red = jnp.sum(lax.all_gather(red_local, 'ind', axis=0, tiled=False), axis=0)]
    all_gather x1, waiting for transfers between devices: 11.5 us -> 0.01 us  [local(): geno_all = lax.all_gather(genotypes, 'var', axis=0, tiled=True)]
    all_to_all x0 -> x2, waiting for transfers between devices: none -> 10.8 us  [reduce_ind(): lax.all_to_all(spread, 'ind', split_axis=0, concat_axis=0, tiled=True)]
    all_to_all x2 -> x4, starting transfers between devices: 11.9 us -> 20.4 us  [exchange(): lax.all_to_all(pieces, 'ind', split_axis=0, concat_axis=0, tiled=True)]
    all_to_all x2 -> x4, waiting for transfers between devices: 63.5 us -> 70.9 us  [exchange(): lax.all_to_all(pieces, 'ind', split_axis=0, concat_axis=0, tiled=True)]
    unnamed x46 -> x78, local copies, waits for them, and re-layouts: 4.91 us -> 11.8 us
    all_to_all x0 -> x2, starting transfers between devices: none -> 6.71 us  [reduce_ind(): lax.all_to_all(spread, 'ind', split_axis=0, concat_axis=0, tiled=True)]
    dot_general x2 -> x4, matrix products: 8.67 us -> 14.4 us  [batched_tile_dot(): lax.dot_general(parts, tiles, (((2,), (2,)), ((0,), (0,))), preferred_ele...]
  transfers between devices with their start and end apart: 3 -> 7, of which waited for: 3 -> 6; matrix products, arithmetic and copies ran while one was open for 7% -> 14% of each run, Pallas kernels for 0% -> 0%
where the time goes in v3:
time: 223 us; the launch traced here: 221 us
  waiting for transfers between devices  82.4 us (37%)
  local copies, waits for them, and re-layouts  35.5 us (16%)
  other arithmetic  29.8 us (13%)
  starting transfers between devices  27.1 us (12%)
  between operations  26.9 us (12%)
  matrix products  14.4 us (6%)
  blocking collectives  5.18 us (2%)
    all_to_all x4, waiting for transfers between devices, exchange(): lax.all_to_all(pieces, 'ind', split_axis=0, concat_axis=0, tiled=True)  70.9 us
    all_to_all x4, starting transfers between devices, exchange(): lax.all_to_all(pieces, 'ind', split_axis=0, concat_axis=0, tiled=True)  20.4 us
    dot_general x4, matrix products, batched_tile_dot(): lax.dot_general(parts, tiles, (((2,), (2,)), ((0,), (0,))), preferred_ele...  14.4 us
    unnamed x78, local copies, waits for them, and re-layouts  11.8 us
    all_to_all x2, waiting for transfers between devices, reduce_ind(): lax.all_to_all(spread, 'ind', split_axis=0, concat_axis=0, tiled=True)  10.8 us
    all_to_all x2, starting transfers between devices, reduce_ind(): lax.all_to_all(spread, 'ind', split_axis=0, concat_axis=0, tiled=True)  6.71 us
    reshape x5, local copies, waits for them, and re-layouts, to_tiles(): return jnp.transpose(x.reshape(cols_here, row_tiles, tile_size), (1, 0, 2))  5.68 us
    all_gather x1, blocking collectives, local(): gathered = lax.all_gather(gram_part, 'var', axis=0, tiled=False)  5.18 us
  transfers between devices with their start and end apart: 7, of which 6 were waited for; matrix products, arithmetic and copies ran while one was open for 14% of the time, Pallas kernels for 0%

profile of v3, /device:TPU:0, one launch (start us, length us, event | category | flops | bytes accessed | tf_op | source)
XLA Modules:
  0.0 221.2 jit_solution(3393050681380166144)
XLA Ops:
  9.7 2.4 %select_reduce_fusion = f32[4,512]{1,0:T(4,128)S(1)} fusion(bf16[10,512,512]{2,1,0:T(8,128)(2,1)} %param.8, pred[512,512]{1,0:T(8,128)(4,1)S(1)} %iota_compare_fusion), kind=kLoop, calls=%fused_computation | loop fusion | flops 3143680 | bytes 2367488 | tf_op jit(solution)/shard_map/reduce_sum | solution.py:47
  15.9 7.4 %all-to-all-start = ((f32[8,72,512]{2,1,0:T(8,128)}), f32[8,72,512]{2,1,0:T(8,128)S(1)}, u32[]{:S(2)}, u32[]{:S(2)}) async-start(f32[8,72,512]{2,1,0:T(8,128)} %pad_maximum_fusion.1), calls=%async_computation | async-start | bytes 2359296 | tf_op jit(solution)/shard_map/all_to_all | solution.py:74
  40.2 11.7 %all-to-all-done = f32[8,72,512]{2,1,0:T(8,128)S(1)} async-done(((f32[8,72,512]{2,1,0:T(8,128)}), f32[8,72,512]{2,1,0:T(8,128)S(1)}, u32[]{:S(2)}, u32[]{:S(2)}) %all-to-all-start) | async-done | bytes 1179680 | tf_op jit(solution)/shard_map/all_to_all | solution.py:74
  51.9 4.3 %all-to-all-start.3 = ((f32[8,72,512]{2,1,0:T(8,128)}), f32[8,72,512]{2,1,0:T(8,128)}, u32[]{:S(2)}, u32[]{:S(2)}) async-start(f32[8,72,512]{2,1,0:T(8,128)} %pad_maximum_fusion.3), calls=%async_computation.3 | async-start | bytes 2359296 | tf_op jit(solution)/shard_map/all_to_all | solution.py:74
  56.6 4.2 %fusion = f32[10,96,512]{2,1,0:T(8,128)S(1)} fusion(bf16[10,512,512]{2,1,0:T(8,128)(2,1)} %param.8, bf16[10,32,512]{2,1,0:T(8,128)(2,1)S(1)} %get-tuple-element.48, bf16[10,32,512]{2,1,0:T(8,128)(2,1)S(1)} %get-tuple-element.49, bf16[10,32,512]{2,1,0:T(8,128)(2,1)S(1)} %get-tuple-element.47), kind=kOutput, calls=%fused_computation.15 | convolution fusion | flops 506265600 | bytes 8192000 | tf_op jit(solution)/shard_map/dot_general | solution.py:23
  61.2 1.5 multiply_reduce_fusion.14
  64.5 1.7 constant_dynamic-slice_fusion.4
  70.7 2.0 pad_maximum_fusion
  76.1 8.4 %all-to-all-done.3 = f32[8,72,512]{2,1,0:T(8,128)} async-done(((f32[8,72,512]{2,1,0:T(8,128)}), f32[8,72,512]{2,1,0:T(8,128)}, u32[]{:S(2)}, u32[]{:S(2)}) %all-to-all-start.3) | async-done | bytes 1179680 | tf_op jit(solution)/shard_map/all_to_all | solution.py:74
  84.5 4.4 %all-to-all-start.1 = ((f32[8,72,512]{2,1,0:T(8,128)}), f32[8,72,512]{2,1,0:T(8,128)}, u32[]{:S(2)}, u32[]{:S(2)}) async-start(f32[8,72,512]{2,1,0:T(8,128)} %pad_maximum_fusion.2), calls=%async_computation.1 | async-start | bytes 2359296 | tf_op jit(solution)/shard_map/all_to_all | solution.py:74
  88.9 2.3 %slice.341 = f32[8,64,512]{2,1,0:T(8,128)} slice(f32[8,72,512]{2,1,0:T(8,128)} %all-to-all-done.3), slice={[0:8], [0:64], [0:512]} | slice | bytes 2097152 | tf_op jit(solution)/shard_map/slice | solution.py:75
  91.2 25.9 %all-to-all-done.1 = f32[8,72,512]{2,1,0:T(8,128)} async-done(((f32[8,72,512]{2,1,0:T(8,128)}), f32[8,72,512]{2,1,0:T(8,128)}, u32[]{:S(2)}, u32[]{:S(2)}) %all-to-all-start.1) | async-done | bytes 1179680 | tf_op jit(solution)/shard_map/all_to_all | solution.py:74
  124.3 4.3 %fusion.6 = f32[10,96,512]{2,1,0:T(8,128)S(1)} fusion(bf16[10,512,512]{2,1,0:T(8,128)(2,1)} %param.8, bf16[10,32,512]{2,1,0:T(8,128)(2,1)S(1)} %get-tuple-element.45, bf16[10,32,512]{2,1,0:T(8,128)(2,1)S(1)} %get-tuple-element.46, bf16[10,32,512]{2,1,0:T(8,128)(2,1)S(1)} %get-tuple-element.44), kind=kOutput, calls=%fused_computation.21 | convolution fusion | flops 506265600 | bytes 8192000 | tf_op jit(solution)/shard_map/dot_general | solution.py:23
  129.7 1.7 fusion.12
  132.6 2.2 constant_dynamic-update-slice_fusion.3
  139.2 4.3 %all-to-all-start.4 = ((f32[8,72,512]{2,1,0:T(8,128)}), f32[8,72,512]{2,1,0:T(8,128)}, u32[]{:S(2)}, u32[]{:S(2)}) async-start(f32[8,72,512]{2,1,0:T(8,128)} %pad_maximum_fusion.4), calls=%async_computation.4 | async-start | bytes 2359296 | tf_op jit(solution)/shard_map/all_to_all | solution.py:74
  146.7 24.9 %all-to-all-done.4 = f32[8,72,512]{2,1,0:T(8,128)} async-done(((f32[8,72,512]{2,1,0:T(8,128)}), f32[8,72,512]{2,1,0:T(8,128)}, u32[]{:S(2)}, u32[]{:S(2)}) %all-to-all-start.4) | async-done | bytes 1179680 | tf_op jit(solution)/shard_map/all_to_all | solution.py:74
  174.3 4.2 %fusion.18 = f32[10,96,512]{2,1,0:T(8,128)S(1)} fusion(bf16[10,512,512]{2,1,0:T(8,128)(2,1)} %param.8, bf16[10,32,512]{2,1,0:T(8,128)(2,1)S(1)} %get-tuple-element.39, bf16[10,32,512]{2,1,0:T(8,128)(2,1)S(1)} %get-tuple-element.40, bf16[10,32,512]{2,1,0:T(8,128)(2,1)S(1)} %get-tuple-element.38), kind=kOutput, calls=%fused_computation.33 | convolution fusion | flops 506265600 | bytes 8192000 | tf_op jit(solution)/shard_map/dot_general | solution.py:23
  179.7 2.8 %fusion.35 = (f32[4,32,512]{2,1,0:T(8,128)S(1)}, f32[4,32,512]{2,1,0:T(8,128)S(1)}, f32[4,32,512]{2,1,0:T(8,128)S(1)}, f32[4,32,512]{2,1,0:T(8,128)S(1)}) fusion(f32[4,32,512]{2,1,0:T(8,128)S(1)} %copy-done.18, f32[10,32,512]{2,1,0:T(8,128)} %copy-done.7, f32[32]{0:T(128)S(1)} %slice_divide_fusion.3, f32[]{:T(128)} %bitcast.2, f32[]{:T(128)} %bitcast.1, ...), kind=kLoop, calls=%fused_computation.83 | loop fusion | flops 1310720 | bytes 4202760 | tf_op jit(solution)/shard_map/add | solution.py:119
  184.8 3.4 %all-to-all-start.5 = ((f32[8,1,224]{2,1,0:T(1,128)}), f32[8,1,224]{2,1,0:T(1,128)S(1)}, u32[]{:S(2)}, u32[]{:S(2)}) async-start(f32[8,1,224]{2,1,0:T(1,128)} %reshape.227), calls=%async_computation.5 | async-start | bytes 16384 | tf_op jit(solution)/shard_map/all_to_all | solution.py:100
  189.1 5.7 %all-to-all-done.5 = f32[8,1,224]{2,1,0:T(1,128)S(1)} async-done(((f32[8,1,224]{2,1,0:T(1,128)}), f32[8,1,224]{2,1,0:T(1,128)S(1)}, u32[]{:S(2)}, u32[]{:S(2)}) %all-to-all-start.5) | async-done | bytes 7200 | tf_op jit(solution)/shard_map/all_to_all | solution.py:100
  194.7 3.3 %all-to-all-start.2 = ((f32[8,1,224]{2,1,0:T(1,128)}), f32[8,1,224]{2,1,0:T(1,128)S(1)}, u32[]{:S(2)}, u32[]{:S(2)}) async-start(f32[8,1,224]{2,1,0:T(1,128)} %reshape.229), calls=%async_computation.2 | async-start | bytes 16384 | tf_op jit(solution)/shard_map/all_to_all | solution.py:100
  199.4 5.2 %all-to-all-done.2 = f32[8,1,224]{2,1,0:T(1,128)S(1)} async-done(((f32[8,1,224]{2,1,0:T(1,128)}), f32[8,1,224]{2,1,0:T(1,128)S(1)}, u32[]{:S(2)}, u32[]{:S(2)}) %all-to-all-start.2) | async-done | bytes 7200 | tf_op jit(solution)/shard_map/all_to_all | solution.py:100
  208.4 5.2 %all-gather.1 = f32[4,4,64]{2,1,0:T(4,128)S(1)} all-gather(f32[1,4,64]{2,1,0:T(4,128)S(1)} %maximum_bitcast_fusion.5), channel_id=2, replica_groups=mesh['ind'=8,'var'=4] {'var'}, dimensions={0}, use_global_device_ids=true | all-gather | bytes 5120 | tf_op jit(solution)/shard_map/all_gather | solution.py:142
  (206 shorter events, 51.1 us)
Async XLA Ops:
  15.9 8.3 %copy-start.19 = (s32[10]{0:T(128)S(1)}, s32[10]{0:T(128)}, u32[]{:S(2)}) copy-start(s32[10]{0:T(128)} %param.10) | copy-start | bytes 124
  15.9 36.0 %all-to-all-start = ((f32[8,72,512]{2,1,0:T(8,128)}), f32[8,72,512]{2,1,0:T(8,128)S(1)}, u32[]{:S(2)}, u32[]{:S(2)}) async-start(f32[8,72,512]{2,1,0:T(8,128)} %pad_maximum_fusion.1), calls=%async_computation | async-start | bytes 2359296 | tf_op jit(solution)/shard_map/all_to_all | solution.py:74
  23.3 11.6 %copy-start.20 = (s32[10]{0:T(128)S(1)}, s32[10]{0:T(128)}, u32[]{:S(2)}) copy-start(s32[10]{0:T(128)} %param.9) | copy-start | bytes 124
  23.3 41.1 %all-gather.4.cloned.1.call-start = ((), (), s32[]{:S(2)}) async-start(), calls=%async_computation.6 | async-start | bytes 2621440 | tf_op jit(solution)/shard_map/all_gather | solution.py:89
  51.9 4.4 %copy-start = (f32[8,72,512]{2,1,0:T(8,128)}, f32[8,72,512]{2,1,0:T(8,128)S(1)}, u32[]{:S(2)}) copy-start(f32[8,72,512]{2,1,0:T(8,128)S(1)} %all-to-all-done) | copy-start | bytes 3538948
  51.9 32.6 %all-to-all-start.3 = ((f32[8,72,512]{2,1,0:T(8,128)}), f32[8,72,512]{2,1,0:T(8,128)}, u32[]{:S(2)}, u32[]{:S(2)}) async-start(f32[8,72,512]{2,1,0:T(8,128)} %pad_maximum_fusion.3), calls=%async_computation.3 | async-start | bytes 2359296 | tf_op jit(solution)/shard_map/all_to_all | solution.py:74
  61.0 2.6 %copy-start.5 = (f32[10,32,512]{2,1,0:T(8,128)}, f32[10,32,512]{2,1,0:T(8,128)S(1)}, u32[]{:S(2)}) copy-start(f32[10,32,512]{2,1,0:T(8,128)S(1)} %slice_add_fusion.6) | copy-start | bytes 1966084
  61.2 2.4 %copy-start.9 = (f32[4,32,512]{2,1,0:T(8,128)}, f32[4,32,512]{2,1,0:T(8,128)S(1)}, u32[]{:S(2)}) copy-start(f32[4,32,512]{2,1,0:T(8,128)S(1)} %multiply_reduce_fusion.3) | copy-start | bytes 786436
  70.7 2.1 copy-start.16
  70.7 2.1 copy-start.17
  84.5 32.6 %all-to-all-start.1 = ((f32[8,72,512]{2,1,0:T(8,128)}), f32[8,72,512]{2,1,0:T(8,128)}, u32[]{:S(2)}, u32[]{:S(2)}) async-start(f32[8,72,512]{2,1,0:T(8,128)} %pad_maximum_fusion.2), calls=%async_computation.1 | async-start | bytes 2359296 | tf_op jit(solution)/shard_map/all_to_all | solution.py:74
  117.1 1.4 copy-start.13
  117.1 1.6 copy-start.14
  124.1 5.6 %slice-start = ((s8[5242880]{0:T(1024)(128)(4,1)}), s8[4194304]{0:T(1024)(128)(4,1)S(1)}, s32[]{:S(2)}) async-start(s8[5242880]{0:T(1024)(128)(4,1)} %bitcast.125), calls=%async_computation.7 | async-start | bytes 8388608
  124.3 5.4 %slice-start.1 = ((s8[5242880]{0:T(1024)(128)(4,1)}), s8[1048576]{0:T(1024)(128)(4,1)S(1)}, s32[]{:S(2)}) async-start(s8[5242880]{0:T(1024)(128)(4,1)} %bitcast.125), calls=%async_computation.8 | async-start | bytes 2097152
  131.6 4.0 %copy-start.6 = (f32[10,32,512]{2,1,0:T(8,128)}, f32[10,32,512]{2,1,0:T(8,128)S(1)}, u32[]{:S(2)}) copy-start(f32[10,32,512]{2,1,0:T(8,128)S(1)} %slice_add_fusion.2) | copy-start | bytes 1966084
  132.6 3.1 %copy-start.11 = (f32[4,32,512]{2,1,0:T(8,128)}, f32[4,32,512]{2,1,0:T(8,128)S(1)}, u32[]{:S(2)}) copy-start(f32[4,32,512]{2,1,0:T(8,128)S(1)} %get-tuple-element.15) | copy-start | bytes 786436
  139.2 32.4 %all-to-all-start.4 = ((f32[8,72,512]{2,1,0:T(8,128)}), f32[8,72,512]{2,1,0:T(8,128)}, u32[]{:S(2)}, u32[]{:S(2)}) async-start(f32[8,72,512]{2,1,0:T(8,128)} %pad_maximum_fusion.4), calls=%async_computation.4 | async-start | bytes 2359296 | tf_op jit(solution)/shard_map/all_to_all | solution.py:74
  171.6 1.4 copy-start.15
  178.5 1.2 copy-start.18
  182.5 1.6 copy-start.3
  182.5 1.5 copy-start.4
  184.8 9.9 %all-to-all-start.5 = ((f32[8,1,224]{2,1,0:T(1,128)}), f32[8,1,224]{2,1,0:T(1,128)S(1)}, u32[]{:S(2)}, u32[]{:S(2)}) async-start(f32[8,1,224]{2,1,0:T(1,128)} %reshape.227), calls=%async_computation.5 | async-start | bytes 16384 | tf_op jit(solution)/shard_map/all_to_all | solution.py:100
  194.7 9.8 %all-to-all-start.2 = ((f32[8,1,224]{2,1,0:T(1,128)}), f32[8,1,224]{2,1,0:T(1,128)S(1)}, u32[]{:S(2)}, u32[]{:S(2)}) async-start(f32[8,1,224]{2,1,0:T(1,128)} %reshape.229), calls=%async_computation.2 | async-start | bytes 16384 | tf_op jit(solution)/shard_map/all_to_all | solution.py:100
  (6 other events, 5.7 us)
Sparse Core Ops, SparseCore 0:
  25.7 23.9 all-gather.3

commit v4 on v3

--- a/solution.py
+++ b/solution.py
@@ -6,7 +6,7 @@
 VARS_GENE = 4
 NEED = 2
 PAD_ROWS = 8
-CHUNKS = 2
+CHUNKS = 1
 
 
 def split3(x):

time: 223 us -> 187 us (0.84)
  starting transfers between devices: 27.1 us -> 15.5 us
  local copies, waits for them, and re-layouts: 35.5 us -> 24.8 us
  other arithmetic: 29.8 us -> 22.7 us
  matrix products: 14.4 us -> 8.66 us
    all_gather x1, waiting for transfers between devices: 0.01 us -> 11.5 us  [local(): geno_all = lax.all_gather(genotypes, 'var', axis=0, tiled=True)]
    all_to_all x4 -> x2, starting transfers between devices: 20.4 us -> 11.9 us  [exchange(): lax.all_to_all(pieces, 'ind', split_axis=0, concat_axis=0, tiled=True)]
    all_to_all x4 -> x2, waiting for transfers between devices: 70.9 us -> 63.5 us  [exchange(): lax.all_to_all(pieces, 'ind', split_axis=0, concat_axis=0, tiled=True)]
    unnamed x78 -> x48, local copies, waits for them, and re-layouts: 11.8 us -> 5.71 us
    dot_general x4 -> x2, matrix products: 14.4 us -> 8.66 us  [batched_tile_dot(): lax.dot_general(parts, tiles, (((2,), (2,)), ((0,), (0,))), preferred_ele...]
    all_to_all x2 -> x1, waiting for transfers between devices: 10.8 us -> 6.42 us  [reduce_ind(): lax.all_to_all(spread, 'ind', split_axis=0, concat_axis=0, tiled=True)]
    all_to_all x2 -> x1, starting transfers between devices: 6.71 us -> 3.53 us  [reduce_ind(): lax.all_to_all(spread, 'ind', split_axis=0, concat_axis=0, tiled=True)]
    slice x4 -> x2, local copies, waits for them, and re-layouts: 5.11 us -> 2.06 us  [exchange(): tiles_in = arrived[:, :NEED * width].reshape(peers * NEED, width, tile_size)]
  transfers between devices with their start and end apart: 7 -> 4, of which waited for: 6 -> 4; matrix products, arithmetic and copies ran while one was open for 14% -> 7% of each run, Pallas kernels for 0% -> 0%
where the time goes in v4:
time: 187 us; the launch traced here: 186 us
  waiting for transfers between devices  82.1 us (44%)
  between operations  26.7 us (14%)
  local copies, waits for them, and re-layouts  24.8 us (13%)
  other arithmetic  22.7 us (12%)
  starting transfers between devices  15.5 us (8%)
  matrix products  8.66 us (5%)
  blocking collectives  5.18 us (3%)
    all_to_all x2, waiting for transfers between devices, exchange(): lax.all_to_all(pieces, 'ind', split_axis=0, concat_axis=0, tiled=True)  63.5 us
    all_to_all x2, starting transfers between devices, exchange(): lax.all_to_all(pieces, 'ind', split_axis=0, concat_axis=0, tiled=True)  11.9 us
    all_gather x1, waiting for transfers between devices, local(): geno_all = lax.all_gather(genotypes, 'var', axis=0, tiled=True)  11.5 us
    dot_general x2, matrix products, batched_tile_dot(): lax.dot_general(parts, tiles, (((2,), (2,)), ((0,), (0,))), preferred_ele...  8.66 us
    reshape x4, local copies, waits for them, and re-layouts, to_tiles(): return jnp.transpose(x.reshape(cols_here, row_tiles, tile_size), (1, 0, 2))  6.53 us
    all_to_all x1, waiting for transfers between devices, reduce_ind(): lax.all_to_all(spread, 'ind', split_axis=0, concat_axis=0, tiled=True)  6.42 us
    unnamed x48, local copies, waits for them, and re-layouts  5.71 us
    all_gather x1, blocking collectives, local(): gathered = lax.all_gather(gram_part, 'var', axis=0, tiled=False)  5.18 us
  transfers between devices with their start and end apart: 4, of which 4 were waited for; matrix products, arithmetic and copies ran while one was open for 7% of the time, Pallas kernels for 0%

profile of v4, /device:TPU:0, one launch (start us, length us, event | category | flops | bytes accessed | tf_op | source)
XLA Modules:
  0.0 185.6 jit_solution(11410289058006568142)
XLA Ops:
  7.3 1.4 fusion.37
  8.7 2.4 %select_reduce_fusion = f32[4,512]{1,0:T(4,128)S(1)} fusion(bf16[10,512,512]{2,1,0:T(8,128)(2,1)} %param.8, pred[512,512]{1,0:T(8,128)(4,1)S(1)} %iota_compare_fusion), kind=kLoop, calls=%fused_computation | loop fusion | flops 3143680 | bytes 2367488 | tf_op jit(solution)/shard_map/reduce_sum | solution.py:47
  11.1 1.3 multiply_add_fusion.1
  14.1 1.7 pad_maximum_fusion
  15.7 7.4 %all-to-all-start = ((f32[8,136,512]{2,1,0:T(8,128)}), f32[8,136,512]{2,1,0:T(8,128)S(1)}, u32[]{:S(2)}, u32[]{:S(2)}) async-start(f32[8,136,512]{2,1,0:T(8,128)} %pad_maximum_fusion), calls=%async_computation | async-start | bytes 4456448 | tf_op jit(solution)/shard_map/all_to_all | solution.py:74
  32.3 1.1 copy.34
  38.1 11.5 %all-gather.4.cloned.1.call-done = f32[256,2048]{1,0:T(8,128)} async-done(((f32[64,2048]{1,0:T(8,128)}), f32[256,2048]{1,0:T(8,128)}) %all-gather.4.cloned.1.call-update) | async-done | bytes 2097168 | tf_op jit(solution)/shard_map/all_gather | solution.py:89
  49.6 2.7 %constant_dynamic-slice_fusion.4 = (f32[64,2048]{1,0:T(8,128)S(1)}, f32[64,2048]{1,0:T(8,128)}, f32[64,2048]{1,0:T(8,128)}, f32[64,2048]{1,0:T(8,128)}) fusion(f32[256,2048]{1,0:T(8,128)} %all-gather.4.cloned.1.call-done, s32[]{:T(128)S(6)} %select_n.83, s32[]{:T(128)S(6)} %select_n.86, s32[]{:T(128)S(6)} %select_n.85, s32[]{:T(128)S(6)} %select_n.84), kind=kLoop, calls=%fused_computation.80 | loop fusion | bytes 4194320 | tf_op jit(solution)/shard_map/dynamic_slice | solution.py:94
  52.6 1.6 reshape.149
  54.2 2.4 %reshape.148 = f32[64,4,512]{2,1,0:T(4,128)} reshape(f32[64,2048]{1,0:T(8,128)} %get-tuple-element.14) | data formatting | bytes 1048576 | tf_op jit(solution)/shard_map/reshape | solution.py:60
  56.6 2.2 %reshape.147 = f32[64,4,512]{2,1,0:T(4,128)} reshape(f32[64,2048]{1,0:T(8,128)} %get-tuple-element.15) | data formatting | bytes 1048576 | tf_op jit(solution)/shard_map/reshape | solution.py:60
  58.8 2.2 %multiply_reduce_fusion.3 = f32[4,64]{1,0:T(4,128)S(1)} fusion(f32[4,64,512]{2,0,1:T(4,128)} %copy.34, f32[1,4,64,512]{3,1,2,0:T(4,128)S(1)} %bitcast.146, f32[1,4,64,512]{3,1,2,0:T(4,128)} %bitcast.148, f32[1,4,64,512]{3,1,2,0:T(4,128)} %bitcast.150, f32[1,4,64,512]{3,1,2,0:T(4,128)S(1)} %bitcast.144), kind=kLoop, calls=%fused_computation.7 | loop fusion | flops 2621184 | bytes 2622464 | tf_op jit(solution)/shard_map/reduce_sum | solution.py:109
  61.1 13.1 %all-to-all-done = f32[8,136,512]{2,1,0:T(8,128)S(1)} async-done(((f32[8,136,512]{2,1,0:T(8,128)}), f32[8,136,512]{2,1,0:T(8,128)S(1)}, u32[]{:S(2)}, u32[]{:S(2)}) %all-to-all-start) | async-done | bytes 2228256 | tf_op jit(solution)/shard_map/all_to_all | solution.py:74
  76.1 4.3 %fusion = f32[10,192,512]{2,1,0:T(8,128)S(1)} fusion(bf16[10,512,512]{2,1,0:T(8,128)(2,1)} %param.8, bf16[10,64,512]{2,1,0:T(8,128)(2,1)S(1)} %get-tuple-element.20, bf16[10,64,512]{2,1,0:T(8,128)(2,1)S(1)} %get-tuple-element.21, bf16[10,64,512]{2,1,0:T(8,128)(2,1)S(1)} %get-tuple-element.19), kind=kOutput, calls=%fused_computation.8 | convolution fusion | flops 1012531200 | bytes 11141120 | tf_op jit(solution)/shard_map/dot_general | solution.py:23
  82.3 2.4 %constant_dynamic-update-slice_fusion.1 = (f32[10,64,512]{2,1,0:T(8,128)}, f32[4,64,512]{2,1,0:T(8,128)S(1)}, f32[4,64,512]{2,1,0:T(8,128)S(1)}) fusion(f32[4,512]{1,0:T(4,128)S(1)} %multiply_add_fusion.1, f32[4,64,512]{2,1,0:T(8,128)S(1)} %multiply_reduce_fusion.1, f32[10,64,512]{2,1,0:T(8,128)S(1)} %slice_add_fusion.2, f32[]{:T(128)} %bitcast.2, ...), kind=kLoop, calls=%fused_computation.73 | loop fusion | flops 786431 | bytes 3153928
  88.4 1.6 pad_maximum_fusion.1
  90.0 4.5 %all-to-all-start.1 = ((f32[8,136,512]{2,1,0:T(8,128)}), f32[8,136,512]{2,1,0:T(8,128)}, u32[]{:S(2)}, u32[]{:S(2)}) async-start(f32[8,136,512]{2,1,0:T(8,128)} %pad_maximum_fusion.1), calls=%async_computation.1 | async-start | bytes 4456448 | tf_op jit(solution)/shard_map/all_to_all | solution.py:74
  94.6 50.4 %all-to-all-done.1 = f32[8,136,512]{2,1,0:T(8,128)} async-done(((f32[8,136,512]{2,1,0:T(8,128)}), f32[8,136,512]{2,1,0:T(8,128)}, u32[]{:S(2)}, u32[]{:S(2)}) %all-to-all-start.1) | async-done | bytes 2228256 | tf_op jit(solution)/shard_map/all_to_all | solution.py:74
  145.1 1.9 %slice.183 = f32[8,128,512]{2,1,0:T(8,128)S(1)} slice(f32[8,136,512]{2,1,0:T(8,128)} %all-to-all-done.1), slice={[0:8], [0:128], [0:512]} | slice | bytes 4194304 | tf_op jit(solution)/shard_map/slice | solution.py:75
  148.6 4.3 %fusion.6 = f32[10,192,512]{2,1,0:T(8,128)S(1)} fusion(bf16[10,512,512]{2,1,0:T(8,128)(2,1)} %param.8, bf16[10,64,512]{2,1,0:T(8,128)(2,1)S(1)} %get-tuple-element.17, bf16[10,64,512]{2,1,0:T(8,128)(2,1)S(1)} %get-tuple-element.18, bf16[10,64,512]{2,1,0:T(8,128)(2,1)S(1)} %get-tuple-element.16), kind=kOutput, calls=%fused_computation.14 | convolution fusion | flops 1012531200 | bytes 11141120 | tf_op jit(solution)/shard_map/dot_general | solution.py:23
  154.4 2.8 %fusion.21 = (f32[4,64,512]{2,1,0:T(8,128)S(1)}, f32[4,64,512]{2,1,0:T(8,128)S(1)}) fusion(f32[4,64,512]{2,1,0:T(8,128)S(1)} %multiply_reduce_fusion, f32[10,64,512]{2,1,0:T(8,128)S(1)} %slice_add_fusion, f32[64]{0:T(128)S(1)} %slice_divide_fusion, f32[]{:T(128)} %bitcast.2, f32[]{:T(128)} %bitcast.1, f32[4,64,512]{2,1,0:T(8,128)S(1)} %copy-done.4, ...), kind=kLoop, calls=%fused_computation.46 | loop fusion | flops 1310720 | bytes 4202760 | tf_op jit(solution)/shard_map/add | solution.py:119
  160.3 3.5 %all-to-all-start.2 = ((f32[8,1,448]{2,1,0:T(1,128)}), f32[8,1,448]{2,1,0:T(1,128)S(1)}, u32[]{:S(2)}, u32[]{:S(2)}) async-start(f32[8,1,448]{2,1,0:T(1,128)} %reshape.166), calls=%async_computation.2 | async-start | bytes 32768 | tf_op jit(solution)/shard_map/all_to_all | solution.py:100
  164.0 6.4 %all-to-all-done.2 = f32[8,1,448]{2,1,0:T(1,128)S(1)} async-done(((f32[8,1,448]{2,1,0:T(1,128)}), f32[8,1,448]{2,1,0:T(1,128)S(1)}, u32[]{:S(2)}, u32[]{:S(2)}) %all-to-all-start.2) | async-done | bytes 14368 | tf_op jit(solution)/shard_map/all_to_all | solution.py:100
  172.8 5.2 %all-gather.1 = f32[4,4,64]{2,1,0:T(4,128)S(1)} all-gather(f32[1,4,64]{2,1,0:T(4,128)S(1)} %add_bitcast_fusion.1), channel_id=2, replica_groups=mesh['ind'=8,'var'=4] {'var'}, dimensions={0}, use_global_device_ids=true | all-gather | bytes 5120 | tf_op jit(solution)/shard_map/all_gather | solution.py:142
  (112 shorter events, 20.5 us)
Async XLA Ops:
  7.2 5.3 %copy-start = (f32[64,2048]{1,0:T(8,128)S(1)}, f32[64,2048]{1,0:T(8,128)}, u32[]{:S(2)}) copy-start(f32[64,2048]{1,0:T(8,128)} %param.6) | copy-start | bytes 1572868
  15.7 8.2 %copy-start.14 = (s32[10]{0:T(128)S(1)}, s32[10]{0:T(128)}, u32[]{:S(2)}) copy-start(s32[10]{0:T(128)} %param.10) | copy-start | bytes 124
  15.7 18.4 %copy-start.15 = (s32[10]{0:T(128)S(1)}, s32[10]{0:T(128)}, u32[]{:S(2)}) copy-start(s32[10]{0:T(128)} %param.9) | copy-start | bytes 124
  15.7 58.5 %all-to-all-start = ((f32[8,136,512]{2,1,0:T(8,128)}), f32[8,136,512]{2,1,0:T(8,128)S(1)}, u32[]{:S(2)}, u32[]{:S(2)}) async-start(f32[8,136,512]{2,1,0:T(8,128)} %pad_maximum_fusion), calls=%async_computation | async-start | bytes 4456448 | tf_op jit(solution)/shard_map/all_to_all | solution.py:74
  23.2 26.4 %all-gather.4.cloned.1.call-start = ((), (), s32[]{:S(2)}) async-start(), calls=%async_computation.3 | async-start | bytes 2621440 | tf_op jit(solution)/shard_map/all_gather | solution.py:89
  52.6 8.5 %copy-start.5 = (f32[64,4,512]{2,1,0:T(4,128)}, f32[64,4,512]{2,1,0:T(4,128)S(1)}, u32[]{:S(2)}) copy-start(f32[64,4,512]{2,1,0:T(4,128)S(1)} %reshape.146) | copy-start | bytes 1572868
  54.2 6.9 %copy-start.7 = (f32[64,4,512]{2,1,0:T(4,128)}, f32[64,4,512]{2,1,0:T(4,128)S(1)}, u32[]{:S(2)}) copy-start(f32[64,4,512]{2,1,0:T(4,128)S(1)} %reshape.149) | copy-start | bytes 1572868
  74.2 1.3 copy-start.12
  80.8 3.8 %copy-start.2 = (f32[10,64,512]{2,1,0:T(8,128)}, f32[10,64,512]{2,1,0:T(8,128)S(1)}, u32[]{:S(2)}) copy-start(f32[10,64,512]{2,1,0:T(8,128)S(1)} %slice_add_fusion.2) | copy-start | bytes 3932164
  80.9 1.4 copy-start.1
  82.3 3.2 %copy-start.3 = (f32[4,64,512]{2,1,0:T(8,128)}, f32[4,64,512]{2,1,0:T(8,128)S(1)}, u32[]{:S(2)}) copy-start(f32[4,64,512]{2,1,0:T(8,128)S(1)} %multiply_reduce_fusion.1) | copy-start | bytes 1572868
  84.6 0.9 copy-start.11
  90.0 55.1 %all-to-all-start.1 = ((f32[8,136,512]{2,1,0:T(8,128)}), f32[8,136,512]{2,1,0:T(8,128)}, u32[]{:S(2)}, u32[]{:S(2)}) async-start(f32[8,136,512]{2,1,0:T(8,128)} %pad_maximum_fusion.1), calls=%async_computation.1 | async-start | bytes 4456448 | tf_op jit(solution)/shard_map/all_to_all | solution.py:74
  145.0 1.9 %copy-start.13 = (f32[10,64,512]{2,1,0:T(8,128)S(1)}, f32[10,64,512]{2,1,0:T(8,128)}, u32[]{:S(2)}) copy-start(f32[10,64,512]{2,1,0:T(8,128)} %get-tuple-element.9) | copy-start | bytes 3932164
  153.3 1.0 copy-start.4
  157.2 1.0 copy-start.6
  157.2 1.2 copy-start.8
  157.2 1.3 copy-start.9
  157.2 1.5 copy-start.10
  160.3 10.1 %all-to-all-start.2 = ((f32[8,1,448]{2,1,0:T(1,128)}), f32[8,1,448]{2,1,0:T(1,128)S(1)}, u32[]{:S(2)}, u32[]{:S(2)}) async-start(f32[8,1,448]{2,1,0:T(1,128)} %reshape.166), calls=%async_computation.2 | async-start | bytes 32768 | tf_op jit(solution)/shard_map/all_to_all | solution.py:100
Sparse Core Ops, SparseCore 0:
  25.5 23.9 all-gather.3

commit v5 on v4

--- a/solution.py
+++ b/solution.py
@@ -67,18 +67,24 @@
         width = x.shape[1]
         rolled = rolled.reshape(row_tiles, NEED * width, tile_size)
         pieces = jnp.tile(rolled, (peers // row_tiles, 1, 1))
-        flat = extra.reshape(-1)
-        flat = jnp.pad(flat, (0, PAD_ROWS * tile_size - flat.shape[0]))
-        side = jnp.broadcast_to(flat.reshape(1, PAD_ROWS, tile_size), (peers, PAD_ROWS, tile_size))
-        pieces = jnp.concatenate([pieces, side], axis=1)
+        if extra is not None:
+            flat = extra.reshape(-1)
+            flat = jnp.pad(flat, (0, PAD_ROWS * tile_size - flat.shape[0]))
+            side = jnp.broadcast_to(flat.reshape(1, PAD_ROWS, tile_size), (peers, PAD_ROWS, tile_size))
+            pieces = jnp.concatenate([pieces, side], axis=1)
         arrived = lax.all_to_all(pieces, "ind", split_axis=0, concat_axis=0, tiled=True)
-        tiles_in = arrived[:, :NEED * width].reshape(peers * NEED, width, tile_size)
-        sums = jnp.sum(arrived[:, NEED * width:].reshape(peers, -1)[:, :extra.size], axis=0)
-        return tiles_in, sums.reshape(extra.shape)
+        sums = None
+        if extra is not None:
+            sums = jnp.sum(arrived[:, NEED * width:].reshape(peers, -1)[:, :extra.size], axis=0)
+            sums = sums.reshape(extra.shape)
+        return arrived, sums
 
-    def kprod(x, tiles_in):
-        picked = jnp.stack([lax.dynamic_index_in_dim(tiles_in, position[s], 0, keepdims=False)
-                            for s in range(off_count)])
+    def kprod(x, arrived):
+        width = x.shape[1]
+        picked = jnp.stack([
+            lax.dynamic_slice(arrived, (position[s] // NEED, position[s] % NEED * width, 0),
+                              (1, width, tile_size))[0]
+            for s in range(off_count)])
         prod = batched_tile_dot(jnp.concatenate([x, picked], axis=0), grm_tiles)
         far = prod[row_tiles:]
         return prod[:row_tiles] + jnp.sum(weight[:, :, None, None] * far[:, None], axis=0)
@@ -95,22 +101,18 @@
          for a in range(VARS_GENE)]
     )
 
-    def reduce_ind(x):
-        spread = jnp.broadcast_to(x[None], (peers,) + x.shape)
-        return jnp.sum(lax.all_to_all(spread, "ind", split_axis=0, concat_axis=0, tiled=True), axis=0)
-
     def chunk(g, geno_sub):
         z0 = g / precond
-        tiles0, sums0 = exchange(z0, colsum(g * z0)[None])
-        rz0 = sums0[0]
+        tiles0, _ = exchange(z0, None)
         kz0 = kprod(z0, tiles0)
         image0 = tau0 * z0 + tau1 * kz0
         w = image0 / precond
         p0_local = jnp.sum(geno_sub * z0[None], axis=(1, 3))
-        extra1 = jnp.concatenate([colsum(z0 * image0)[None], p0_local], axis=0)
+        extra1 = jnp.concatenate([colsum(g * z0)[None], colsum(z0 * image0)[None], p0_local], axis=0)
         tiles1, sums1 = exchange(w, extra1)
-        dad0 = sums1[0]
-        p0 = sums1[1:]
+        rz0 = sums1[0]
+        dad0 = sums1[1]
+        p0 = sums1[2:]
         alpha0 = rz0 / dad0
         resid1 = g - alpha0[None, :, None] * image0
         z1 = resid1 / precond
@@ -122,15 +124,28 @@
              colsum(z1 * image0 + z0 * az1)[None], jnp.sum(geno_sub * z1[None], axis=(1, 3))],
             axis=0,
         )
-        red = reduce_ind(red_local)
-        rz1 = red[0]
-        beta = rz1 / rz0
-        dad1 = red[1] + beta * (red[2] + beta * dad0)
-        alpha1 = rz1 / dad1
+        lead = (me == 0).astype(jnp.float32)
+        payload = jnp.concatenate(
+            [red_local, lead * rz0[None], lead * dad0[None], lead * p0], axis=0)
+        spread = jnp.broadcast_to(payload[None], (peers * nvar,) + payload.shape)
+        got = lax.all_to_all(spread, ("ind", "var"), split_axis=0, concat_axis=0, tiled=True)
+        tot = jnp.sum(got.reshape((peers, nvar) + payload.shape), axis=0)
+        nv = VARS_GENE
+        rz1_all = tot[:, 0]
+        rz0_all = tot[:, 3 + nv]
+        dad0_all = tot[:, 4 + nv]
+        p0_all = tot[:, 5 + nv:]
+        p1_all = tot[:, 3:3 + nv]
+        alpha0_all = rz0_all / dad0_all
+        beta_all = rz1_all / rz0_all
+        dad1_all = tot[:, 1] + beta_all * (tot[:, 2] + beta_all * dad0_all)
+        alpha1_all = rz1_all / dad1_all
+        mine = lambda t: lax.dynamic_index_in_dim(t, v, 0, keepdims=False)
+        beta = mine(beta_all)
+        alpha1 = mine(alpha1_all)
         dir1 = z1 + beta[None, :, None] * z0
         sol = alpha0[None, :, None] * z0 + alpha1[None, :, None] * dir1
-        p1 = red[3:]
-        part = alpha0[None] * p0 + alpha1[None] * (p1 + beta[None] * p0)
+        part = alpha0_all[:, None] * p0_all + alpha1_all[:, None] * (p1_all + beta_all[:, None] * p0_all)
         return sol, part
 
     g_all = to_tiles(genotypes)
@@ -138,9 +153,8 @@
     outs = [chunk(g_all[:, k * width:(k + 1) * width], geno_sub[:, :, k * width:(k + 1) * width])
             for k in range(CHUNKS)]
     solution = jnp.concatenate([o[0] for o in outs], axis=1)
-    gram_part = jnp.concatenate([o[1] for o in outs], axis=1)
-    gathered = lax.all_gather(gram_part, "var", axis=0, tiled=False)
-    full = jnp.transpose(gathered, (1, 0, 2)).reshape(VARS_GENE, ncol)
+    gram_part = jnp.concatenate([o[1] for o in outs], axis=2)
+    full = jnp.transpose(gram_part, (1, 0, 2)).reshape(VARS_GENE, ncol)
     gram_cols = lax.dynamic_index_in_dim(full, a_out, 0, keepdims=False)
     gram_cols = lax.dynamic_slice_in_dim(gram_cols.reshape(VARS_GENE, genes), g0, cols_here, 1)
     gene_gram = jnp.transpose(gram_cols) / total_ind

time: 187 us -> 199 us (1.064)
  local copies, waits for them, and re-layouts: 24.8 us -> 38.3 us
  blocking collectives: 5.18 us -> 0 us
  between operations: 26.7 us -> 30.7 us
  other arithmetic: 22.7 us -> 20.7 us
    unnamed x48 -> x40, local copies, waits for them, and re-layouts: 5.71 us -> 18.9 us
    all_gather x1, waiting for transfers between devices: 11.5 us -> 0.01 us  [local(): geno_all = lax.all_gather(genotypes, 'var', axis=0, tiled=True)]
    all_to_all x2, waiting for transfers between devices: 63.5 us -> 74.7 us  [exchange(): lax.all_to_all(pieces, 'ind', split_axis=0, concat_axis=0, tiled=True)]
    all_gather x1 -> x0, blocking collectives: 5.18 us -> none  [local(): gathered = lax.all_gather(gram_part, 'var', axis=0, tiled=False)]
    reshape x4, local copies, waits for them, and re-layouts: 6.53 us -> 2.63 us  [to_tiles(): return jnp.transpose(x.reshape(cols_here, row_tiles, tile_size), (1, 0, 2))]
    concatenate x2, local copies, waits for them, and re-layouts: 0.04 us -> 3.12 us  [kprod(): prod = batched_tile_dot(jnp.concatenate([x, picked], axis=0), grm_tiles)]
    convert_element_type x2, other arithmetic: 0.76 us -> 3.37 us  [split3(): hi.astype(jnp.bfloat16)]
    slice x5 -> x1, local copies, waits for them, and re-layouts: 2.89 us -> 0.67 us  [kprod(): position[s] // NEED]
  transfers between devices with their start and end apart: 4 -> 4, of which waited for: 4 -> 3; matrix products, arithmetic and copies ran while one was open for 7% -> 8% of each run, Pallas kernels for 0% -> 0%
where the time goes in v5:
time: 199 us; the launch traced here: 197 us
  waiting for transfers between devices  83.3 us (42%)
  local copies, waits for them, and re-layouts  38.3 us (19%)
  between operations  30.7 us (15%)
  other arithmetic  20.7 us (10%)
  starting transfers between devices  15.6 us (8%)
  matrix products  8.66 us (4%)
    all_to_all x2, waiting for transfers between devices, exchange(): lax.all_to_all(pieces, 'ind', split_axis=0, concat_axis=0, tiled=True)  74.7 us
    unnamed x40, local copies, waits for them, and re-layouts  18.9 us
    all_to_all x2, starting transfers between devices, exchange(): lax.all_to_all(pieces, 'ind', split_axis=0, concat_axis=0, tiled=True)  11.9 us
    dot_general x2, matrix products, batched_tile_dot(): lax.dot_general(parts, tiles, (((2,), (2,)), ((0,), (0,))), preferred_ele...  8.66 us
    all_to_all x1, waiting for transfers between devices, chunk(): lax.all_to_all(spread, ('ind', 'var'), split_axis=0, concat_axis=0, tiled...  7.98 us
  transfers between devices with their start and end apart: 4, of which 3 were waited for; matrix products, arithmetic and copies ran while one was open for 8% of the time, Pallas kernels for 0%

profile of v5, /device:TPU:0, one launch (start us, length us, event | category | flops | bytes accessed | tf_op | source)
XLA Modules:
  0.0 197.4 jit_solution(6268582079524255567)
XLA Ops:
  9.3 2.4 %select_reduce_fusion = f32[4,512]{1,0:T(4,128)S(1)} fusion(bf16[10,512,512]{2,1,0:T(8,128)(2,1)} %param.8, pred[512,512]{1,0:T(8,128)(4,1)S(1)} %iota_compare_fusion), kind=kLoop, calls=%fused_computation | loop fusion | flops 3143680 | bytes 2367488 | tf_op jit(solution)/shard_map/reduce_sum | solution.py:47
  14.2 1.6 tile.21
  15.9 7.4 %all-to-all-start = ((f32[8,128,512]{2,1,0:T(8,128)}), f32[8,128,512]{2,1,0:T(8,128)}, u32[]{:S(2)}, u32[]{:S(2)}) async-start(f32[8,128,512]{2,1,0:T(8,128)} %bitcast.6), calls=%async_computation | async-start | bytes 4194304 | tf_op jit(solution)/shard_map/all_to_all | solution.py:75
  40.7 2.5 %constant_dynamic-slice_fusion.6 = (f32[64,2048]{1,0:T(8,128)S(1)}, f32[64,2048]{1,0:T(8,128)S(1)}, f32[64,2048]{1,0:T(8,128)S(1)}, f32[64,2048]{1,0:T(8,128)}) fusion(f32[256,2048]{1,0:T(8,128)} %all-gather.2.cloned.1.call-done, s32[]{:T(128)S(6)} %select_n.201, s32[]{:T(128)S(6)} %select_n.204, s32[]{:T(128)S(6)} %select_n.203, s32[]{:T(128)S(6)} %select_n.202), kind=kLoop, calls=%fused_computation.84 | loop fusion | bytes 4194320 | tf_op jit(solution)/shard_map/dynamic_slice | solution.py:100
  44.3 1.6 reshape.139
  47.4 24.2 %all-to-all-done = f32[8,128,512]{2,1,0:T(8,128)} async-done(((f32[8,128,512]{2,1,0:T(8,128)}), f32[8,128,512]{2,1,0:T(8,128)}, u32[]{:S(2)}, u32[]{:S(2)}) %all-to-all-start) | async-done | bytes 2097184 | tf_op jit(solution)/shard_map/all_to_all | solution.py:75
  73.2 1.6 dynamic-slice_dynamic-update-slice_fusion.10
  76.3 1.6 dynamic-slice_dynamic-update-slice_fusion.8
  81.0 1.7 reduce-precision_convert_fusion.3
  82.7 4.3 %fusion = f32[10,192,512]{2,1,0:T(8,128)S(1)} fusion(bf16[10,512,512]{2,1,0:T(8,128)(2,1)} %param.8, bf16[10,64,512]{2,1,0:T(8,128)(2,1)S(1)} %get-tuple-element.24, bf16[10,64,512]{2,1,0:T(8,128)(2,1)S(1)} %get-tuple-element.25, bf16[10,64,512]{2,1,0:T(8,128)(2,1)S(1)} %get-tuple-element.23), kind=kOutput, calls=%fused_computation.7 | convolution fusion | flops 1012531200 | bytes 11141120 | tf_op jit(solution)/shard_map/dot_general | solution.py:23
  87.9 2.3 %constant_dynamic-update-slice_fusion.1 = (f32[10,64,512]{2,1,0:T(8,128)}, f32[4,64,512]{2,1,0:T(8,128)S(1)}, f32[4,64,512]{2,1,0:T(8,128)S(1)}) fusion(f32[4,512]{1,0:T(4,128)S(1)} %multiply_add_fusion.1, f32[4,64,512]{2,1,0:T(8,128)S(1)} %multiply_reduce_fusion.1, f32[10,64,512]{2,1,0:T(8,128)S(1)} %slice_add_fusion.2, f32[]{:T(128)} %bitcast.2, ...), kind=kLoop, calls=%fused_computation.71 | loop fusion | flops 786431 | bytes 3153928
  96.5 1.6 pad_maximum_fusion
  98.1 4.5 %all-to-all-start.1 = ((f32[8,136,512]{2,1,0:T(8,128)}), f32[8,136,512]{2,1,0:T(8,128)}, u32[]{:S(2)}, u32[]{:S(2)}) async-start(f32[8,136,512]{2,1,0:T(8,128)} %pad_maximum_fusion), calls=%async_computation.1 | async-start | bytes 4456448 | tf_op jit(solution)/shard_map/all_to_all | solution.py:75
  102.7 50.5 %all-to-all-done.1 = f32[8,136,512]{2,1,0:T(8,128)} async-done(((f32[8,136,512]{2,1,0:T(8,128)}), f32[8,136,512]{2,1,0:T(8,128)}, u32[]{:S(2)}, u32[]{:S(2)}) %all-to-all-start.1) | async-done | bytes 2228256 | tf_op jit(solution)/shard_map/all_to_all | solution.py:75
  154.4 1.6 dynamic-slice_dynamic-update-slice_fusion.5
  155.9 1.6 dynamic-slice_dynamic-update-slice_fusion.4
  159.1 1.6 dynamic-slice_dynamic-update-slice_fusion.2
  160.6 1.6 dynamic-slice_dynamic-update-slice_fusion.1
  162.2 1.6 dynamic-slice_dynamic-update-slice_fusion
  163.8 1.7 reduce-precision_convert_fusion.1
  165.5 4.3 %fusion.6 = f32[10,192,512]{2,1,0:T(8,128)S(1)} fusion(bf16[10,512,512]{2,1,0:T(8,128)(2,1)} %param.8, bf16[10,64,512]{2,1,0:T(8,128)(2,1)S(1)} %get-tuple-element.21, bf16[10,64,512]{2,1,0:T(8,128)(2,1)S(1)} %get-tuple-element.22, bf16[10,64,512]{2,1,0:T(8,128)(2,1)S(1)} %get-tuple-element.20), kind=kOutput, calls=%fused_computation.13 | convolution fusion | flops 1012531200 | bytes 11141120 | tf_op jit(solution)/shard_map/dot_general | solution.py:23
  170.6 1.6 fusion.21
  175.5 3.6 %all-to-all-start.2 = ((f32[32,1,832]{2,1,0:T(1,128)}), f32[32,1,832]{2,1,0:T(1,128)S(1)}, u32[]{:S(2)}, u32[]{:S(2)}) async-start(f32[32,1,832]{2,1,0:T(1,128)} %reshape.154), calls=%async_computation.2 | async-start | bytes 229376 | tf_op jit(solution)/shard_map/all_to_all | solution.py:131
  179.1 8.0 %all-to-all-done.2 = f32[32,1,832]{2,1,0:T(1,128)S(1)} async-done(((f32[32,1,832]{2,1,0:T(1,128)}), f32[32,1,832]{2,1,0:T(1,128)S(1)}, u32[]{:S(2)}, u32[]{:S(2)}) %all-to-all-start.2) | async-done | bytes 106528 | tf_op jit(solution)/shard_map/all_to_all | solution.py:131
  (97 shorter events, 32.0 us)
Async XLA Ops:
  7.2 5.8 %copy-start = (f32[64,2048]{1,0:T(8,128)S(1)}, f32[64,2048]{1,0:T(8,128)}, u32[]{:S(2)}) copy-start(f32[64,2048]{1,0:T(8,128)} %param.6) | copy-start | bytes 1572868
  7.2 33.6 %all-gather.2.cloned.1.call-start = ((), (), s32[]{:S(2)}) async-start(), calls=%async_computation.3 | async-start | bytes 2621440 | tf_op jit(solution)/shard_map/all_gather | solution.py:95
  15.9 7.4 %copy-start.11 = (s32[10]{0:T(128)S(1)}, s32[10]{0:T(128)}, u32[]{:S(2)}) copy-start(s32[10]{0:T(128)} %param.10) | copy-start | bytes 124
  15.9 24.7 %copy-start.12 = (s32[10]{0:T(128)S(1)}, s32[10]{0:T(128)}, u32[]{:S(2)}) copy-start(s32[10]{0:T(128)} %param.9) | copy-start | bytes 124
  15.9 55.8 %all-to-all-start = ((f32[8,128,512]{2,1,0:T(8,128)}), f32[8,128,512]{2,1,0:T(8,128)}, u32[]{:S(2)}, u32[]{:S(2)}) async-start(f32[8,128,512]{2,1,0:T(8,128)} %bitcast.6), calls=%async_computation | async-start | bytes 4194304 | tf_op jit(solution)/shard_map/all_to_all | solution.py:75
  43.6 3.8 %copy-start.1 = (f32[64,4,512]{2,1,0:T(4,128)}, f32[64,4,512]{2,1,0:T(4,128)S(1)}, u32[]{:S(2)}) copy-start(f32[64,4,512]{2,1,0:T(4,128)S(1)} %reshape.138) | copy-start | bytes 1572868
  43.9 3.5 %copy-start.3 = (f32[64,4,512]{2,1,0:T(4,128)}, f32[64,4,512]{2,1,0:T(4,128)S(1)}, u32[]{:S(2)}) copy-start(f32[64,4,512]{2,1,0:T(4,128)S(1)} %reshape.141) | copy-start | bytes 1572868
  44.3 28.9 %copy-start.5 = (f32[64,4,512]{2,1,0:T(4,128)}, f32[64,4,512]{2,1,0:T(4,128)S(1)}, u32[]{:S(2)}) copy-start(f32[64,4,512]{2,1,0:T(4,128)S(1)} %reshape.140) | copy-start | bytes 1572868
  45.9 33.5 %copy-start.7 = (f32[64,4,512]{2,1,0:T(4,128)}, f32[64,4,512]{2,1,0:T(4,128)S(1)}, u32[]{:S(2)}) copy-start(f32[64,4,512]{2,1,0:T(4,128)S(1)} %reshape.139) | copy-start | bytes 1572868
  87.9 3.3 %copy-start.10 = (f32[4,64]{1,0:T(4,128)S(1)}, f32[4,64]{1,0:T(4,128)}, u32[]{:S(2)}) copy-start(f32[4,64]{1,0:T(4,128)} %multiply_reduce_fusion.3) | copy-start | bytes 3076
  95.5 0.7 copy-start.9
  98.1 55.1 %all-to-all-start.1 = ((f32[8,136,512]{2,1,0:T(8,128)}), f32[8,136,512]{2,1,0:T(8,128)}, u32[]{:S(2)}, u32[]{:S(2)}) async-start(f32[8,136,512]{2,1,0:T(8,128)} %pad_maximum_fusion), calls=%async_computation.1 | async-start | bytes 4456448 | tf_op jit(solution)/shard_map/all_to_all | solution.py:75
  172.2 1.0 copy-start.2
  172.2 1.2 copy-start.4
  172.2 1.3 copy-start.6
  172.2 1.5 copy-start.8
  175.5 11.6 %all-to-all-start.2 = ((f32[32,1,832]{2,1,0:T(1,128)}), f32[32,1,832]{2,1,0:T(1,128)S(1)}, u32[]{:S(2)}, u32[]{:S(2)}) async-start(f32[32,1,832]{2,1,0:T(1,128)} %reshape.154), calls=%async_computation.2 | async-start | bytes 229376 | tf_op jit(solution)/shard_map/all_to_all | solution.py:131
Sparse Core Ops, SparseCore 0:
  9.5 25.2 all-gather.1

commit v6 on v5

--- a/solution.py
+++ b/solution.py
@@ -73,18 +73,16 @@
             side = jnp.broadcast_to(flat.reshape(1, PAD_ROWS, tile_size), (peers, PAD_ROWS, tile_size))
             pieces = jnp.concatenate([pieces, side], axis=1)
         arrived = lax.all_to_all(pieces, "ind", split_axis=0, concat_axis=0, tiled=True)
-        sums = None
-        if extra is not None:
-            sums = jnp.sum(arrived[:, NEED * width:].reshape(peers, -1)[:, :extra.size], axis=0)
-            sums = sums.reshape(extra.shape)
-        return arrived, sums
+        if extra is None:
+            return arrived.reshape(peers * NEED, width, tile_size), None
+        tiles_in = arrived[:, :NEED * width].reshape(peers * NEED, width, tile_size)
+        sums = jnp.sum(arrived[:, NEED * width:].reshape(peers, -1)[:, :extra.size], axis=0)
+        return tiles_in, sums.reshape(extra.shape)
 
     def kprod(x, arrived):
         width = x.shape[1]
-        picked = jnp.stack([
-            lax.dynamic_slice(arrived, (position[s] // NEED, position[s] % NEED * width, 0),
-                              (1, width, tile_size))[0]
-            for s in range(off_count)])
+        picked = jnp.stack([lax.dynamic_index_in_dim(arrived, position[s], 0, keepdims=False)
+                            for s in range(off_count)])
         prod = batched_tile_dot(jnp.concatenate([x, picked], axis=0), grm_tiles)
         far = prod[row_tiles:]
         return prod[:row_tiles] + jnp.sum(weight[:, :, None, None] * far[:, None], axis=0)

time: 199 us -> 189 us (0.950)
  local copies, waits for them, and re-layouts: 38.3 us -> 28.6 us
  waiting for transfers between devices: 83.3 us -> 88.8 us
  between operations: 30.7 us -> 26.5 us
    all_to_all x2, waiting for transfers between devices: 74.7 us -> 80.1 us  [exchange(): lax.all_to_all(pieces, 'ind', split_axis=0, concat_axis=0, tiled=True)]
    unnamed x40 -> x42, local copies, waits for them, and re-layouts: 18.9 us -> 13.6 us
where the time goes in v6:
time: 189 us; the launch traced here: 188 us
  waiting for transfers between devices  88.8 us (47%)
  local copies, waits for them, and re-layouts  28.6 us (15%)
  between operations  26.5 us (14%)
  other arithmetic  20.7 us (11%)
  starting transfers between devices  14.9 us (8%)
  matrix products  8.67 us (5%)
    all_to_all x2, waiting for transfers between devices, exchange(): lax.all_to_all(pieces, 'ind', split_axis=0, concat_axis=0, tiled=True)  80.1 us
    unnamed x42, local copies, waits for them, and re-layouts  13.6 us
    all_to_all x2, starting transfers between devices, exchange(): lax.all_to_all(pieces, 'ind', split_axis=0, concat_axis=0, tiled=True)  11.2 us
    dot_general x2, matrix products, batched_tile_dot(): lax.dot_general(parts, tiles, (((2,), (2,)), ((0,), (0,))), preferred_ele...  8.67 us
    all_to_all x1, waiting for transfers between devices, chunk(): lax.all_to_all(spread, ('ind', 'var'), split_axis=0, concat_axis=0, tiled...  7.98 us
  transfers between devices with their start and end apart: 4, of which 3 were waited for; matrix products, arithmetic and copies ran while one was open for 8% of the time, Pallas kernels for 0%

profile of v6, /device:TPU:0, one launch (start us, length us, event | category | flops | bytes accessed | tf_op | source)
XLA Modules:
  0.0 188.1 jit_solution(1689769584492082245)
XLA Ops:
  8.0 1.4 fusion.38
  9.4 2.4 %select_reduce_fusion = f32[4,512]{1,0:T(4,128)S(1)} fusion(bf16[10,512,512]{2,1,0:T(8,128)(2,1)} %param.8, pred[512,512]{1,0:T(8,128)(4,1)S(1)} %iota_compare_fusion), kind=kLoop, calls=%fused_computation | loop fusion | flops 3143680 | bytes 2367488 | tf_op jit(solution)/shard_map/reduce_sum | solution.py:47
  14.4 1.6 tile.21
  16.1 7.4 %all-to-all-start = ((f32[8,128,512]{2,1,0:T(8,128)}), f32[8,128,512]{2,1,0:T(8,128)}, u32[]{:S(2)}, u32[]{:S(2)}) async-start(f32[8,128,512]{2,1,0:T(8,128)} %bitcast.6), calls=%async_computation | async-start | bytes 4194304 | tf_op jit(solution)/shard_map/all_to_all | solution.py:75
  36.7 2.5 %constant_dynamic-slice_fusion.6 = (f32[64,2048]{1,0:T(8,128)S(1)}, f32[64,2048]{1,0:T(8,128)S(1)}, f32[64,2048]{1,0:T(8,128)S(1)}, f32[64,2048]{1,0:T(8,128)}) fusion(f32[256,2048]{1,0:T(8,128)} %all-gather.2.cloned.1.call-done, s32[]{:T(128)S(6)} %select_n.88, s32[]{:T(128)S(6)} %select_n.91, s32[]{:T(128)S(6)} %select_n.90, s32[]{:T(128)S(6)} %select_n.89), kind=kLoop, calls=%fused_computation.84 | loop fusion | bytes 4194320 | tf_op jit(solution)/shard_map/dynamic_slice | solution.py:98
  40.3 1.6 reshape.146
  42.8 29.0 %all-to-all-done = f32[8,128,512]{2,1,0:T(8,128)} async-done(((f32[8,128,512]{2,1,0:T(8,128)}), f32[8,128,512]{2,1,0:T(8,128)}, u32[]{:S(2)}, u32[]{:S(2)}) %all-to-all-start) | async-done | bytes 2097184 | tf_op jit(solution)/shard_map/all_to_all | solution.py:75
  71.8 1.6 dynamic-slice_dynamic-update-slice_fusion.11
  73.4 1.6 dynamic-slice_dynamic-update-slice_fusion.10
  75.0 1.6 dynamic-slice_dynamic-update-slice_fusion.9
  76.5 1.6 dynamic-slice_dynamic-update-slice_fusion.8
  78.1 1.6 dynamic-slice_dynamic-update-slice_fusion.7
  79.6 1.6 dynamic-slice_dynamic-update-slice_fusion.6
  81.2 1.7 reduce-precision_convert_fusion.3
  82.9 4.3 %fusion = f32[10,192,512]{2,1,0:T(8,128)S(1)} fusion(bf16[10,512,512]{2,1,0:T(8,128)(2,1)} %param.8, bf16[10,64,512]{2,1,0:T(8,128)(2,1)S(1)} %get-tuple-element.24, bf16[10,64,512]{2,1,0:T(8,128)(2,1)S(1)} %get-tuple-element.25, bf16[10,64,512]{2,1,0:T(8,128)(2,1)S(1)} %get-tuple-element.23), kind=kOutput, calls=%fused_computation.7 | convolution fusion | flops 1012531200 | bytes 11141120 | tf_op jit(solution)/shard_map/dot_general | solution.py:23
  88.1 2.4 %constant_dynamic-update-slice_fusion.1 = (f32[10,64,512]{2,1,0:T(8,128)}, f32[4,64,512]{2,1,0:T(8,128)S(1)}, f32[4,64,512]{2,1,0:T(8,128)S(1)}) fusion(f32[4,512]{1,0:T(4,128)S(1)} %multiply_add_fusion.1, f32[4,64,512]{2,1,0:T(8,128)S(1)} %multiply_reduce_fusion.1, f32[10,64,512]{2,1,0:T(8,128)S(1)} %slice_add_fusion.2, f32[]{:T(128)} %bitcast.2, ...), kind=kLoop, calls=%fused_computation.71 | loop fusion | flops 786431 | bytes 3153928
  91.4 1.7 pad_maximum_fusion
  93.0 3.8 %all-to-all-start.1 = ((f32[8,136,512]{2,1,0:T(8,128)}), f32[8,136,512]{2,1,0:T(8,128)S(1)}, u32[]{:S(2)}, u32[]{:S(2)}) async-start(f32[8,136,512]{2,1,0:T(8,128)} %pad_maximum_fusion), calls=%async_computation.1 | async-start | bytes 4456448 | tf_op jit(solution)/shard_map/all_to_all | solution.py:75
  96.9 51.1 %all-to-all-done.1 = f32[8,136,512]{2,1,0:T(8,128)S(1)} async-done(((f32[8,136,512]{2,1,0:T(8,128)}), f32[8,136,512]{2,1,0:T(8,128)S(1)}, u32[]{:S(2)}, u32[]{:S(2)}) %all-to-all-start.1) | async-done | bytes 2228256 | tf_op jit(solution)/shard_map/all_to_all | solution.py:75
  152.4 1.7 reduce-precision_convert_fusion.1
  154.1 4.3 %fusion.6 = f32[10,192,512]{2,1,0:T(8,128)S(1)} fusion(bf16[10,512,512]{2,1,0:T(8,128)(2,1)} %param.8, bf16[10,64,512]{2,1,0:T(8,128)(2,1)S(1)} %get-tuple-element.21, bf16[10,64,512]{2,1,0:T(8,128)(2,1)S(1)} %get-tuple-element.22, bf16[10,64,512]{2,1,0:T(8,128)(2,1)S(1)} %get-tuple-element.20), kind=kOutput, calls=%fused_computation.13 | convolution fusion | flops 1012531200 | bytes 11141120 | tf_op jit(solution)/shard_map/dot_general | solution.py:23
  160.1 2.8 %fusion.21 = (f32[4,64,512]{2,1,0:T(8,128)S(1)}, f32[4,64,512]{2,1,0:T(8,128)S(1)}) fusion(f32[4,64,512]{2,1,0:T(8,128)S(1)} %multiply_reduce_fusion, f32[10,64,512]{2,1,0:T(8,128)S(1)} %slice_add_fusion, f32[64]{0:T(128)S(1)} %get-tuple-element.36, f32[]{:T(128)} %bitcast.2, f32[]{:T(128)} %bitcast, f32[4,64,512]{2,1,0:T(8,128)S(1)} %copy-done.3, ...), kind=kLoop, calls=%fused_computation.45 | loop fusion | flops 1310720 | bytes 4202760 | tf_op jit(solution)/shard_map/add | solution.py:119
  166.2 3.6 %all-to-all-start.2 = ((f32[32,1,832]{2,1,0:T(1,128)}), f32[32,1,832]{2,1,0:T(1,128)S(1)}, u32[]{:S(2)}, u32[]{:S(2)}) async-start(f32[32,1,832]{2,1,0:T(1,128)} %reshape.162), calls=%async_computation.2 | async-start | bytes 229376 | tf_op jit(solution)/shard_map/all_to_all | solution.py:129
  169.8 8.0 %all-to-all-done.2 = f32[32,1,832]{2,1,0:T(1,128)S(1)} async-done(((f32[32,1,832]{2,1,0:T(1,128)}), f32[32,1,832]{2,1,0:T(1,128)S(1)}, u32[]{:S(2)}, u32[]{:S(2)}) %all-to-all-start.2) | async-done | bytes 106528 | tf_op jit(solution)/shard_map/all_to_all | solution.py:129
  (100 shorter events, 20.9 us)
Async XLA Ops:
  7.2 6.0 %copy-start = (f32[64,2048]{1,0:T(8,128)S(1)}, f32[64,2048]{1,0:T(8,128)}, u32[]{:S(2)}) copy-start(f32[64,2048]{1,0:T(8,128)} %param.6) | copy-start | bytes 1572868
  7.2 29.6 %all-gather.2.cloned.1.call-start = ((), (), s32[]{:S(2)}) async-start(), calls=%async_computation.3 | async-start | bytes 2621440 | tf_op jit(solution)/shard_map/all_gather | solution.py:93
  16.1 7.4 %copy-start.12 = (s32[10]{0:T(128)S(1)}, s32[10]{0:T(128)}, u32[]{:S(2)}) copy-start(s32[10]{0:T(128)} %param.10) | copy-start | bytes 124
  16.1 16.7 %copy-start.13 = (s32[10]{0:T(128)S(1)}, s32[10]{0:T(128)}, u32[]{:S(2)}) copy-start(s32[10]{0:T(128)} %param.9) | copy-start | bytes 124
  16.1 55.8 %all-to-all-start = ((f32[8,128,512]{2,1,0:T(8,128)}), f32[8,128,512]{2,1,0:T(8,128)}, u32[]{:S(2)}, u32[]{:S(2)}) async-start(f32[8,128,512]{2,1,0:T(8,128)} %bitcast.6), calls=%async_computation | async-start | bytes 4194304 | tf_op jit(solution)/shard_map/all_to_all | solution.py:75
  39.6 3.2 %copy-start.4 = (f32[64,4,512]{2,1,0:T(4,128)}, f32[64,4,512]{2,1,0:T(4,128)S(1)}, u32[]{:S(2)}) copy-start(f32[64,4,512]{2,1,0:T(4,128)S(1)} %reshape.145) | copy-start | bytes 1572868
  39.9 2.9 %copy-start.6 = (f32[64,4,512]{2,1,0:T(4,128)}, f32[64,4,512]{2,1,0:T(4,128)S(1)}, u32[]{:S(2)}) copy-start(f32[64,4,512]{2,1,0:T(4,128)S(1)} %reshape.148) | copy-start | bytes 1572868
  40.3 34.7 %copy-start.8 = (f32[64,4,512]{2,1,0:T(4,128)}, f32[64,4,512]{2,1,0:T(4,128)S(1)}, u32[]{:S(2)}) copy-start(f32[64,4,512]{2,1,0:T(4,128)S(1)} %reshape.147) | copy-start | bytes 1572868
  41.9 39.3 %copy-start.10 = (f32[64,4,512]{2,1,0:T(4,128)}, f32[64,4,512]{2,1,0:T(4,128)S(1)}, u32[]{:S(2)}) copy-start(f32[64,4,512]{2,1,0:T(4,128)S(1)} %reshape.146) | copy-start | bytes 1572868
  87.7 2.8 %copy-start.1 = (f32[10,64,512]{2,1,0:T(8,128)}, f32[10,64,512]{2,1,0:T(8,128)S(1)}, u32[]{:S(2)}) copy-start(f32[10,64,512]{2,1,0:T(8,128)S(1)} %slice_add_fusion.2) | copy-start | bytes 3932164
  88.1 2.5 %copy-start.2 = (f32[4,64,512]{2,1,0:T(8,128)}, f32[4,64,512]{2,1,0:T(8,128)S(1)}, u32[]{:S(2)}) copy-start(f32[4,64,512]{2,1,0:T(8,128)S(1)} %multiply_reduce_fusion.1) | copy-start | bytes 1572868
  93.0 54.9 %all-to-all-start.1 = ((f32[8,136,512]{2,1,0:T(8,128)}), f32[8,136,512]{2,1,0:T(8,128)S(1)}, u32[]{:S(2)}, u32[]{:S(2)}) async-start(f32[8,136,512]{2,1,0:T(8,128)} %pad_maximum_fusion), calls=%async_computation.1 | async-start | bytes 4456448 | tf_op jit(solution)/shard_map/all_to_all | solution.py:75
  159.1 1.0 copy-start.3
  162.9 1.0 copy-start.5
  162.9 1.2 copy-start.7
  162.9 1.3 copy-start.9
  162.9 1.5 copy-start.11
  166.2 11.6 %all-to-all-start.2 = ((f32[32,1,832]{2,1,0:T(1,128)}), f32[32,1,832]{2,1,0:T(1,128)S(1)}, u32[]{:S(2)}, u32[]{:S(2)}) async-start(f32[32,1,832]{2,1,0:T(1,128)} %reshape.162), calls=%async_computation.2 | async-start | bytes 229376 | tf_op jit(solution)/shard_map/all_to_all | solution.py:129
Sparse Core Ops, SparseCore 0:
  9.5 25.2 all-gather.1

commit v7 on v6

--- a/solution.py
+++ b/solution.py
@@ -101,16 +101,16 @@
 
     def chunk(g, geno_sub):
         z0 = g / precond
-        tiles0, _ = exchange(z0, None)
+        tiles0, sums0 = exchange(z0, colsum(g * z0)[None])
+        rz0 = sums0[0]
         kz0 = kprod(z0, tiles0)
         image0 = tau0 * z0 + tau1 * kz0
         w = image0 / precond
         p0_local = jnp.sum(geno_sub * z0[None], axis=(1, 3))
-        extra1 = jnp.concatenate([colsum(g * z0)[None], colsum(z0 * image0)[None], p0_local], axis=0)
+        extra1 = jnp.concatenate([colsum(z0 * image0)[None], p0_local], axis=0)
         tiles1, sums1 = exchange(w, extra1)
-        rz0 = sums1[0]
-        dad0 = sums1[1]
-        p0 = sums1[2:]
+        dad0 = sums1[0]
+        p0 = sums1[1:]
         alpha0 = rz0 / dad0
         resid1 = g - alpha0[None, :, None] * image0
         z1 = resid1 / precond

time: 189 us -> 184 us (0.974)
  waiting for transfers between devices: 88.8 us -> 83.6 us
  local copies, waits for them, and re-layouts: 28.6 us -> 24.9 us
  other arithmetic: 20.7 us -> 23.1 us
    all_to_all x2, waiting for transfers between devices: 80.1 us -> 63.5 us  [exchange(): lax.all_to_all(pieces, 'ind', split_axis=0, concat_axis=0, tiled=True)]
    all_gather x1, waiting for transfers between devices: 0.01 us -> 11.5 us  [local(): geno_all = lax.all_gather(genotypes, 'var', axis=0, tiled=True)]
    unnamed x42 -> x48, local copies, waits for them, and re-layouts: 13.6 us -> 5.86 us
    reshape x4, local copies, waits for them, and re-layouts: 2.63 us -> 6.53 us  [to_tiles(): return jnp.transpose(x.reshape(cols_here, row_tiles, tile_size), (1, 0, 2))]
    convert_element_type x2, other arithmetic: 3.37 us -> 0.75 us  [split3(): hi.astype(jnp.bfloat16)]
    concatenate x2, local copies, waits for them, and re-layouts: 2.22 us -> 0.04 us  [kprod(): prod = batched_tile_dot(jnp.concatenate([x, picked], axis=0), grm_tiles)]
    another operation x5, other arithmetic: 1.22 us -> 3.35 us  [exchange(): rolled = jnp.stack([jnp.roll(x, -t, axis=0) for t in range(NEED)], axis=1)]
  transfers between devices with their start and end apart: 4 -> 4, of which waited for: 3 -> 4; matrix products, arithmetic and copies ran while one was open for 8% -> 7% of each run, Pallas kernels for 0% -> 0%
where the time goes in v7:
time: 184 us; the launch traced here: 183 us
  waiting for transfers between devices  83.6 us (45%)
  between operations  26.8 us (15%)
  local copies, waits for them, and re-layouts  24.9 us (14%)
  other arithmetic  23.1 us (13%)
  starting transfers between devices  15.6 us (8%)
  matrix products  8.66 us (5%)
    all_to_all x2, waiting for transfers between devices, exchange(): lax.all_to_all(pieces, 'ind', split_axis=0, concat_axis=0, tiled=True)  63.5 us
    all_to_all x2, starting transfers between devices, exchange(): lax.all_to_all(pieces, 'ind', split_axis=0, concat_axis=0, tiled=True)  11.9 us
    all_gather x1, waiting for transfers between devices, local(): geno_all = lax.all_gather(genotypes, 'var', axis=0, tiled=True)  11.5 us
    dot_general x2, matrix products, batched_tile_dot(): lax.dot_general(parts, tiles, (((2,), (2,)), ((0,), (0,))), preferred_ele...  8.66 us
    all_to_all x1, waiting for transfers between devices, chunk(): lax.all_to_all(spread, ('ind', 'var'), split_axis=0, concat_axis=0, tiled...  7.98 us
    reshape x4, local copies, waits for them, and re-layouts, to_tiles(): return jnp.transpose(x.reshape(cols_here, row_tiles, tile_size), (1, 0, 2))  6.53 us
    unnamed x48, local copies, waits for them, and re-layouts  5.86 us
  transfers between devices with their start and end apart: 4, of which 4 were waited for; matrix products, arithmetic and copies ran while one was open for 7% of the time, Pallas kernels for 0%

profile of v7, /device:TPU:0, one launch (start us, length us, event | category | flops | bytes accessed | tf_op | source)
XLA Modules:
  0.0 182.5 jit_solution(5755092635167568204)
XLA Ops:
  7.3 1.4 fusion.38
  8.7 2.4 %select_reduce_fusion = f32[4,512]{1,0:T(4,128)S(1)} fusion(bf16[10,512,512]{2,1,0:T(8,128)(2,1)} %param.8, pred[512,512]{1,0:T(8,128)(4,1)S(1)} %iota_compare_fusion), kind=kLoop, calls=%fused_computation | loop fusion | flops 3143680 | bytes 2367488 | tf_op jit(solution)/shard_map/reduce_sum | solution.py:47
  11.1 1.3 multiply_add_fusion.1
  14.1 1.6 pad_maximum_fusion
  15.8 7.4 %all-to-all-start = ((f32[8,136,512]{2,1,0:T(8,128)}), f32[8,136,512]{2,1,0:T(8,128)S(1)}, u32[]{:S(2)}, u32[]{:S(2)}) async-start(f32[8,136,512]{2,1,0:T(8,128)} %pad_maximum_fusion), calls=%async_computation | async-start | bytes 4456448 | tf_op jit(solution)/shard_map/all_to_all | solution.py:75
  32.3 1.1 copy.41
  38.1 11.5 %all-gather.2.cloned.1.call-done = f32[256,2048]{1,0:T(8,128)} async-done(((f32[64,2048]{1,0:T(8,128)}), f32[256,2048]{1,0:T(8,128)}) %all-gather.2.cloned.1.call-update) | async-done | bytes 2097168 | tf_op jit(solution)/shard_map/all_gather | solution.py:93
  49.6 2.7 %constant_dynamic-slice_fusion.6 = (f32[64,2048]{1,0:T(8,128)S(1)}, f32[64,2048]{1,0:T(8,128)}, f32[64,2048]{1,0:T(8,128)}, f32[64,2048]{1,0:T(8,128)}) fusion(f32[256,2048]{1,0:T(8,128)} %all-gather.2.cloned.1.call-done, s32[]{:T(128)S(6)} %select_n.88, s32[]{:T(128)S(6)} %select_n.91, s32[]{:T(128)S(6)} %select_n.90, s32[]{:T(128)S(6)} %select_n.89), kind=kLoop, calls=%fused_computation.86 | loop fusion | bytes 4194320 | tf_op jit(solution)/shard_map/dynamic_slice | solution.py:98
  52.6 1.6 reshape.161
  54.2 2.4 %reshape.160 = f32[64,4,512]{2,1,0:T(4,128)} reshape(f32[64,2048]{1,0:T(8,128)} %get-tuple-element.16) | data formatting | bytes 1048576 | tf_op jit(solution)/shard_map/reshape | solution.py:60
  56.6 2.2 %reshape.159 = f32[64,4,512]{2,1,0:T(4,128)} reshape(f32[64,2048]{1,0:T(8,128)} %get-tuple-element.17) | data formatting | bytes 1048576 | tf_op jit(solution)/shard_map/reshape | solution.py:60
  58.8 2.2 %multiply_reduce_fusion.3 = f32[4,64]{1,0:T(4,128)S(1)} fusion(f32[4,64,512]{2,0,1:T(4,128)} %copy.41, f32[1,4,64,512]{3,1,2,0:T(4,128)S(1)} %bitcast.150, f32[1,4,64,512]{3,1,2,0:T(4,128)} %bitcast.152, f32[1,4,64,512]{3,1,2,0:T(4,128)} %bitcast.154, f32[1,4,64,512]{3,1,2,0:T(4,128)S(1)} %bitcast.148), kind=kLoop, calls=%fused_computation.7 | loop fusion | flops 2621184 | bytes 2622464 | tf_op jit(solution)/shard_map/reduce_sum | solution.py:109
  61.1 13.1 %all-to-all-done = f32[8,136,512]{2,1,0:T(8,128)S(1)} async-done(((f32[8,136,512]{2,1,0:T(8,128)}), f32[8,136,512]{2,1,0:T(8,128)S(1)}, u32[]{:S(2)}, u32[]{:S(2)}) %all-to-all-start) | async-done | bytes 2228256 | tf_op jit(solution)/shard_map/all_to_all | solution.py:75
  76.1 4.3 %fusion = f32[10,192,512]{2,1,0:T(8,128)S(1)} fusion(bf16[10,512,512]{2,1,0:T(8,128)(2,1)} %param.8, bf16[10,64,512]{2,1,0:T(8,128)(2,1)S(1)} %get-tuple-element.22, bf16[10,64,512]{2,1,0:T(8,128)(2,1)S(1)} %get-tuple-element.23, bf16[10,64,512]{2,1,0:T(8,128)(2,1)S(1)} %get-tuple-element.21), kind=kOutput, calls=%fused_computation.8 | convolution fusion | flops 1012531200 | bytes 11141120 | tf_op jit(solution)/shard_map/dot_general | solution.py:23
  82.3 2.4 %constant_dynamic-update-slice_fusion.1 = (f32[10,64,512]{2,1,0:T(8,128)}, f32[4,64,512]{2,1,0:T(8,128)S(1)}, f32[4,64,512]{2,1,0:T(8,128)S(1)}) fusion(f32[4,512]{1,0:T(4,128)S(1)} %multiply_add_fusion.1, f32[4,64,512]{2,1,0:T(8,128)S(1)} %multiply_reduce_fusion.1, f32[10,64,512]{2,1,0:T(8,128)S(1)} %slice_add_fusion.2, f32[]{:T(128)} %bitcast.2, ...), kind=kLoop, calls=%fused_computation.73 | loop fusion | flops 786431 | bytes 3153928
  86.9 1.1 pad_maximum_fusion.4
  88.4 1.6 pad_maximum_fusion.1
  90.0 4.5 %all-to-all-start.1 = ((f32[8,136,512]{2,1,0:T(8,128)}), f32[8,136,512]{2,1,0:T(8,128)}, u32[]{:S(2)}, u32[]{:S(2)}) async-start(f32[8,136,512]{2,1,0:T(8,128)} %pad_maximum_fusion.1), calls=%async_computation.1 | async-start | bytes 4456448 | tf_op jit(solution)/shard_map/all_to_all | solution.py:75
  94.7 50.4 %all-to-all-done.1 = f32[8,136,512]{2,1,0:T(8,128)} async-done(((f32[8,136,512]{2,1,0:T(8,128)}), f32[8,136,512]{2,1,0:T(8,128)}, u32[]{:S(2)}, u32[]{:S(2)}) %all-to-all-start.1) | async-done | bytes 2228256 | tf_op jit(solution)/shard_map/all_to_all | solution.py:75
  145.1 1.8 slice.192
  148.6 4.3 %fusion.6 = f32[10,192,512]{2,1,0:T(8,128)S(1)} fusion(bf16[10,512,512]{2,1,0:T(8,128)(2,1)} %param.8, bf16[10,64,512]{2,1,0:T(8,128)(2,1)S(1)} %get-tuple-element.19, bf16[10,64,512]{2,1,0:T(8,128)(2,1)S(1)} %get-tuple-element.20, bf16[10,64,512]{2,1,0:T(8,128)(2,1)S(1)} %get-tuple-element.18), kind=kOutput, calls=%fused_computation.14 | convolution fusion | flops 1012531200 | bytes 11141120 | tf_op jit(solution)/shard_map/dot_general | solution.py:23
  154.6 2.8 %fusion.21 = (f32[4,64,512]{2,1,0:T(8,128)S(1)}, f32[4,64,512]{2,1,0:T(8,128)S(1)}) fusion(f32[4,64,512]{2,1,0:T(8,128)S(1)} %multiply_reduce_fusion, f32[10,64,512]{2,1,0:T(8,128)S(1)} %slice_add_fusion, f32[64]{0:T(128)S(1)} %get-tuple-element.35, f32[]{:T(128)} %bitcast.2, f32[]{:T(128)} %bitcast.1, f32[4,64,512]{2,1,0:T(8,128)S(1)} %copy-done.4, ...), kind=kLoop, calls=%fused_computation.46 | loop fusion | flops 1310720 | bytes 4202760 | tf_op jit(solution)/shard_map/add | solution.py:119
  160.6 3.6 %all-to-all-start.2 = ((f32[32,1,832]{2,1,0:T(1,128)}), f32[32,1,832]{2,1,0:T(1,128)S(1)}, u32[]{:S(2)}, u32[]{:S(2)}) async-start(f32[32,1,832]{2,1,0:T(1,128)} %reshape.175), calls=%async_computation.2 | async-start | bytes 229376 | tf_op jit(solution)/shard_map/all_to_all | solution.py:129
  164.2 8.0 %all-to-all-done.2 = f32[32,1,832]{2,1,0:T(1,128)S(1)} async-done(((f32[32,1,832]{2,1,0:T(1,128)}), f32[32,1,832]{2,1,0:T(1,128)S(1)}, u32[]{:S(2)}, u32[]{:S(2)}) %all-to-all-start.2) | async-done | bytes 106528 | tf_op jit(solution)/shard_map/all_to_all | solution.py:129
  (112 shorter events, 19.9 us)
Async XLA Ops:
  7.2 5.3 %copy-start = (f32[64,2048]{1,0:T(8,128)S(1)}, f32[64,2048]{1,0:T(8,128)}, u32[]{:S(2)}) copy-start(f32[64,2048]{1,0:T(8,128)} %param.6) | copy-start | bytes 1572868
  15.7 8.2 %copy-start.14 = (s32[10]{0:T(128)S(1)}, s32[10]{0:T(128)}, u32[]{:S(2)}) copy-start(s32[10]{0:T(128)} %param.10) | copy-start | bytes 124
  15.8 18.4 %copy-start.15 = (s32[10]{0:T(128)S(1)}, s32[10]{0:T(128)}, u32[]{:S(2)}) copy-start(s32[10]{0:T(128)} %param.9) | copy-start | bytes 124
  15.8 58.5 %all-to-all-start = ((f32[8,136,512]{2,1,0:T(8,128)}), f32[8,136,512]{2,1,0:T(8,128)S(1)}, u32[]{:S(2)}, u32[]{:S(2)}) async-start(f32[8,136,512]{2,1,0:T(8,128)} %pad_maximum_fusion), calls=%async_computation | async-start | bytes 4456448 | tf_op jit(solution)/shard_map/all_to_all | solution.py:75
  23.2 26.4 %all-gather.2.cloned.1.call-start = ((), (), s32[]{:S(2)}) async-start(), calls=%async_computation.3 | async-start | bytes 2621440 | tf_op jit(solution)/shard_map/all_gather | solution.py:93
  52.6 8.5 %copy-start.5 = (f32[64,4,512]{2,1,0:T(4,128)}, f32[64,4,512]{2,1,0:T(4,128)S(1)}, u32[]{:S(2)}) copy-start(f32[64,4,512]{2,1,0:T(4,128)S(1)} %reshape.158) | copy-start | bytes 1572868
  54.2 6.9 %copy-start.7 = (f32[64,4,512]{2,1,0:T(4,128)}, f32[64,4,512]{2,1,0:T(4,128)S(1)}, u32[]{:S(2)}) copy-start(f32[64,4,512]{2,1,0:T(4,128)S(1)} %reshape.161) | copy-start | bytes 1572868
  74.2 1.3 copy-start.12
  80.9 3.8 %copy-start.2 = (f32[10,64,512]{2,1,0:T(8,128)}, f32[10,64,512]{2,1,0:T(8,128)S(1)}, u32[]{:S(2)}) copy-start(f32[10,64,512]{2,1,0:T(8,128)S(1)} %slice_add_fusion.2) | copy-start | bytes 3932164
  80.9 1.4 copy-start.1
  82.3 3.2 %copy-start.3 = (f32[4,64,512]{2,1,0:T(8,128)}, f32[4,64,512]{2,1,0:T(8,128)S(1)}, u32[]{:S(2)}) copy-start(f32[4,64,512]{2,1,0:T(8,128)S(1)} %multiply_reduce_fusion.1) | copy-start | bytes 1572868
  84.6 0.9 copy-start.11
  90.0 55.1 %all-to-all-start.1 = ((f32[8,136,512]{2,1,0:T(8,128)}), f32[8,136,512]{2,1,0:T(8,128)}, u32[]{:S(2)}, u32[]{:S(2)}) async-start(f32[8,136,512]{2,1,0:T(8,128)} %pad_maximum_fusion.1), calls=%async_computation.1 | async-start | bytes 4456448 | tf_op jit(solution)/shard_map/all_to_all | solution.py:75
  94.7 52.2 %copy-start.13 = (f32[10,64,512]{2,1,0:T(8,128)S(1)}, f32[10,64,512]{2,1,0:T(8,128)}, u32[]{:S(2)}) copy-start(f32[10,64,512]{2,1,0:T(8,128)} %get-tuple-element.11) | copy-start | bytes 3932164
  153.5 1.0 copy-start.4
  157.3 1.0 copy-start.6
  157.3 1.2 copy-start.8
  157.4 1.3 copy-start.9
  157.4 1.5 copy-start.10
  160.6 11.6 %all-to-all-start.2 = ((f32[32,1,832]{2,1,0:T(1,128)}), f32[32,1,832]{2,1,0:T(1,128)S(1)}, u32[]{:S(2)}, u32[]{:S(2)}) async-start(f32[32,1,832]{2,1,0:T(1,128)} %reshape.175), calls=%async_computation.2 | async-start | bytes 229376 | tf_op jit(solution)/shard_map/all_to_all | solution.py:129
Sparse Core Ops, SparseCore 0:
  25.5 23.9 all-gather.1

commit v8 on v7

--- a/solution.py
+++ b/solution.py
@@ -9,21 +9,19 @@
 CHUNKS = 1
 
 
-def split3(x):
+def split2(x):
     hi = lax.reduce_precision(x, exponent_bits=8, mantissa_bits=7)
-    rest = x - hi
-    mid = lax.reduce_precision(rest, exponent_bits=8, mantissa_bits=7)
-    lo = rest - mid
-    return hi.astype(jnp.bfloat16), mid.astype(jnp.bfloat16), lo.astype(jnp.bfloat16)
+    lo = x - hi
+    return hi.astype(jnp.bfloat16), lo.astype(jnp.bfloat16)
 
 
 def batched_tile_dot(lhs, tiles):
     cols = lhs.shape[1]
-    parts = jnp.concatenate(split3(lhs), axis=1)
+    parts = jnp.concatenate(split2(lhs), axis=1)
     prod = lax.dot_general(
         parts, tiles, (((2,), (2,)), ((0,), (0,))), preferred_element_type=jnp.float32
     )
-    return (prod[:, :cols] + prod[:, cols:2 * cols]) + prod[:, 2 * cols:]
+    return prod[:, :cols] + prod[:, cols:]
 
 
 def local(genotypes, variance_comp, grm_tiles, tile_rows, tile_cols, tile_live):
@@ -83,9 +81,9 @@
         width = x.shape[1]
         picked = jnp.stack([lax.dynamic_index_in_dim(arrived, position[s], 0, keepdims=False)
                             for s in range(off_count)])
-        prod = batched_tile_dot(jnp.concatenate([x, picked], axis=0), grm_tiles)
-        far = prod[row_tiles:]
-        return prod[:row_tiles] + jnp.sum(weight[:, :, None, None] * far[:, None], axis=0)
+        near = batched_tile_dot(x, grm_tiles[:row_tiles])
+        far = batched_tile_dot(picked, grm_tiles[row_tiles:])
+        return near + jnp.sum(weight[:, :, None, None] * far[:, None], axis=0)
 
     def colsum(x):
         return jnp.sum(x, axis=(0, 2))

time: 184 us -> 178 us (0.967)
  waiting for transfers between devices: 83.6 us -> 75.9 us
  matrix products: 8.66 us -> 13 us
  other arithmetic: 23.1 us -> 21 us
    all_to_all x2, waiting for transfers between devices: 63.5 us -> 58.9 us  [exchange(): lax.all_to_all(pieces, 'ind', split_axis=0, concat_axis=0, tiled=True)]
    dot_general x2 -> x4, matrix products: 8.66 us -> 13 us  [batched_tile_dot(): lax.dot_general(parts, tiles, (((2,), (2,)), ((0,), (0,))), preferred_ele...]
    convert_element_type x2 -> x5, other arithmetic: 0.75 us -> 3.86 us  [split2(): return (hi.astype(jnp.bfloat16), lo.astype(jnp.bfloat16))]
    all_gather x1, waiting for transfers between devices: 11.5 us -> 8.36 us  [local(): geno_all = lax.all_gather(genotypes, 'var', axis=0, tiled=True)]
    unnamed x2 -> x1, other arithmetic: 2.54 us -> 0.19 us
  transfers between devices with their start and end apart: 4 -> 4, of which waited for: 4 -> 4; matrix products, arithmetic and copies ran while one was open for 7% -> 12% of each run, Pallas kernels for 0% -> 0%
where the time goes in v8:
time: 178 us; the launch traced here: 177 us
  waiting for transfers between devices  75.9 us (43%)
  between operations  26.5 us (15%)
  local copies, waits for them, and re-layouts  24.8 us (14%)
  other arithmetic  21 us (12%)
  starting transfers between devices  15.6 us (9%)
  matrix products  13 us (7%)
    all_to_all x2, waiting for transfers between devices, exchange(): lax.all_to_all(pieces, 'ind', split_axis=0, concat_axis=0, tiled=True)  58.9 us
    dot_general x4, matrix products, batched_tile_dot(): lax.dot_general(parts, tiles, (((2,), (2,)), ((0,), (0,))), preferred_ele...  13 us
    all_to_all x2, starting transfers between devices, exchange(): lax.all_to_all(pieces, 'ind', split_axis=0, concat_axis=0, tiled=True)  11.9 us
    all_gather x1, waiting for transfers between devices, local(): geno_all = lax.all_gather(genotypes, 'var', axis=0, tiled=True)  8.36 us
    all_to_all x1, waiting for transfers between devices, chunk(): lax.all_to_all(spread, ('ind', 'var'), split_axis=0, concat_axis=0, tiled...  7.98 us
    reshape x4, local copies, waits for them, and re-layouts, to_tiles(): return jnp.transpose(x.reshape(cols_here, row_tiles, tile_size), (1, 0, 2))  6.53 us
    unnamed x48, local copies, waits for them, and re-layouts  5.92 us
    convert_element_type x5, other arithmetic, split2(): return (hi.astype(jnp.bfloat16), lo.astype(jnp.bfloat16))  3.86 us
  transfers between devices with their start and end apart: 4, of which 4 were waited for; matrix products, arithmetic and copies ran while one was open for 12% of the time, Pallas kernels for 0%

profile of v8, /device:TPU:0, one launch (start us, length us, event | category | flops | bytes accessed | tf_op | source)
XLA Modules:
  0.0 176.6 jit_solution(9726477578502542814)
XLA Ops:
  7.3 1.4 fusion.52
  8.6 2.4 %select_reduce_fusion = f32[4,512]{1,0:T(4,128)S(1)} fusion(pred[512,512]{1,0:T(8,128)(4,1)S(1)} %iota_compare_fusion, bf16[10,512,512]{2,1,0:T(8,128)(2,1)} %param.8), kind=kLoop, calls=%fused_computation | loop fusion | flops 3143680 | bytes 2367488 | tf_op jit(solution)/shard_map/reduce_sum | solution.py:45
  11.0 1.3 multiply_add_fusion.1
  13.2 1.6 pad_maximum_fusion
  14.8 7.4 %all-to-all-start = ((f32[8,136,512]{2,1,0:T(8,128)}), f32[8,136,512]{2,1,0:T(8,128)S(1)}, u32[]{:S(2)}, u32[]{:S(2)}) async-start(f32[8,136,512]{2,1,0:T(8,128)} %pad_maximum_fusion), calls=%async_computation | async-start | bytes 4456448 | tf_op jit(solution)/shard_map/all_to_all | solution.py:73
  36.9 3.4 %fusion.6 = f32[4,128,512]{2,1,0:T(8,128)} fusion(bf16[10,512,512]{2,1,0:T(8,128)(2,1)} %param.8, bf16[4,64,512]{2,1,0:T(8,128)(2,1)S(1)} %get-tuple-element.25, bf16[4,64,512]{2,1,0:T(8,128)(2,1)S(1)} %get-tuple-element.22), kind=kOutput, calls=%fused_computation.14 | convolution fusion | flops 269484032 | bytes 3670016 | tf_op jit(solution)/shard_map/dot_general | solution.py:21
  40.3 8.4 %all-gather.2.cloned.1.call-done = f32[256,2048]{1,0:T(8,128)} async-done(((f32[64,2048]{1,0:T(8,128)}), f32[256,2048]{1,0:T(8,128)}) %all-gather.2.cloned.1.call-update) | async-done | bytes 2097168 | tf_op jit(solution)/shard_map/all_gather | solution.py:91
  48.6 2.7 %constant_dynamic-slice_fusion.6 = (f32[64,2048]{1,0:T(8,128)S(1)}, f32[64,2048]{1,0:T(8,128)}, f32[64,2048]{1,0:T(8,128)}, f32[64,2048]{1,0:T(8,128)}) fusion(f32[256,2048]{1,0:T(8,128)} %all-gather.2.cloned.1.call-done, s32[]{:T(128)S(6)} %select_n.88, s32[]{:T(128)S(6)} %select_n.91, s32[]{:T(128)S(6)} %select_n.90, s32[]{:T(128)S(6)} %select_n.89), kind=kLoop, calls=%fused_computation.94 | loop fusion | bytes 4194320 | tf_op jit(solution)/shard_map/dynamic_slice | solution.py:96
  51.8 1.6 reshape.161
  53.3 2.4 %reshape.160 = f32[64,4,512]{2,1,0:T(4,128)} reshape(f32[64,2048]{1,0:T(8,128)} %get-tuple-element.16) | data formatting | bytes 1048576 | tf_op jit(solution)/shard_map/reshape | solution.py:58
  55.7 2.2 %reshape.159 = f32[64,4,512]{2,1,0:T(4,128)} reshape(f32[64,2048]{1,0:T(8,128)} %get-tuple-element.17) | data formatting | bytes 1048576 | tf_op jit(solution)/shard_map/reshape | solution.py:58
  58.0 2.2 %multiply_reduce_fusion.3 = f32[4,64]{1,0:T(4,128)S(1)} fusion(f32[4,64,512]{2,0,1:T(4,128)} %copy.41, f32[1,4,64,512]{3,1,2,0:T(4,128)S(1)} %bitcast.153, f32[1,4,64,512]{3,1,2,0:T(4,128)} %bitcast.155, f32[1,4,64,512]{3,1,2,0:T(4,128)} %bitcast.157, f32[1,4,64,512]{3,1,2,0:T(4,128)S(1)} %bitcast.151), kind=kLoop, calls=%fused_computation.11 | loop fusion | flops 2621184 | bytes 2622464 | tf_op jit(solution)/shard_map/reduce_sum | solution.py:107
  60.2 13.1 %all-to-all-done = f32[8,136,512]{2,1,0:T(8,128)S(1)} async-done(((f32[8,136,512]{2,1,0:T(8,128)}), f32[8,136,512]{2,1,0:T(8,128)S(1)}, u32[]{:S(2)}, u32[]{:S(2)}) %all-to-all-start) | async-done | bytes 2228256 | tf_op jit(solution)/shard_map/all_to_all | solution.py:73
  73.8 3.0 %fusion.2 = f32[6,128,512]{2,1,0:T(8,128)S(1)} fusion(bf16[10,512,512]{2,1,0:T(8,128)(2,1)} %param.8, bf16[6,64,512]{2,1,0:T(8,128)(2,1)S(1)} %get-tuple-element.21, bf16[6,64,512]{2,1,0:T(8,128)(2,1)S(1)} %get-tuple-element.20), kind=kOutput, calls=%fused_computation.5 | convolution fusion | flops 404226048 | bytes 5505024 | tf_op jit(solution)/shard_map/dot_general | solution.py:21
  78.2 2.3 %reduce-precision_convert_fusion.2 = (bf16[4,64,512]{2,1,0:T(8,128)(2,1)}, f32[4,64,512]{2,1,0:T(8,128)S(1)}, f32[4,64,512]{2,1,0:T(8,128)S(1)}) fusion(f32[4,512]{1,0:T(4,128)S(1)} %multiply_add_fusion.1, f32[4,64,512]{2,1,0:T(8,128)S(1)} %multiply_reduce_fusion.1, f32[4,128,512]{2,1,0:T(8,128)S(1)} %copy-done.11, f32[]{:T(128)} %bitcast.2, ...), kind=kLoop, calls=%fused_computation.34 | loop fusion | flops 1179648 | bytes 3416072 | tf_op jit(solution)/shard_map/convert_element_type | solution.py:15
  84.9 1.6 pad_maximum_fusion.1
  86.5 4.5 %all-to-all-start.1 = ((f32[8,136,512]{2,1,0:T(8,128)}), f32[8,136,512]{2,1,0:T(8,128)}, u32[]{:S(2)}, u32[]{:S(2)}) async-start(f32[8,136,512]{2,1,0:T(8,128)} %pad_maximum_fusion.1), calls=%async_computation.1 | async-start | bytes 4456448 | tf_op jit(solution)/shard_map/all_to_all | solution.py:73
  92.3 3.5 %fusion.4 = f32[4,128,512]{2,1,0:T(8,128)} fusion(bf16[10,512,512]{2,1,0:T(8,128)(2,1)} %param.8, bf16[4,64,512]{2,1,0:T(8,128)(2,1)S(1)} %fusion.17, bf16[4,64,512]{2,1,0:T(8,128)(2,1)} %get-tuple-element.11), kind=kOutput, calls=%fused_computation.12 | convolution fusion | flops 269484032 | bytes 3670016 | tf_op jit(solution)/shard_map/dot_general | solution.py:21
  95.8 45.8 %all-to-all-done.1 = f32[8,136,512]{2,1,0:T(8,128)} async-done(((f32[8,136,512]{2,1,0:T(8,128)}), f32[8,136,512]{2,1,0:T(8,128)}, u32[]{:S(2)}, u32[]{:S(2)}) %all-to-all-start.1) | async-done | bytes 2228256 | tf_op jit(solution)/shard_map/all_to_all | solution.py:73
  142.8 1.8 %slice.192 = f32[8,128,512]{2,1,0:T(8,128)S(1)} slice(f32[8,136,512]{2,1,0:T(8,128)} %all-to-all-done.1), slice={[0:8], [0:128], [0:512]} | slice | bytes 4194304 | tf_op jit(solution)/shard_map/slice | solution.py:76
  144.9 3.0 %fusion = f32[6,128,512]{2,1,0:T(8,128)S(1)} fusion(bf16[10,512,512]{2,1,0:T(8,128)(2,1)} %param.8, bf16[6,64,512]{2,1,0:T(8,128)(2,1)S(1)} %get-tuple-element.19, bf16[6,64,512]{2,1,0:T(8,128)(2,1)S(1)} %get-tuple-element.18), kind=kOutput, calls=%fused_computation.3 | convolution fusion | flops 404226048 | bytes 5505024 | tf_op jit(solution)/shard_map/dot_general | solution.py:21
  149.6 1.8 %fusion.26 = (f32[4,64,512]{2,1,0:T(8,128)S(1)}, f32[4,64,512]{2,1,0:T(8,128)S(1)}) fusion(f32[4,64,512]{2,1,0:T(8,128)S(1)} %multiply_reduce_fusion, f32[4,128,512]{2,1,0:T(8,128)S(1)} %copy-done.13, f32[64]{0:T(128)S(1)} %get-tuple-element.34, f32[]{:T(128)} %bitcast.2, f32[]{:T(128)} %bitcast.1, f32[4,64,512]{2,1,0:T(8,128)S(1)} %copy-done.4, ...), kind=kLoop, calls=%fused_computation.49 | loop fusion | flops 1572864 | bytes 5251336 | tf_op jit(solution)/shard_map/add | solution.py:117
  154.7 3.6 %all-to-all-start.2 = ((f32[32,1,832]{2,1,0:T(1,128)}), f32[32,1,832]{2,1,0:T(1,128)S(1)}, u32[]{:S(2)}, u32[]{:S(2)}) async-start(f32[32,1,832]{2,1,0:T(1,128)} %reshape.175), calls=%async_computation.2 | async-start | bytes 229376 | tf_op jit(solution)/shard_map/all_to_all | solution.py:127
  158.3 8.0 %all-to-all-done.2 = f32[32,1,832]{2,1,0:T(1,128)S(1)} async-done(((f32[32,1,832]{2,1,0:T(1,128)}), f32[32,1,832]{2,1,0:T(1,128)S(1)}, u32[]{:S(2)}, u32[]{:S(2)}) %all-to-all-start.2) | async-done | bytes 106528 | tf_op jit(solution)/shard_map/all_to_all | solution.py:127
  (113 shorter events, 21.1 us)
Async XLA Ops:
  7.2 5.2 %copy-start = (f32[64,2048]{1,0:T(8,128)S(1)}, f32[64,2048]{1,0:T(8,128)}, u32[]{:S(2)}) copy-start(f32[64,2048]{1,0:T(8,128)} %param.6) | copy-start | bytes 1572868
  14.8 8.2 %copy-start.14 = (s32[10]{0:T(128)S(1)}, s32[10]{0:T(128)}, u32[]{:S(2)}) copy-start(s32[10]{0:T(128)} %param.10) | copy-start | bytes 124
  14.8 18.2 %copy-start.15 = (s32[10]{0:T(128)S(1)}, s32[10]{0:T(128)}, u32[]{:S(2)}) copy-start(s32[10]{0:T(128)} %param.9) | copy-start | bytes 124
  14.8 58.5 %all-to-all-start = ((f32[8,136,512]{2,1,0:T(8,128)}), f32[8,136,512]{2,1,0:T(8,128)S(1)}, u32[]{:S(2)}, u32[]{:S(2)}) async-start(f32[8,136,512]{2,1,0:T(8,128)} %pad_maximum_fusion), calls=%async_computation | async-start | bytes 4456448 | tf_op jit(solution)/shard_map/all_to_all | solution.py:73
  22.3 26.4 %all-gather.2.cloned.1.call-start = ((), (), s32[]{:S(2)}) async-start(), calls=%async_computation.3 | async-start | bytes 2621440 | tf_op jit(solution)/shard_map/all_gather | solution.py:91
  51.7 8.5 %copy-start.5 = (f32[64,4,512]{2,1,0:T(4,128)}, f32[64,4,512]{2,1,0:T(4,128)S(1)}, u32[]{:S(2)}) copy-start(f32[64,4,512]{2,1,0:T(4,128)S(1)} %reshape.158) | copy-start | bytes 1572868
  53.3 6.9 %copy-start.7 = (f32[64,4,512]{2,1,0:T(4,128)}, f32[64,4,512]{2,1,0:T(4,128)S(1)}, u32[]{:S(2)}) copy-start(f32[64,4,512]{2,1,0:T(4,128)S(1)} %reshape.161) | copy-start | bytes 1572868
  76.8 1.0 copy-start.1
  76.9 1.4 copy-start.11
  78.2 3.9 %copy-start.3 = (f32[4,64,512]{2,1,0:T(8,128)}, f32[4,64,512]{2,1,0:T(8,128)S(1)}, u32[]{:S(2)}) copy-start(f32[4,64,512]{2,1,0:T(8,128)S(1)} %multiply_reduce_fusion.1) | copy-start | bytes 1572868
  80.5 0.8 copy-start.2
  86.5 55.1 %all-to-all-start.1 = ((f32[8,136,512]{2,1,0:T(8,128)}), f32[8,136,512]{2,1,0:T(8,128)}, u32[]{:S(2)}, u32[]{:S(2)}) async-start(f32[8,136,512]{2,1,0:T(8,128)} %pad_maximum_fusion.1), calls=%async_computation.1 | async-start | bytes 4456448 | tf_op jit(solution)/shard_map/all_to_all | solution.py:73
  147.9 1.0 copy-start.4
  147.9 1.4 copy-start.12
  148.0 1.7 copy-start.13
  151.4 1.0 copy-start.6
  151.4 1.2 copy-start.8
  151.5 1.3 copy-start.9
  151.5 1.5 copy-start.10
  154.7 11.6 %all-to-all-start.2 = ((f32[32,1,832]{2,1,0:T(1,128)}), f32[32,1,832]{2,1,0:T(1,128)S(1)}, u32[]{:S(2)}, u32[]{:S(2)}) async-start(f32[32,1,832]{2,1,0:T(1,128)} %reshape.175), calls=%async_computation.2 | async-start | bytes 229376 | tf_op jit(solution)/shard_map/all_to_all | solution.py:127
Sparse Core Ops, SparseCore 0:
  24.6 23.9 all-gather.1

commit v9 on v8

--- a/solution.py
+++ b/solution.py
@@ -61,15 +61,16 @@
         return jnp.transpose(x, (1, 0, 2)).reshape(cols_here, rows_here)
 
     def exchange(x, extra):
-        rolled = jnp.stack([jnp.roll(x, -t, axis=0) for t in range(NEED)], axis=1)
         width = x.shape[1]
-        rolled = rolled.reshape(row_tiles, NEED * width, tile_size)
-        pieces = jnp.tile(rolled, (peers // row_tiles, 1, 1))
+        side = []
         if extra is not None:
             flat = extra.reshape(-1)
             flat = jnp.pad(flat, (0, PAD_ROWS * tile_size - flat.shape[0]))
-            side = jnp.broadcast_to(flat.reshape(1, PAD_ROWS, tile_size), (peers, PAD_ROWS, tile_size))
-            pieces = jnp.concatenate([pieces, side], axis=1)
+            side = [flat.reshape(PAD_ROWS, tile_size)]
+        rows = []
+        for p in range(peers):
+            rows += [x[(p + t) % row_tiles] for t in range(NEED)] + side
+        pieces = jnp.concatenate(rows, axis=0).reshape(peers, -1, tile_size)
         arrived = lax.all_to_all(pieces, "ind", split_axis=0, concat_axis=0, tiled=True)
         if extra is None:
             return arrived.reshape(peers * NEED, width, tile_size), None
@@ -79,8 +80,7 @@
 
     def kprod(x, arrived):
         width = x.shape[1]
-        picked = jnp.stack([lax.dynamic_index_in_dim(arrived, position[s], 0, keepdims=False)
-                            for s in range(off_count)])
+        picked = jnp.take(arrived, position, axis=0, mode="clip")
         near = batched_tile_dot(x, grm_tiles[:row_tiles])
         far = batched_tile_dot(picked, grm_tiles[row_tiles:])
         return near + jnp.sum(weight[:, :, None, None] * far[:, None], axis=0)
@@ -99,16 +99,16 @@
 
     def chunk(g, geno_sub):
         z0 = g / precond
-        tiles0, sums0 = exchange(z0, colsum(g * z0)[None])
-        rz0 = sums0[0]
+        tiles0, _ = exchange(z0, None)
         kz0 = kprod(z0, tiles0)
         image0 = tau0 * z0 + tau1 * kz0
         w = image0 / precond
         p0_local = jnp.sum(geno_sub * z0[None], axis=(1, 3))
-        extra1 = jnp.concatenate([colsum(z0 * image0)[None], p0_local], axis=0)
+        extra1 = jnp.concatenate([colsum(g * z0)[None], colsum(z0 * image0)[None], p0_local], axis=0)
         tiles1, sums1 = exchange(w, extra1)
-        dad0 = sums1[0]
-        p0 = sums1[1:]
+        rz0 = sums1[0]
+        dad0 = sums1[1]
+        p0 = sums1[2:]
         alpha0 = rz0 / dad0
         resid1 = g - alpha0[None, :, None] * image0
         z1 = resid1 / precond

time: 178 us -> 182 us (1.022)
  waiting for transfers between devices: 75.9 us -> 94 us
  between operations: 26.5 us -> 15.3 us
  other arithmetic: 21 us -> 12.6 us
  local copies, waits for them, and re-layouts: 24.8 us -> 31.8 us
    all_to_all x2, waiting for transfers between devices: 58.9 us -> 85.4 us  [exchange(): lax.all_to_all(pieces, 'ind', split_axis=0, concat_axis=0, tiled=True)]
    unnamed x48 -> x80, local copies, waits for them, and re-layouts: 5.92 us -> 15.5 us
    all_gather x1, waiting for transfers between devices: 8.36 us -> 0.01 us  [local(): geno_all = lax.all_gather(genotypes, 'var', axis=0, tiled=True)]
    gather x0 -> x2, local copies, waits for them, and re-layouts: none -> 4.37 us  [kprod(): picked = jnp.take(arrived, position, axis=0, mode='clip')]
    reshape x4, local copies, waits for them, and re-layouts: 6.53 us -> 2.63 us  [to_tiles(): return jnp.transpose(x.reshape(cols_here, row_tiles, tile_size), (1, 0, 2))]
    concatenate x3 -> x1, other arithmetic: 3.24 us -> 0.01 us  [chunk(): jnp.concatenate([colsum(g * z0)[None], colsum(z0 * image0)[None], p0_loca...]
    another operation x4 -> x0, other arithmetic: 2.29 us -> none  [exchange(): rolled = jnp.stack([jnp.roll(x, -t, axis=0) for t in range(NEED)], axis=1)]
    convert_element_type x5, other arithmetic: 3.86 us -> 2.02 us  [split2(): return (hi.astype(jnp.bfloat16), lo.astype(jnp.bfloat16))]
  transfers between devices with their start and end apart: 4 -> 4, of which waited for: 4 -> 3; matrix products, arithmetic and copies ran while one was open for 12% -> 16% of each run, Pallas kernels for 0% -> 0%
where the time goes in v9:
time: 182 us; the launch traced here: 181 us
  waiting for transfers between devices  94 us (52%)
  local copies, waits for them, and re-layouts  31.8 us (17%)
  between operations  15.3 us (8%)
  starting transfers between devices  14.8 us (8%)
  matrix products  12.8 us (7%)
  other arithmetic  12.6 us (7%)
    all_to_all x2, waiting for transfers between devices, exchange(): lax.all_to_all(pieces, 'ind', split_axis=0, concat_axis=0, tiled=True)  85.4 us
    unnamed x80, local copies, waits for them, and re-layouts  15.5 us
    dot_general x4, matrix products, batched_tile_dot(): lax.dot_general(parts, tiles, (((2,), (2,)), ((0,), (0,))), preferred_ele...  12.8 us
    all_to_all x2, starting transfers between devices, exchange(): lax.all_to_all(pieces, 'ind', split_axis=0, concat_axis=0, tiled=True)  11.1 us
    all_to_all x1, waiting for transfers between devices, chunk(): lax.all_to_all(spread, ('ind', 'var'), split_axis=0, concat_axis=0, tiled...  7.98 us
    gather x2, local copies, waits for them, and re-layouts, kprod(): picked = jnp.take(arrived, position, axis=0, mode='clip')  4.37 us
    all_to_all x1, starting transfers between devices, chunk(): lax.all_to_all(spread, ('ind', 'var'), split_axis=0, concat_axis=0, tiled...  3.68 us
  transfers between devices with their start and end apart: 4, of which 3 were waited for; matrix products, arithmetic and copies ran while one was open for 16% of the time, Pallas kernels for 0%

profile of v9, /device:TPU:0, one launch (start us, length us, event | category | flops | bytes accessed | tf_op | source)
XLA Modules:
  0.0 181.4 jit_solution(12309589584208854277)
XLA Ops:
  8.0 1.4 fusion.82
  9.4 2.4 %select_reduce_fusion = f32[4,512]{1,0:T(4,128)S(1)} fusion(pred[512,512]{1,0:T(8,128)(4,1)S(1)} %iota_compare_fusion, bf16[10,512,512]{2,1,0:T(8,128)(2,1)} %param.8), kind=kLoop, calls=%fused_computation.2 | loop fusion | flops 3143680 | bytes 2367488 | tf_op jit(solution)/shard_map/reduce_sum | solution.py:45
  11.8 1.3 multiply_add_fusion.1
  23.9 7.4 %all-to-all-start = ((f32[8,128,512]{2,1,0:T(8,128)}), f32[8,128,512]{2,1,0:T(8,128)}, u32[]{:S(2)}, u32[]{:S(2)}) async-start(f32[8,128,512]{2,1,0:T(8,128)} %bitcast.8), calls=%async_computation | async-start | bytes 4194304 | tf_op jit(solution)/shard_map/all_to_all | solution.py:74
  32.6 3.4 %fusion.6 = f32[4,128,512]{2,1,0:T(8,128)} fusion(bf16[10,512,512]{2,1,0:T(8,128)(2,1)} %param.8, bf16[4,64,512]{2,1,0:T(8,128)(2,1)S(1)} %get-tuple-element.25, bf16[4,64,512]{2,1,0:T(8,128)(2,1)S(1)} %get-tuple-element.24), kind=kOutput, calls=%fused_computation.14 | convolution fusion | flops 269484032 | bytes 3670016 | tf_op jit(solution)/shard_map/dot_general | solution.py:21
  36.0 2.5 %constant_dynamic-slice_fusion.6 = (f32[64,2048]{1,0:T(8,128)S(1)}, f32[64,2048]{1,0:T(8,128)}, f32[64,2048]{1,0:T(8,128)S(1)}, f32[64,2048]{1,0:T(8,128)S(1)}) fusion(f32[256,2048]{1,0:T(8,128)} %all-gather.2.cloned.1.call-done, s32[]{:T(128)S(6)} %select_n.57, s32[]{:T(128)S(6)} %select_n.60, s32[]{:T(128)S(6)} %select_n.59, s32[]{:T(128)S(6)} %select_n.58), kind=kLoop, calls=%fused_computation.137 | loop fusion | bytes 4194320 | tf_op jit(solution)/shard_map/dynamic_slice | solution.py:96
  39.6 1.6 reshape.148
  41.2 0.9 multiply_reduce_fusion.3
  42.1 37.6 %all-to-all-done = f32[8,128,512]{2,1,0:T(8,128)} async-done(((f32[8,128,512]{2,1,0:T(8,128)}), f32[8,128,512]{2,1,0:T(8,128)}, u32[]{:S(2)}, u32[]{:S(2)}) %all-to-all-start) | async-done | bytes 2097184 | tf_op jit(solution)/shard_map/all_to_all | solution.py:74
  79.7 2.2 %gather_fusion = f32[6,64,512]{2,1,0:T(8,128)S(1)} fusion(f32[16,64,512]{2,1,0:T(8,128)} %bitcast.9, s32[1024]{0:T(1024)S(1)} %pad_clamp_fusion), kind=kCustom, calls=%fused_computation | custom fusion | bytes 1572888 | tf_op jit(solution)/shard_map/jit(_take)/gather | solution.py:83
  82.0 3.0 %fusion.2 = f32[6,128,512]{2,1,0:T(8,128)S(1)} fusion(bf16[10,512,512]{2,1,0:T(8,128)(2,1)} %param.8, bf16[6,64,512]{2,1,0:T(8,128)(2,1)S(1)} %get-tuple-element.23, bf16[6,64,512]{2,1,0:T(8,128)(2,1)S(1)} %get-tuple-element.22), kind=kOutput, calls=%fused_computation.7 | convolution fusion | flops 404226048 | bytes 5505024 | tf_op jit(solution)/shard_map/dot_general | solution.py:21
  86.3 1.6 reduce-precision_convert_fusion.2
  89.4 1.4 copy-done.15
  90.8 3.6 %all-to-all-start.1 = ((f32[8,136,512]{2,1,0:T(8,128)}), f32[8,136,512]{2,1,0:T(8,128)S(1)}, u32[]{:S(2)}, u32[]{:S(2)}) async-start(f32[8,136,512]{2,1,0:T(8,128)} %bitcast.216), calls=%async_computation.1 | async-start | bytes 4456448 | tf_op jit(solution)/shard_map/all_to_all | solution.py:74
  94.5 3.4 %fusion.4 = f32[4,128,512]{2,1,0:T(8,128)} fusion(bf16[10,512,512]{2,1,0:T(8,128)(2,1)} %param.8, bf16[4,64,512]{2,1,0:T(8,128)(2,1)S(1)} %fusion.17, bf16[4,64,512]{2,1,0:T(8,128)(2,1)S(1)} %get-tuple-element.13), kind=kOutput, calls=%fused_computation.12 | convolution fusion | flops 269484032 | bytes 3670016 | tf_op jit(solution)/shard_map/dot_general | solution.py:21
  97.9 47.8 %all-to-all-done.1 = f32[8,136,512]{2,1,0:T(8,128)S(1)} async-done(((f32[8,136,512]{2,1,0:T(8,128)}), f32[8,136,512]{2,1,0:T(8,128)S(1)}, u32[]{:S(2)}, u32[]{:S(2)}) %all-to-all-start.1) | async-done | bytes 2228256 | tf_op jit(solution)/shard_map/all_to_all | solution.py:74
  145.9 1.6 slice.198
  147.5 2.2 %gather_fusion.1 = f32[6,64,512]{2,1,0:T(8,128)S(1)} fusion(f32[16,64,512]{2,1,0:T(8,128)} %bitcast.215, s32[1024]{0:T(1024)S(1)} %pad_clamp_fusion), kind=kCustom, calls=%fused_computation.1 | custom fusion | bytes 1572888 | tf_op jit(solution)/shard_map/jit(_take)/gather | solution.py:83
  149.8 3.0 %fusion = f32[6,128,512]{2,1,0:T(8,128)S(1)} fusion(bf16[10,512,512]{2,1,0:T(8,128)(2,1)} %param.8, bf16[6,64,512]{2,1,0:T(8,128)(2,1)S(1)} %get-tuple-element.21, bf16[6,64,512]{2,1,0:T(8,128)(2,1)S(1)} %get-tuple-element.20), kind=kOutput, calls=%fused_computation.5 | convolution fusion | flops 404226048 | bytes 5505024 | tf_op jit(solution)/shard_map/dot_general | solution.py:21
  154.7 2.0 %fusion.26 = (f32[4,64,512]{2,1,0:T(8,128)S(1)}, f32[4,64,512]{2,1,0:T(8,128)S(1)}) fusion(f32[4,64,512]{2,1,0:T(8,128)S(1)} %multiply_reduce_fusion, f32[4,128,512]{2,1,0:T(8,128)S(1)} %copy-done.16, f32[64]{0:T(128)S(1)} %get-tuple-element.34, f32[]{:T(128)} %bitcast.2, f32[]{:T(128)} %bitcast, f32[4,64,512]{2,1,0:T(8,128)S(1)} %copy-done.4, ...), kind=kLoop, calls=%fused_computation.47 | loop fusion | flops 1572864 | bytes 5251336 | tf_op jit(solution)/shard_map/add | solution.py:117
  157.1 0.9 multiply_reduce_fusion.2
  159.4 3.7 %all-to-all-start.2 = ((f32[32,1,832]{2,1,0:T(1,128)}), f32[32,1,832]{2,1,0:T(1,128)S(1)}, u32[]{:S(2)}, u32[]{:S(2)}) async-start(f32[32,1,832]{2,1,0:T(1,128)} %reshape.182), calls=%async_computation.2 | async-start | bytes 229376 | tf_op jit(solution)/shard_map/all_to_all | solution.py:127
  163.1 8.0 %all-to-all-done.2 = f32[32,1,832]{2,1,0:T(1,128)S(1)} async-done(((f32[32,1,832]{2,1,0:T(1,128)}), f32[32,1,832]{2,1,0:T(1,128)S(1)}, u32[]{:S(2)}, u32[]{:S(2)}) %all-to-all-start.2) | async-done | bytes 106528 | tf_op jit(solution)/shard_map/all_to_all | solution.py:127
  171.6 0.9 reduce.4
  (127 shorter events, 22.3 us)
Async XLA Ops:
  7.2 6.0 %copy-start = (f32[64,2048]{1,0:T(8,128)S(1)}, f32[64,2048]{1,0:T(8,128)}, u32[]{:S(2)}) copy-start(f32[64,2048]{1,0:T(8,128)} %param.6) | copy-start | bytes 1572868
  7.2 28.8 %all-gather.2.cloned.1.call-start = ((), (), s32[]{:S(2)}) async-start(), calls=%async_computation.3 | async-start | bytes 2621440 | tf_op jit(solution)/shard_map/all_gather | solution.py:91
  23.9 8.4 %copy-start.17 = (s32[10]{0:T(128)S(1)}, s32[10]{0:T(128)}, u32[]{:S(2)}) copy-start(s32[10]{0:T(128)} %param.9) | copy-start | bytes 124
  23.9 8.5 %copy-start.18 = (s32[10]{0:T(128)S(1)}, s32[10]{0:T(128)}, u32[]{:S(2)}) copy-start(s32[10]{0:T(128)} %param.10) | copy-start | bytes 124
  23.9 55.8 %all-to-all-start = ((f32[8,128,512]{2,1,0:T(8,128)}), f32[8,128,512]{2,1,0:T(8,128)}, u32[]{:S(2)}, u32[]{:S(2)}) async-start(f32[8,128,512]{2,1,0:T(8,128)} %bitcast.8), calls=%async_computation | async-start | bytes 4194304 | tf_op jit(solution)/shard_map/all_to_all | solution.py:74
  38.8 3.2 %copy-start.5 = (f32[64,4,512]{2,1,0:T(4,128)}, f32[64,4,512]{2,1,0:T(4,128)S(1)}, u32[]{:S(2)}) copy-start(f32[64,4,512]{2,1,0:T(4,128)S(1)} %reshape.145) | copy-start | bytes 1572868
  39.2 2.9 %copy-start.7 = (f32[64,4,512]{2,1,0:T(4,128)}, f32[64,4,512]{2,1,0:T(4,128)S(1)}, u32[]{:S(2)}) copy-start(f32[64,4,512]{2,1,0:T(4,128)S(1)} %reshape.146) | copy-start | bytes 1572868
  39.6 42.3 %copy-start.9 = (f32[64,4,512]{2,1,0:T(4,128)}, f32[64,4,512]{2,1,0:T(4,128)S(1)}, u32[]{:S(2)}) copy-start(f32[64,4,512]{2,1,0:T(4,128)S(1)} %reshape.147) | copy-start | bytes 1572868
  41.2 40.8 %copy-start.11 = (f32[64,4,512]{2,1,0:T(4,128)}, f32[64,4,512]{2,1,0:T(4,128)S(1)}, u32[]{:S(2)}) copy-start(f32[64,4,512]{2,1,0:T(4,128)S(1)} %reshape.148) | copy-start | bytes 1572868
  85.0 1.2 copy-start.13
  86.3 2.6 %copy-start.3 = (f32[4,64,512]{2,1,0:T(8,128)}, f32[4,64,512]{2,1,0:T(8,128)S(1)}, u32[]{:S(2)}) copy-start(f32[4,64,512]{2,1,0:T(8,128)S(1)} %multiply_reduce_fusion.1) | copy-start | bytes 1572868
  87.9 0.8 copy-start.1
  89.4 1.4 copy-start.15
  90.8 54.9 %all-to-all-start.1 = ((f32[8,136,512]{2,1,0:T(8,128)}), f32[8,136,512]{2,1,0:T(8,128)S(1)}, u32[]{:S(2)}, u32[]{:S(2)}) async-start(f32[8,136,512]{2,1,0:T(8,128)} %bitcast.216), calls=%async_computation.1 | async-start | bytes 4456448 | tf_op jit(solution)/shard_map/all_to_all | solution.py:74
  152.8 1.0 copy-start.2
  152.8 1.2 copy-start.4
  152.9 1.5 copy-start.14
  152.9 1.8 %copy-start.16 = (f32[4,128,512]{2,1,0:T(8,128)S(1)}, f32[4,128,512]{2,1,0:T(8,128)}, u32[]{:S(2)}) copy-start(f32[4,128,512]{2,1,0:T(8,128)} %fusion.4) | copy-start | bytes 3145732
  154.7 2.4 %copy-start.6 = (f32[64,4,512]{2,1,0:T(4,128)S(1)}, f32[64,4,512]{2,1,0:T(4,128)}, u32[]{:S(2)}) copy-start(f32[64,4,512]{2,1,0:T(4,128)} %copy-done.5) | copy-start | bytes 1572868
  154.7 2.4 %copy-start.8 = (f32[64,4,512]{2,1,0:T(4,128)S(1)}, f32[64,4,512]{2,1,0:T(4,128)}, u32[]{:S(2)}) copy-start(f32[64,4,512]{2,1,0:T(4,128)} %copy-done.7) | copy-start | bytes 1572868
  154.7 2.4 %copy-start.10 = (f32[64,4,512]{2,1,0:T(4,128)S(1)}, f32[64,4,512]{2,1,0:T(4,128)}, u32[]{:S(2)}) copy-start(f32[64,4,512]{2,1,0:T(4,128)} %copy-done.9) | copy-start | bytes 1572868
  154.7 2.4 %copy-start.12 = (f32[64,4,512]{2,1,0:T(4,128)S(1)}, f32[64,4,512]{2,1,0:T(4,128)}, u32[]{:S(2)}) copy-start(f32[64,4,512]{2,1,0:T(4,128)} %copy-done.11) | copy-start | bytes 1572868
  159.4 11.7 %all-to-all-start.2 = ((f32[32,1,832]{2,1,0:T(1,128)}), f32[32,1,832]{2,1,0:T(1,128)S(1)}, u32[]{:S(2)}, u32[]{:S(2)}) async-start(f32[32,1,832]{2,1,0:T(1,128)} %reshape.182), calls=%async_computation.2 | async-start | bytes 229376 | tf_op jit(solution)/shard_map/all_to_all | solution.py:127
Sparse Core Ops, SparseCore 0:
  9.5 25.2 all-gather.1

commit v10 on v8

--- a/solution.py
+++ b/solution.py
@@ -60,19 +60,23 @@
     def from_tiles(x):
         return jnp.transpose(x, (1, 0, 2)).reshape(cols_here, rows_here)
 
-    def exchange(x, extra):
-        rolled = jnp.stack([jnp.roll(x, -t, axis=0) for t in range(NEED)], axis=1)
+    def exchange(x, extra, by_concat=False):
         width = x.shape[1]
-        rolled = rolled.reshape(row_tiles, NEED * width, tile_size)
-        pieces = jnp.tile(rolled, (peers // row_tiles, 1, 1))
-        if extra is not None:
-            flat = extra.reshape(-1)
-            flat = jnp.pad(flat, (0, PAD_ROWS * tile_size - flat.shape[0]))
+        flat = extra.reshape(-1)
+        flat = jnp.pad(flat, (0, PAD_ROWS * tile_size - flat.shape[0]))
+        if by_concat:
+            rows = []
+            for p in range(peers):
+                rows += [x[(p + t) % row_tiles] for t in range(NEED)]
+                rows.append(flat.reshape(PAD_ROWS, tile_size))
+            pieces = jnp.concatenate(rows, axis=0).reshape(peers, -1, tile_size)
+        else:
+            rolled = jnp.stack([jnp.roll(x, -t, axis=0) for t in range(NEED)], axis=1)
+            rolled = rolled.reshape(row_tiles, NEED * width, tile_size)
+            pieces = jnp.tile(rolled, (peers // row_tiles, 1, 1))
             side = jnp.broadcast_to(flat.reshape(1, PAD_ROWS, tile_size), (peers, PAD_ROWS, tile_size))
             pieces = jnp.concatenate([pieces, side], axis=1)
         arrived = lax.all_to_all(pieces, "ind", split_axis=0, concat_axis=0, tiled=True)
-        if extra is None:
-            return arrived.reshape(peers * NEED, width, tile_size), None
         tiles_in = arrived[:, :NEED * width].reshape(peers * NEED, width, tile_size)
         sums = jnp.sum(arrived[:, NEED * width:].reshape(peers, -1)[:, :extra.size], axis=0)
         return tiles_in, sums.reshape(extra.shape)
@@ -106,7 +110,7 @@
         w = image0 / precond
         p0_local = jnp.sum(geno_sub * z0[None], axis=(1, 3))
         extra1 = jnp.concatenate([colsum(z0 * image0)[None], p0_local], axis=0)
-        tiles1, sums1 = exchange(w, extra1)
+        tiles1, sums1 = exchange(w, extra1, by_concat=True)
         dad0 = sums1[0]
         p0 = sums1[1:]
         alpha0 = rz0 / dad0

time: 178 us -> 175 us (0.983)
  other arithmetic: 21 us -> 16.2 us
    another operation x4 -> x2, other arithmetic: 2.29 us -> 0.14 us  [exchange(): rolled = jnp.stack([jnp.roll(x, -t, axis=0) for t in range(NEED)], axis=1)]
    unnamed x48 -> x75, local copies, waits for them, and re-layouts: 5.92 us -> 7.69 us
where the time goes in v10:
time: 175 us; the launch traced here: 174 us
  waiting for transfers between devices  76.9 us (44%)
  between operations  26.7 us (15%)
  local copies, waits for them, and re-layouts  25.4 us (15%)
  other arithmetic  16.2 us (9%)
  starting transfers between devices  15.6 us (9%)
  matrix products  12.9 us (7%)
    all_to_all x2, waiting for transfers between devices, exchange(): lax.all_to_all(pieces, 'ind', split_axis=0, concat_axis=0, tiled=True)  59.9 us
    dot_general x4, matrix products, batched_tile_dot(): lax.dot_general(parts, tiles, (((2,), (2,)), ((0,), (0,))), preferred_ele...  12.9 us
    all_to_all x2, starting transfers between devices, exchange(): lax.all_to_all(pieces, 'ind', split_axis=0, concat_axis=0, tiled=True)  11.9 us
    all_gather x1, waiting for transfers between devices, local(): geno_all = lax.all_gather(genotypes, 'var', axis=0, tiled=True)  8.36 us
    all_to_all x1, waiting for transfers between devices, chunk(): lax.all_to_all(spread, ('ind', 'var'), split_axis=0, concat_axis=0, tiled...  7.98 us
    unnamed x75, local copies, waits for them, and re-layouts  7.69 us
    reshape x4, local copies, waits for them, and re-layouts, to_tiles(): return jnp.transpose(x.reshape(cols_here, row_tiles, tile_size), (1, 0, 2))  6.53 us
    all_to_all x1, starting transfers between devices, chunk(): lax.all_to_all(spread, ('ind', 'var'), split_axis=0, concat_axis=0, tiled...  3.6 us
  transfers between devices with their start and end apart: 4, of which 4 were waited for; matrix products, arithmetic and copies ran while one was open for 12% of the time, Pallas kernels for 0%

profile of v10, /device:TPU:0, one launch (start us, length us, event | category | flops | bytes accessed | tf_op | source)
XLA Modules:
  0.0 173.7 jit_solution(16137713693294986663)
XLA Ops:
  7.3 1.4 fusion.68
  8.6 2.4 %select_reduce_fusion = f32[4,512]{1,0:T(4,128)S(1)} fusion(pred[512,512]{1,0:T(8,128)(4,1)S(1)} %iota_compare_fusion, bf16[10,512,512]{2,1,0:T(8,128)(2,1)} %param.8), kind=kLoop, calls=%fused_computation | loop fusion | flops 3143680 | bytes 2367488 | tf_op jit(solution)/shard_map/reduce_sum | solution.py:45
  11.0 1.3 multiply_add_fusion.1
  13.2 1.6 pad_maximum_fusion
  14.8 7.4 %all-to-all-start = ((f32[8,136,512]{2,1,0:T(8,128)}), f32[8,136,512]{2,1,0:T(8,128)S(1)}, u32[]{:S(2)}, u32[]{:S(2)}) async-start(f32[8,136,512]{2,1,0:T(8,128)} %pad_maximum_fusion), calls=%async_computation | async-start | bytes 4456448 | tf_op jit(solution)/shard_map/all_to_all | solution.py:79
  36.9 3.4 %fusion.6 = f32[4,128,512]{2,1,0:T(8,128)} fusion(bf16[10,512,512]{2,1,0:T(8,128)(2,1)} %param.8, bf16[4,64,512]{2,1,0:T(8,128)(2,1)S(1)} %get-tuple-element.25, bf16[4,64,512]{2,1,0:T(8,128)(2,1)S(1)} %get-tuple-element.22), kind=kOutput, calls=%fused_computation.13 | convolution fusion | flops 269484032 | bytes 3670016 | tf_op jit(solution)/shard_map/dot_general | solution.py:21
  40.3 8.4 %all-gather.2.cloned.1.call-done = f32[256,2048]{1,0:T(8,128)} async-done(((f32[64,2048]{1,0:T(8,128)}), f32[256,2048]{1,0:T(8,128)}) %all-gather.2.cloned.1.call-update) | async-done | bytes 2097168 | tf_op jit(solution)/shard_map/all_gather | solution.py:95
  48.6 2.7 %constant_dynamic-slice_fusion.6 = (f32[64,2048]{1,0:T(8,128)S(1)}, f32[64,2048]{1,0:T(8,128)}, f32[64,2048]{1,0:T(8,128)}, f32[64,2048]{1,0:T(8,128)}) fusion(f32[256,2048]{1,0:T(8,128)} %all-gather.2.cloned.1.call-done, s32[]{:T(128)S(6)} %select_n.88, s32[]{:T(128)S(6)} %select_n.91, s32[]{:T(128)S(6)} %select_n.90, s32[]{:T(128)S(6)} %select_n.89), kind=kLoop, calls=%fused_computation.119 | loop fusion | bytes 4194320 | tf_op jit(solution)/shard_map/dynamic_slice | solution.py:100
  51.8 1.6 reshape.168
  53.3 2.4 %reshape.167 = f32[64,4,512]{2,1,0:T(4,128)} reshape(f32[64,2048]{1,0:T(8,128)} %get-tuple-element.16) | data formatting | bytes 1048576 | tf_op jit(solution)/shard_map/reshape | solution.py:58
  55.7 2.2 %reshape.166 = f32[64,4,512]{2,1,0:T(4,128)} reshape(f32[64,2048]{1,0:T(8,128)} %get-tuple-element.17) | data formatting | bytes 1048576 | tf_op jit(solution)/shard_map/reshape | solution.py:58
  58.0 2.2 %multiply_reduce_fusion.3 = f32[4,64]{1,0:T(4,128)S(1)} fusion(f32[4,64,512]{2,0,1:T(4,128)} %copy.37, f32[1,4,64,512]{3,1,2,0:T(4,128)S(1)} %bitcast.187, f32[1,4,64,512]{3,1,2,0:T(4,128)} %bitcast.189, f32[1,4,64,512]{3,1,2,0:T(4,128)} %bitcast.191, f32[1,4,64,512]{3,1,2,0:T(4,128)S(1)} %bitcast.185), kind=kLoop, calls=%fused_computation.10 | loop fusion | flops 2621184 | bytes 2622464 | tf_op jit(solution)/shard_map/reduce_sum | solution.py:111
  60.2 13.1 %all-to-all-done = f32[8,136,512]{2,1,0:T(8,128)S(1)} async-done(((f32[8,136,512]{2,1,0:T(8,128)}), f32[8,136,512]{2,1,0:T(8,128)S(1)}, u32[]{:S(2)}, u32[]{:S(2)}) %all-to-all-start) | async-done | bytes 2228256 | tf_op jit(solution)/shard_map/all_to_all | solution.py:79
  73.8 3.0 %fusion.2 = f32[6,128,512]{2,1,0:T(8,128)S(1)} fusion(bf16[10,512,512]{2,1,0:T(8,128)(2,1)} %param.8, bf16[6,64,512]{2,1,0:T(8,128)(2,1)S(1)} %get-tuple-element.21, bf16[6,64,512]{2,1,0:T(8,128)(2,1)S(1)} %get-tuple-element.20), kind=kOutput, calls=%fused_computation.5 | convolution fusion | flops 404226048 | bytes 5505024 | tf_op jit(solution)/shard_map/dot_general | solution.py:21
  78.2 2.3 %reduce-precision_convert_fusion.2 = (bf16[4,64,512]{2,1,0:T(8,128)(2,1)}, f32[4,64,512]{2,1,0:T(8,128)S(1)}, f32[4,64,512]{2,1,0:T(8,128)S(1)}) fusion(f32[4,512]{1,0:T(4,128)S(1)} %multiply_add_fusion.1, f32[4,64,512]{2,1,0:T(8,128)S(1)} %multiply_reduce_fusion.1, f32[4,128,512]{2,1,0:T(8,128)S(1)} %copy-done.12, f32[]{:T(128)} %bitcast.2, ...), kind=kLoop, calls=%fused_computation.32 | loop fusion | flops 1179648 | bytes 3416072 | tf_op jit(solution)/shard_map/convert_element_type | solution.py:15
  82.0 1.4 copy-done.14
  83.4 4.5 %all-to-all-start.1 = ((f32[8,136,512]{2,1,0:T(8,128)}), f32[8,136,512]{2,1,0:T(8,128)}, u32[]{:S(2)}, u32[]{:S(2)}) async-start(f32[8,136,512]{2,1,0:T(8,128)} %bitcast.206), calls=%async_computation.1 | async-start | bytes 4456448 | tf_op jit(solution)/shard_map/all_to_all | solution.py:79
  88.1 3.5 %fusion.4 = f32[4,128,512]{2,1,0:T(8,128)} fusion(bf16[10,512,512]{2,1,0:T(8,128)(2,1)} %param.8, bf16[4,64,512]{2,1,0:T(8,128)(2,1)S(1)} %fusion.17, bf16[4,64,512]{2,1,0:T(8,128)(2,1)} %get-tuple-element.11), kind=kOutput, calls=%fused_computation.11 | convolution fusion | flops 269484032 | bytes 3670016 | tf_op jit(solution)/shard_map/dot_general | solution.py:21
  91.6 46.8 %all-to-all-done.1 = f32[8,136,512]{2,1,0:T(8,128)} async-done(((f32[8,136,512]{2,1,0:T(8,128)}), f32[8,136,512]{2,1,0:T(8,128)}, u32[]{:S(2)}, u32[]{:S(2)}) %all-to-all-start.1) | async-done | bytes 2228256 | tf_op jit(solution)/shard_map/all_to_all | solution.py:79
  139.6 1.8 %slice.214 = f32[8,128,512]{2,1,0:T(8,128)S(1)} slice(f32[8,136,512]{2,1,0:T(8,128)} %all-to-all-done.1), slice={[0:8], [0:128], [0:512]} | slice | bytes 4194304 | tf_op jit(solution)/shard_map/slice | solution.py:80
  141.8 3.0 %fusion = f32[6,128,512]{2,1,0:T(8,128)S(1)} fusion(bf16[10,512,512]{2,1,0:T(8,128)(2,1)} %param.8, bf16[6,64,512]{2,1,0:T(8,128)(2,1)S(1)} %get-tuple-element.19, bf16[6,64,512]{2,1,0:T(8,128)(2,1)S(1)} %get-tuple-element.18), kind=kOutput, calls=%fused_computation.3 | convolution fusion | flops 404226048 | bytes 5505024 | tf_op jit(solution)/shard_map/dot_general | solution.py:21
  146.7 1.8 %fusion.26 = (f32[4,64,512]{2,1,0:T(8,128)S(1)}, f32[4,64,512]{2,1,0:T(8,128)S(1)}) fusion(f32[4,64,512]{2,1,0:T(8,128)S(1)} %multiply_reduce_fusion, f32[4,128,512]{2,1,0:T(8,128)S(1)} %copy-done.15, f32[64]{0:T(128)S(1)} %get-tuple-element.34, f32[]{:T(128)} %bitcast.2, f32[]{:T(128)} %bitcast.1, f32[4,64,512]{2,1,0:T(8,128)S(1)} %copy-done.5, ...), kind=kLoop, calls=%fused_computation.47 | loop fusion | flops 1572864 | bytes 5251336 | tf_op jit(solution)/shard_map/add | solution.py:121
  151.7 3.6 %all-to-all-start.2 = ((f32[32,1,832]{2,1,0:T(1,128)}), f32[32,1,832]{2,1,0:T(1,128)S(1)}, u32[]{:S(2)}, u32[]{:S(2)}) async-start(f32[32,1,832]{2,1,0:T(1,128)} %reshape.184), calls=%async_computation.2 | async-start | bytes 229376 | tf_op jit(solution)/shard_map/all_to_all | solution.py:131
  155.4 8.0 %all-to-all-done.2 = f32[32,1,832]{2,1,0:T(1,128)S(1)} async-done(((f32[32,1,832]{2,1,0:T(1,128)}), f32[32,1,832]{2,1,0:T(1,128)S(1)}, u32[]{:S(2)}, u32[]{:S(2)}) %all-to-all-start.2) | async-done | bytes 106528 | tf_op jit(solution)/shard_map/all_to_all | solution.py:131
  (133 shorter events, 17.2 us)
Async XLA Ops:
  7.2 5.2 %copy-start = (f32[64,2048]{1,0:T(8,128)S(1)}, f32[64,2048]{1,0:T(8,128)}, u32[]{:S(2)}) copy-start(f32[64,2048]{1,0:T(8,128)} %param.6) | copy-start | bytes 1572868
  14.8 8.2 %copy-start.16 = (s32[10]{0:T(128)S(1)}, s32[10]{0:T(128)}, u32[]{:S(2)}) copy-start(s32[10]{0:T(128)} %param.10) | copy-start | bytes 124
  14.8 18.2 %copy-start.17 = (s32[10]{0:T(128)S(1)}, s32[10]{0:T(128)}, u32[]{:S(2)}) copy-start(s32[10]{0:T(128)} %param.9) | copy-start | bytes 124
  14.8 58.5 %all-to-all-start = ((f32[8,136,512]{2,1,0:T(8,128)}), f32[8,136,512]{2,1,0:T(8,128)S(1)}, u32[]{:S(2)}, u32[]{:S(2)}) async-start(f32[8,136,512]{2,1,0:T(8,128)} %pad_maximum_fusion), calls=%async_computation | async-start | bytes 4456448 | tf_op jit(solution)/shard_map/all_to_all | solution.py:79
  22.3 26.4 %all-gather.2.cloned.1.call-start = ((), (), s32[]{:S(2)}) async-start(), calls=%async_computation.3 | async-start | bytes 2621440 | tf_op jit(solution)/shard_map/all_gather | solution.py:95
  51.7 8.5 %copy-start.6 = (f32[64,4,512]{2,1,0:T(4,128)}, f32[64,4,512]{2,1,0:T(4,128)S(1)}, u32[]{:S(2)}) copy-start(f32[64,4,512]{2,1,0:T(4,128)S(1)} %reshape.165) | copy-start | bytes 1572868
  53.3 6.9 %copy-start.8 = (f32[64,4,512]{2,1,0:T(4,128)}, f32[64,4,512]{2,1,0:T(4,128)S(1)}, u32[]{:S(2)}) copy-start(f32[64,4,512]{2,1,0:T(4,128)S(1)} %reshape.168) | copy-start | bytes 1572868
  76.8 1.0 copy-start.1
  76.9 1.4 copy-start.12
  78.2 3.3 %copy-start.4 = (f32[4,64,512]{2,1,0:T(8,128)}, f32[4,64,512]{2,1,0:T(8,128)S(1)}, u32[]{:S(2)}) copy-start(f32[4,64,512]{2,1,0:T(8,128)S(1)} %multiply_reduce_fusion.1) | copy-start | bytes 1572868
  80.5 0.8 copy-start.2
  82.0 1.4 copy-start.14
  83.4 55.1 %all-to-all-start.1 = ((f32[8,136,512]{2,1,0:T(8,128)}), f32[8,136,512]{2,1,0:T(8,128)}, u32[]{:S(2)}, u32[]{:S(2)}) async-start(f32[8,136,512]{2,1,0:T(8,128)} %bitcast.206), calls=%async_computation.1 | async-start | bytes 4456448 | tf_op jit(solution)/shard_map/all_to_all | solution.py:79
  144.8 1.0 copy-start.3
  144.8 1.2 copy-start.5
  144.8 1.5 copy-start.13
  144.8 1.8 %copy-start.15 = (f32[4,128,512]{2,1,0:T(8,128)S(1)}, f32[4,128,512]{2,1,0:T(8,128)}, u32[]{:S(2)}) copy-start(f32[4,128,512]{2,1,0:T(8,128)} %fusion.4) | copy-start | bytes 3145732
  148.4 1.0 copy-start.7
  148.5 1.2 copy-start.9
  148.5 1.3 copy-start.10
  148.5 1.5 copy-start.11
  151.7 11.6 %all-to-all-start.2 = ((f32[32,1,832]{2,1,0:T(1,128)}), f32[32,1,832]{2,1,0:T(1,128)S(1)}, u32[]{:S(2)}, u32[]{:S(2)}) async-start(f32[32,1,832]{2,1,0:T(1,128)} %reshape.184), calls=%async_computation.2 | async-start | bytes 229376 | tf_op jit(solution)/shard_map/all_to_all | solution.py:131
Sparse Core Ops, SparseCore 0:
  24.6 23.9 all-gather.1

commit v11 on v10

--- a/solution.py
+++ b/solution.py
@@ -2,6 +2,8 @@
 import jax.numpy as jnp
 from jax import lax
 from jax.sharding import PartitionSpec as P
+from jax.experimental import pallas as pl
+from jax.experimental.pallas import tpu as pltpu
 
 VARS_GENE = 4
 NEED = 2
@@ -22,6 +24,54 @@
         parts, tiles, (((2,), (2,)), ((0,), (0,))), preferred_element_type=jnp.float32
     )
     return prod[:, :cols] + prod[:, cols:]
+
+
+def far_kernel(pos_ref, rows_ref, nlive_ref, a_ref, t_ref, o_ref):
+    s = pl.program_id(0)
+
+    @pl.when(s == 0)
+    def _():
+        o_ref[...] = jnp.zeros_like(o_ref)
+
+    @pl.when(s < nlive_ref[0])
+    def _():
+        x = a_ref[0]
+        hi = x.astype(jnp.bfloat16)
+        lo = (x - hi.astype(jnp.float32)).astype(jnp.bfloat16)
+        tile = t_ref[0]
+        dims = (((1,), (1,)), ((), ()))
+        prod = lax.dot_general(hi, tile, dims, preferred_element_type=jnp.float32)
+        prod = prod + lax.dot_general(lo, tile, dims, preferred_element_type=jnp.float32)
+        r = rows_ref[s]
+        o_ref[r] = o_ref[r] + prod
+
+
+def far_product(arrived, tiles, pos, rows, nlive, width, row_tiles):
+    off_count = pos.shape[0]
+    tile_size = tiles.shape[1]
+    grid_spec = pltpu.PrefetchScalarGridSpec(
+        num_scalar_prefetch=3,
+        grid=(off_count,),
+        in_specs=[
+            pl.BlockSpec((1, width, tile_size),
+                         lambda s, p, r, n: (p[s] // NEED, p[s] % NEED, 0)),
+            pl.BlockSpec((1, tile_size, tile_size), lambda s, p, r, n: (row_tiles + s, 0, 0)),
+        ],
+        out_specs=pl.BlockSpec((row_tiles, width, tile_size), lambda s, p, r, n: (0, 0, 0)),
+    )
+    cost = pl.CostEstimate(
+        flops=off_count * 4 * width * tile_size * tile_size,
+        transcendentals=0,
+        bytes_accessed=off_count * (tile_size * tile_size * 2 + width * tile_size * 4)
+        + row_tiles * width * tile_size * 4,
+    )
+    return pl.pallas_call(
+        far_kernel,
+        grid_spec=grid_spec,
+        out_shape=jax.ShapeDtypeStruct((row_tiles, width, tile_size), jnp.float32),
+        compiler_params=pltpu.CompilerParams(dimension_semantics=("arbitrary",)),
+        cost_estimate=cost,
+    )(pos, rows, nlive, arrived, tiles)
 
 
 def local(genotypes, variance_comp, grm_tiles, tile_rows, tile_cols, tile_live):
@@ -53,6 +103,8 @@
     weight = weight * live_mask[:, None]
     position = off_cols // row_tiles * NEED + (off_cols % row_tiles - me) % row_tiles
     position = jnp.clip(position, 0, peers * NEED - 1)
+    rows_safe = jnp.clip(off_rows, 0, row_tiles - 1)
+    nlive = jnp.reshape(live - row_tiles, (1,))
 
     def to_tiles(x):
         return jnp.transpose(x.reshape(cols_here, row_tiles, tile_size), (1, 0, 2))
@@ -77,17 +129,13 @@
             side = jnp.broadcast_to(flat.reshape(1, PAD_ROWS, tile_size), (peers, PAD_ROWS, tile_size))
             pieces = jnp.concatenate([pieces, side], axis=1)
         arrived = lax.all_to_all(pieces, "ind", split_axis=0, concat_axis=0, tiled=True)
-        tiles_in = arrived[:, :NEED * width].reshape(peers * NEED, width, tile_size)
         sums = jnp.sum(arrived[:, NEED * width:].reshape(peers, -1)[:, :extra.size], axis=0)
-        return tiles_in, sums.reshape(extra.shape)
+        return arrived, sums.reshape(extra.shape)
 
     def kprod(x, arrived):
-        width = x.shape[1]
-        picked = jnp.stack([lax.dynamic_index_in_dim(arrived, position[s], 0, keepdims=False)
-                            for s in range(off_count)])
         near = batched_tile_dot(x, grm_tiles[:row_tiles])
-        far = batched_tile_dot(picked, grm_tiles[row_tiles:])
-        return near + jnp.sum(weight[:, :, None, None] * far[:, None], axis=0)
+        far = far_product(arrived, grm_tiles, position, rows_safe, nlive, x.shape[1], row_tiles)
+        return near + far
 
     def colsum(x):
         return jnp.sum(x, axis=(0, 2))

time: 175 us -> 183 us (1.046)
  Pallas kernels: 0 us -> 12 us
  between operations: 26.7 us -> 15.2 us
  waiting for transfers between devices: 76.9 us -> 88.1 us
  matrix products: 12.9 us -> 6.88 us
  other arithmetic: 16.2 us -> 21 us
  local copies, waits for them, and re-layouts: 25.4 us -> 22.7 us
    pallas_call x0 -> x2, Pallas kernels: none -> 12 us  [far_product(): pl.pallas_call(far_kernel, grid_spec=grid_spec, out_shape=jax.ShapeDtypeS...]
    all_gather x1, waiting for transfers between devices: 8.36 us -> 19.8 us  [local(): geno_all = lax.all_gather(genotypes, 'var', axis=0, tiled=True)]
    dot_general x4 -> x2, matrix products: 12.9 us -> 6.88 us  [batched_tile_dot(): lax.dot_general(parts, tiles, (((2,), (2,)), ((0,), (0,))), preferred_ele...]
    slice x4 -> x0, local copies, waits for them, and re-layouts: 2.76 us -> none  [the longest x2 2.03 us: exchange(): tiles_in = arrived[:, :NEED * width].reshape(peers * NEED, width, tile_size)]
    add x1, other arithmetic: 1.78 us -> 3.86 us  [chunk(): az1 = tau0 * z1 + tau1 * kz1]
    convert_element_type x5 -> x3, other arithmetic: 2.81 us -> 4.81 us  [split2(): return (hi.astype(jnp.bfloat16), lo.astype(jnp.bfloat16))]
    unnamed x75 -> x63, local copies, waits for them, and re-layouts: 7.69 us -> 7.05 us
where the time goes in v11:
time: 183 us; the launch traced here: 181 us
  waiting for transfers between devices  88.1 us (48%)
  local copies, waits for them, and re-layouts  22.7 us (12%)
  other arithmetic  21 us (11%)
  starting transfers between devices  15.4 us (8%)
  between operations  15.2 us (8%)
  Pallas kernels  12 us (7%)
  matrix products  6.88 us (4%)
    all_to_all x2, waiting for transfers between devices, exchange(): lax.all_to_all(pieces, 'ind', split_axis=0, concat_axis=0, tiled=True)  59.7 us
    all_gather x1, waiting for transfers between devices, local(): geno_all = lax.all_gather(genotypes, 'var', axis=0, tiled=True)  19.8 us
    pallas_call x2, Pallas kernels, far_product(): pl.pallas_call(far_kernel, grid_spec=grid_spec, out_shape=jax.ShapeDtypeS...  12 us
    all_to_all x2, starting transfers between devices, exchange(): lax.all_to_all(pieces, 'ind', split_axis=0, concat_axis=0, tiled=True)  11.4 us
    all_to_all x1, waiting for transfers between devices, chunk(): lax.all_to_all(spread, ('ind', 'var'), split_axis=0, concat_axis=0, tiled...  7.98 us
    unnamed x63, local copies, waits for them, and re-layouts  7.05 us
    dot_general x2, matrix products, batched_tile_dot(): lax.dot_general(parts, tiles, (((2,), (2,)), ((0,), (0,))), preferred_ele...  6.88 us
    reshape x4, local copies, waits for them, and re-layouts, to_tiles(): return jnp.transpose(x.reshape(cols_here, row_tiles, tile_size), (1, 0, 2))  6.53 us
  transfers between devices with their start and end apart: 4, of which 4 were waited for; matrix products, arithmetic and copies ran while one was open for 12% of the time, Pallas kernels for 0%

profile of v11, /device:TPU:0, one launch (start us, length us, event | category | flops | bytes accessed | tf_op | source)
XLA Modules:
  0.0 181.5 jit_solution(13249557112680000794)
XLA Ops:
  7.3 1.4 fusion.52
  8.6 2.4 %select_reduce_fusion = f32[4,512]{1,0:T(4,128)S(1)} fusion(pred[512,512]{1,0:T(8,128)(4,1)S(1)} %iota_compare_fusion, bf16[10,512,512]{2,1,0:T(8,128)(2,1)} %t_ref.3), kind=kLoop, calls=%fused_computation | loop fusion | flops 3143680 | bytes 2367488 | tf_op jit(solution)/shard_map/reduce_sum | solution.py:95
  14.1 1.6 pad_maximum_fusion
  15.8 7.4 %all-to-all-start = ((f32[8,136,512]{2,1,0:T(8,128)}), f32[8,136,512]{2,1,0:T(8,128)S(1)}, u32[]{:S(2)}, u32[]{:S(2)}) async-start(f32[8,136,512]{2,1,0:T(8,128)} %pad_maximum_fusion), calls=%async_computation | async-start | bytes 4456448 | tf_op jit(solution)/shard_map/all_to_all | solution.py:131
  26.4 3.4 %fusion.2 = f32[4,128,512]{2,1,0:T(8,128)} fusion(bf16[10,512,512]{2,1,0:T(8,128)(2,1)} %t_ref.3, bf16[4,64,512]{2,1,0:T(8,128)(2,1)S(1)} %copy-done.14, bf16[4,64,512]{2,1,0:T(8,128)(2,1)S(1)} %copy-done.13), kind=kOutput, calls=%fused_computation.7 | convolution fusion | flops 269484032 | bytes 3670016 | tf_op jit(solution)/shard_map/dot_general | solution.py:23
  29.8 19.8 %all-gather.2.cloned.1.call-done = f32[256,2048]{1,0:T(8,128)} async-done(((f32[64,2048]{1,0:T(8,128)}), f32[256,2048]{1,0:T(8,128)}) %all-gather.2.cloned.1.call-update) | async-done | bytes 2097168 | tf_op jit(solution)/shard_map/all_gather | solution.py:143
  49.6 2.7 %constant_dynamic-slice_fusion.6 = (f32[64,2048]{1,0:T(8,128)S(1)}, f32[64,2048]{1,0:T(8,128)}, f32[64,2048]{1,0:T(8,128)}, f32[64,2048]{1,0:T(8,128)}) fusion(f32[256,2048]{1,0:T(8,128)} %all-gather.2.cloned.1.call-done, s32[]{:T(128)S(6)} %select_n.57, s32[]{:T(128)S(6)} %select_n.60, s32[]{:T(128)S(6)} %select_n.59, s32[]{:T(128)S(6)} %select_n.58), kind=kLoop, calls=%fused_computation.96 | loop fusion | bytes 4194320 | tf_op jit(solution)/shard_map/dynamic_slice | solution.py:148
  52.7 1.6 reshape.121
  54.3 2.4 %reshape.120 = f32[64,4,512]{2,1,0:T(4,128)} reshape(f32[64,2048]{1,0:T(8,128)} %get-tuple-element.16) | data formatting | bytes 1048576 | tf_op jit(solution)/shard_map/reshape | solution.py:110
  56.7 2.2 %reshape.119 = f32[64,4,512]{2,1,0:T(4,128)} reshape(f32[64,2048]{1,0:T(8,128)} %get-tuple-element.17) | data formatting | bytes 1048576 | tf_op jit(solution)/shard_map/reshape | solution.py:110
  58.9 2.2 %multiply_reduce_fusion.1 = f32[4,64]{1,0:T(4,128)S(1)} fusion(f32[4,64,512]{2,0,1:T(4,128)} %copy.37, f32[1,4,64,512]{3,1,2,0:T(4,128)S(1)} %bitcast.177, f32[1,4,64,512]{3,1,2,0:T(4,128)} %bitcast.179, f32[1,4,64,512]{3,1,2,0:T(4,128)} %bitcast.181, f32[1,4,64,512]{3,1,2,0:T(4,128)S(1)} %bitcast.175), kind=kLoop, calls=%fused_computation.4 | loop fusion | flops 2621184 | bytes 2622464 | tf_op jit(solution)/shard_map/reduce_sum | solution.py:159
  61.1 13.1 %all-to-all-done.a_ref = f32[8,136,512]{2,1,0:T(8,128)S(1)} async-done(((f32[8,136,512]{2,1,0:T(8,128)}), f32[8,136,512]{2,1,0:T(8,128)S(1)}, u32[]{:S(2)}, u32[]{:S(2)}) %all-to-all-start) | async-done | bytes 2228256 | tf_op jit(solution)/shard_map/all_to_all | solution.py:131
  74.2 1.4 copy-done.2
  75.6 6.1 %shard_map.77 = f32[4,64,512]{2,1,0:T(8,128)} custom-call(s32[6]{0:T(128)} %get-tuple-element.35.pos_ref, s32[6]{0:T(128)} %get-tuple-element.34.rows_ref, s32[1]{0:T(128)S(6)} %sub.33.nlive_ref, f32[8,136,512]{2,1,0:T(8,128)} %copy-done.2, bf16[10,512,512]{2,1,0:T(8,128)(2,1)} %t_ref.3), custom_call_target="tpu_custom_call" | custom-call | flops 402653184 | bytes 4456448 | tf_op jit(solution)/shard_map/pallas_call | solution.py:68
  81.7 3.6 %reduce-precision_convert_fusion = (bf16[4,64,512]{2,1,0:T(8,128)(2,1)}, f32[4,64,512]{2,1,0:T(8,128)S(1)}, f32[4,64,512]{2,1,0:T(8,128)S(1)}) fusion(f32[4,512]{1,0:T(4,128)S(1)} %multiply_add_fusion.1, f32[4,64,512]{2,1,0:T(8,128)} %shard_map.77, f32[4,128,512]{2,1,0:T(8,128)} %fusion.2, f32[]{:T(128)} %bitcast.2, f32[8,4,8,512]{3,2,1,0:T(8,128)S(1)} %bitcast.169, ...), kind=kLoop, calls=%fused_computation.12 | loop fusion | flops 1179648 | bytes 3416072 | tf_op jit(solution)/shard_map/convert_element_type | solution.py:17
  86.9 1.4 copy-done.12
  88.2 3.9 %all-to-all-start.1 = ((f32[8,136,512]{2,1,0:T(8,128)}), f32[8,136,512]{2,1,0:T(8,128)S(1)}, u32[]{:S(2)}, u32[]{:S(2)}) async-start(f32[8,136,512]{2,1,0:T(8,128)} %bitcast.184), calls=%async_computation.1 | async-start | bytes 4456448 | tf_op jit(solution)/shard_map/all_to_all | solution.py:131
  93.3 3.5 %fusion = f32[4,128,512]{2,1,0:T(8,128)} fusion(bf16[10,512,512]{2,1,0:T(8,128)(2,1)} %t_ref.3, bf16[4,64,512]{2,1,0:T(8,128)(2,1)S(1)} %fusion.5, bf16[4,64,512]{2,1,0:T(8,128)(2,1)} %get-tuple-element.11), kind=kOutput, calls=%fused_computation.5 | convolution fusion | flops 269484032 | bytes 3670016 | tf_op jit(solution)/shard_map/dot_general | solution.py:23
  96.8 46.6 %all-to-all-done.1.a_ref = f32[8,136,512]{2,1,0:T(8,128)S(1)} async-done(((f32[8,136,512]{2,1,0:T(8,128)}), f32[8,136,512]{2,1,0:T(8,128)S(1)}, u32[]{:S(2)}, u32[]{:S(2)}) %all-to-all-start.1) | async-done | bytes 2228256 | tf_op jit(solution)/shard_map/all_to_all | solution.py:131
  144.8 6.0 %shard_map.78 = f32[4,64,512]{2,1,0:T(8,128)} custom-call(s32[6]{0:T(128)} %get-tuple-element.35.pos_ref, s32[6]{0:T(128)} %get-tuple-element.34.rows_ref, s32[1]{0:T(128)S(6)} %sub.33.nlive_ref, f32[8,136,512]{2,1,0:T(8,128)} %copy-done.3, bf16[10,512,512]{2,1,0:T(8,128)(2,1)} %t_ref.3), custom_call_target="tpu_custom_call" | custom-call | flops 402653184 | bytes 4456448 | tf_op jit(solution)/shard_map/pallas_call | solution.py:68
  150.8 3.9 %fusion.14 = (f32[4,64,512]{2,1,0:T(8,128)S(1)}, f32[4,64,512]{2,1,0:T(8,128)S(1)}) fusion(f32[4,64,512]{2,1,0:T(8,128)} %shard_map.78, f32[4,128,512]{2,1,0:T(8,128)} %fusion, f32[64]{0:T(128)S(1)} %get-tuple-element.30, f32[]{:T(128)} %bitcast.2, f32[]{:T(128)} %bitcast.1, f32[4,64,512]{2,1,0:T(8,128)} %shard_map.77, f32[4,128,512]{2,1,0:T(8,128)} %fusion.2, ...), kind=kLoop, calls=%fused_computation.27 | loop fusion | flops 1572864 | bytes 5251336 | tf_op jit(solution)/shard_map/add | solution.py:169
  156.3 1.9 %multiply_reduce_fusion = f32[4,64]{1,0:T(4,128)S(1)} fusion(f32[4,64,512]{2,0,1:T(4,128)} %copy.38, f32[1,4,64,512]{3,1,2,0:T(4,128)S(1)} %bitcast.178, f32[1,4,64,512]{3,1,2,0:T(4,128)S(1)} %bitcast.180, f32[1,4,64,512]{3,1,2,0:T(4,128)S(1)} %bitcast.182, f32[1,4,64,512]{3,1,2,0:T(4,128)S(1)} %bitcast.176), kind=kLoop, calls=%fused_computation.3 | loop fusion | flops 2621184 | bytes 2622464 | tf_op jit(solution)/shard_map/reduce_sum | solution.py:172
  159.1 4.0 %all-to-all-start.2 = ((f32[32,1,832]{2,1,0:T(1,128)}), f32[32,1,832]{2,1,0:T(1,128)S(1)}, u32[]{:S(2)}, u32[]{:S(2)}) async-start(f32[32,1,832]{2,1,0:T(1,128)} %reshape.136), calls=%async_computation.2 | async-start | bytes 229376 | tf_op jit(solution)/shard_map/all_to_all | solution.py:179
  163.2 8.0 %all-to-all-done.2 = f32[32,1,832]{2,1,0:T(1,128)S(1)} async-done(((f32[32,1,832]{2,1,0:T(1,128)}), f32[32,1,832]{2,1,0:T(1,128)S(1)}, u32[]{:S(2)}, u32[]{:S(2)}) %all-to-all-start.2) | async-done | bytes 106528 | tf_op jit(solution)/shard_map/all_to_all | solution.py:179
  (108 shorter events, 15.7 us)
Async XLA Ops:
  7.2 5.2 %copy-start = (f32[64,2048]{1,0:T(8,128)S(1)}, f32[64,2048]{1,0:T(8,128)}, u32[]{:S(2)}) copy-start(f32[64,2048]{1,0:T(8,128)} %param.6) | copy-start | bytes 1572868
  15.7 10.0 %copy-start.15 = (s32[10]{0:T(128)S(1)}, s32[10]{0:T(128)}, u32[]{:S(2)}) copy-start(s32[10]{0:T(128)} %param.9) | copy-start | bytes 124
  15.7 10.0 %copy-start.16 = (s32[10]{0:T(128)S(1)}, s32[10]{0:T(128)}, u32[]{:S(2)}) copy-start(s32[10]{0:T(128)} %param.10) | copy-start | bytes 124
  15.8 10.7 %copy-start.13 = (bf16[4,64,512]{2,1,0:T(8,128)(2,1)S(1)}, bf16[4,64,512]{2,1,0:T(8,128)(2,1)}, u32[]{:S(2)}) copy-start(bf16[4,64,512]{2,1,0:T(8,128)(2,1)} %get-tuple-element.18) | copy-start | bytes 786436
  15.8 10.7 %copy-start.14 = (bf16[4,64,512]{2,1,0:T(8,128)(2,1)S(1)}, bf16[4,64,512]{2,1,0:T(8,128)(2,1)}, u32[]{:S(2)}) copy-start(bf16[4,64,512]{2,1,0:T(8,128)(2,1)} %get-tuple-element.21) | copy-start | bytes 786436
  15.8 58.5 %all-to-all-start = ((f32[8,136,512]{2,1,0:T(8,128)}), f32[8,136,512]{2,1,0:T(8,128)S(1)}, u32[]{:S(2)}, u32[]{:S(2)}) async-start(f32[8,136,512]{2,1,0:T(8,128)} %pad_maximum_fusion), calls=%async_computation | async-start | bytes 4456448 | tf_op jit(solution)/shard_map/all_to_all | solution.py:131
  23.2 26.4 %all-gather.2.cloned.1.call-start = ((), (), s32[]{:S(2)}) async-start(), calls=%async_computation.3 | async-start | bytes 2621440 | tf_op jit(solution)/shard_map/all_gather | solution.py:143
  52.7 8.5 %copy-start.6 = (f32[64,4,512]{2,1,0:T(4,128)}, f32[64,4,512]{2,1,0:T(4,128)S(1)}, u32[]{:S(2)}) copy-start(f32[64,4,512]{2,1,0:T(4,128)S(1)} %reshape.118) | copy-start | bytes 1572868
  54.3 6.9 %copy-start.8 = (f32[64,4,512]{2,1,0:T(4,128)}, f32[64,4,512]{2,1,0:T(4,128)S(1)}, u32[]{:S(2)}) copy-start(f32[64,4,512]{2,1,0:T(4,128)S(1)} %reshape.121) | copy-start | bytes 1572868
  74.2 1.4 copy-start.2
  75.6 6.1 %copy-start.1 = (f32[64,2048]{1,0:T(8,128)S(1)}, f32[64,2048]{1,0:T(8,128)}, u32[]{:S(2)}) copy-start(f32[64,2048]{1,0:T(8,128)} %param.6) | copy-start | bytes 1572868
  85.4 0.8 copy-start.4
  86.9 1.4 copy-start.12
  88.2 55.2 %all-to-all-start.1 = ((f32[8,136,512]{2,1,0:T(8,128)}), f32[8,136,512]{2,1,0:T(8,128)S(1)}, u32[]{:S(2)}, u32[]{:S(2)}) async-start(f32[8,136,512]{2,1,0:T(8,128)} %bitcast.184), calls=%async_computation.1 | async-start | bytes 4456448 | tf_op jit(solution)/shard_map/all_to_all | solution.py:131
  143.4 1.4 copy-start.3
  150.8 5.0 %copy-start.5 = (f32[4,64,512]{2,1,0:T(8,128)S(1)}, f32[4,64,512]{2,1,0:T(8,128)}, u32[]{:S(2)}) copy-start(f32[4,64,512]{2,1,0:T(8,128)} %copy-done.4) | copy-start | bytes 1572868
  154.6 1.7 copy-start.7
  154.6 1.7 copy-start.9
  154.6 1.7 copy-start.10
  154.6 1.7 copy-start.11
  159.1 12.0 %all-to-all-start.2 = ((f32[32,1,832]{2,1,0:T(1,128)}), f32[32,1,832]{2,1,0:T(1,128)S(1)}, u32[]{:S(2)}, u32[]{:S(2)}) async-start(f32[32,1,832]{2,1,0:T(1,128)} %reshape.136), calls=%async_computation.2 | async-start | bytes 229376 | tf_op jit(solution)/shard_map/all_to_all | solution.py:179
Sparse Core Ops, SparseCore 0:
  25.5 23.9 all-gather.1

commit v12 on v10

--- a/solution.py
+++ b/solution.py
@@ -41,10 +41,14 @@
     tau1 = variance_comp[1]
     live = tile_live[0]
 
-    eye = jnp.arange(tile_size)[:, None] == jnp.arange(tile_size)[None, :]
+    lane = 128
+    nblk = tile_size // lane
+    split_tiles = grm_tiles[:row_tiles].reshape(row_tiles, nblk, lane, nblk, lane)
+    diag_blocks = jnp.stack([split_tiles[:, b, :, b, :] for b in range(nblk)], axis=1)
+    eye = jnp.arange(lane)[:, None] == jnp.arange(lane)[None, :]
     diag_values = jnp.sum(
-        jnp.where(eye[None], grm_tiles[:row_tiles].astype(jnp.float32), 0.0), axis=2
-    )
+        jnp.where(eye[None, None], diag_blocks.astype(jnp.float32), 0.0), axis=2
+    ).reshape(row_tiles, tile_size)
     precond = (tau0 + tau1 * diag_values)[:, None, :]
     off_rows = tile_rows[row_tiles:]
     off_cols = tile_cols[row_tiles:]
@@ -77,14 +81,17 @@
             side = jnp.broadcast_to(flat.reshape(1, PAD_ROWS, tile_size), (peers, PAD_ROWS, tile_size))
             pieces = jnp.concatenate([pieces, side], axis=1)
         arrived = lax.all_to_all(pieces, "ind", split_axis=0, concat_axis=0, tiled=True)
-        tiles_in = arrived[:, :NEED * width].reshape(peers * NEED, width, tile_size)
         sums = jnp.sum(arrived[:, NEED * width:].reshape(peers, -1)[:, :extra.size], axis=0)
-        return tiles_in, sums.reshape(extra.shape)
+        return arrived, sums.reshape(extra.shape)
 
     def kprod(x, arrived):
         width = x.shape[1]
-        picked = jnp.stack([lax.dynamic_index_in_dim(arrived, position[s], 0, keepdims=False)
-                            for s in range(off_count)])
+        sub = 8
+        view = arrived.reshape(peers, arrived.shape[1] // sub, sub, tile_size)
+        picked = jnp.stack([
+            lax.dynamic_slice(view, (position[s] // NEED, position[s] % NEED * (width // sub), 0, 0),
+                              (1, width // sub, sub, tile_size)).reshape(width, tile_size)
+            for s in range(off_count)])
         near = batched_tile_dot(x, grm_tiles[:row_tiles])
         far = batched_tile_dot(picked, grm_tiles[row_tiles:])
         return near + jnp.sum(weight[:, :, None, None] * far[:, None], axis=0)

time: 175 us -> 184 us (1.051)
  local copies, waits for them, and re-layouts: 25.4 us -> 31.7 us
  other arithmetic: 16.2 us -> 11.5 us
  between operations: 26.7 us -> 30.6 us
  waiting for transfers between devices: 76.9 us -> 80.6 us
    unnamed x75 -> x63, local copies, waits for them, and re-layouts: 7.69 us -> 16.2 us
    all_to_all x2, waiting for transfers between devices: 59.9 us -> 66.7 us  [exchange(): lax.all_to_all(pieces, 'ind', split_axis=0, concat_axis=0, tiled=True)]
    reshape x4, local copies, waits for them, and re-layouts: 6.53 us -> 1.4 us  [to_tiles(): return jnp.transpose(x.reshape(cols_here, row_tiles, tile_size), (1, 0, 2))]
    all_gather x1, waiting for transfers between devices: 8.36 us -> 5.23 us  [local(): geno_all = lax.all_gather(genotypes, 'var', axis=0, tiled=True)]
    reduce_sum x1, other arithmetic: 2.42 us -> 0.13 us  [local(): jnp.sum(jnp.where(eye[None, None], diag_blocks.astype(jnp.float32), 0.0),...]
    reshape x0 -> x1, local copies, waits for them, and re-layouts: none -> 2.07 us  [local(): grm_tiles[:row_tiles].reshape(row_tiles, nblk, lane, nblk, lane)]
    another operation x2 -> x4, local copies, waits for them, and re-layouts: 0.04 us -> 1.92 us  [the longest x2 1.84 us: kprod(): jnp.stack([lax.dynamic_slice(view, (position[s] // NEED, position[s] % NE...]
  transfers between devices with their start and end apart: 4 -> 4, of which waited for: 4 -> 4; matrix products, arithmetic and copies ran while one was open for 12% -> 7% of each run, Pallas kernels for 0% -> 0%
where the time goes in v12:
time: 184 us; the launch traced here: 183 us
  waiting for transfers between devices  80.6 us (44%)
  local copies, waits for them, and re-layouts  31.7 us (17%)
  between operations  30.6 us (17%)
  starting transfers between devices  15.6 us (8%)
  matrix products  12.8 us (7%)
  other arithmetic  11.5 us (6%)
    all_to_all x2, waiting for transfers between devices, exchange(): lax.all_to_all(pieces, 'ind', split_axis=0, concat_axis=0, tiled=True)  66.7 us
    unnamed x63, local copies, waits for them, and re-layouts  16.2 us
    dot_general x4, matrix products, batched_tile_dot(): lax.dot_general(parts, tiles, (((2,), (2,)), ((0,), (0,))), preferred_ele...  12.8 us
    all_to_all x2, starting transfers between devices, exchange(): lax.all_to_all(pieces, 'ind', split_axis=0, concat_axis=0, tiled=True)  11.9 us
    all_to_all x1, waiting for transfers between devices, chunk(): lax.all_to_all(spread, ('ind', 'var'), split_axis=0, concat_axis=0, tiled...  7.98 us
    all_gather x1, waiting for transfers between devices, local(): geno_all = lax.all_gather(genotypes, 'var', axis=0, tiled=True)  5.23 us
  transfers between devices with their start and end apart: 4, of which 4 were waited for; matrix products, arithmetic and copies ran while one was open for 7% of the time, Pallas kernels for 0%

profile of v12, /device:TPU:0, one launch (start us, length us, event | category | flops | bytes accessed | tf_op | source)
XLA Modules:
  0.0 182.9 jit_solution(2913809776141886913)
XLA Ops:
  7.2 1.4 fusion.69
  8.8 2.1 %reshape.173 = bf16[4,4,128,4,128]{4,3,2,1,0:T(4,128)(2,1)} reshape(bf16[4,512,512]{2,1,0:T(8,128)(2,1)S(1)} %slice-done) | data formatting | bytes 4194304 | tf_op jit(solution)/shard_map/reshape | solution.py:46
  10.9 2.7 %fusion.67 = (bf16[4,1,128,1,128]{4,3,2,1,0:T(2,128)(2,1)S(1)}, bf16[4,1,128,1,128]{4,3,2,1,0:T(2,128)(2,1)S(1)}, bf16[4,1,128,1,128]{4,3,2,1,0:T(2,128)(2,1)S(1)}, bf16[4,1,128,1,128]{4,3,2,1,0:T(2,128)(2,1)S(1)}) fusion(bf16[4,4,128,4,128]{4,3,2,1,0:T(4,128)(2,1)} %reshape.173), kind=kLoop, calls=%fused_computation.158 | loop fusion | bytes 1048576 | tf_op jit(solution)/shard_map/slice | solution.py:47
  13.8 1.2 add_bitcast_fusion.1
  15.9 1.6 pad_maximum_fusion
  17.5 7.4 %all-to-all-start = ((f32[8,136,512]{2,1,0:T(8,128)}), f32[8,136,512]{2,1,0:T(8,128)}, u32[]{:S(2)}, u32[]{:S(2)}) async-start(f32[8,136,512]{2,1,0:T(8,128)} %pad_maximum_fusion), calls=%async_computation | async-start | bytes 4456448 | tf_op jit(solution)/shard_map/all_to_all | solution.py:83
  42.8 3.4 %fusion.24 = f32[4,128,512]{2,1,0:T(8,128)} fusion(bf16[4,64,512]{2,1,0:T(8,128)(2,1)S(1)} %get-tuple-element.29, bf16[4,64,512]{2,1,0:T(8,128)(2,1)S(1)} %get-tuple-element.26, bf16[10,512,512]{2,1,0:T(8,128)(2,1)} %param.8), kind=kOutput, calls=%fused_computation.46 | convolution fusion | flops 269484032 | bytes 3670016 | tf_op jit(solution)/shard_map/dot_general | solution.py:21
  46.1 5.2 %all-gather.2.cloned.1.call-done = f32[256,2048]{1,0:T(8,128)} async-done(((f32[64,2048]{1,0:T(8,128)}), f32[256,2048]{1,0:T(8,128)}) %all-gather.2.cloned.1.call-update) | async-done | bytes 2097168 | tf_op jit(solution)/shard_map/all_gather | solution.py:102
  51.4 1.7 constant_dynamic-slice_fusion.6
  55.4 20.7 %all-to-all-done = f32[8,136,512]{2,1,0:T(8,128)} async-done(((f32[8,136,512]{2,1,0:T(8,128)}), f32[8,136,512]{2,1,0:T(8,128)}, u32[]{:S(2)}, u32[]{:S(2)}) %all-to-all-start) | async-done | bytes 2228256 | tf_op jit(solution)/shard_map/all_to_all | solution.py:83
  77.9 0.9 bitcast_dynamic-update-slice_fusion.9
  78.9 0.9 bitcast_dynamic-update-slice_fusion.8
  81.8 3.0 %fusion.2 = f32[6,128,512]{2,1,0:T(8,128)S(1)} fusion(bf16[10,512,512]{2,1,0:T(8,128)(2,1)} %param.8, bf16[6,64,512]{2,1,0:T(8,128)(2,1)S(1)} %get-tuple-element.25, bf16[6,64,512]{2,1,0:T(8,128)(2,1)S(1)} %get-tuple-element.24), kind=kOutput, calls=%fused_computation.4 | convolution fusion | flops 404226048 | bytes 5505024 | tf_op jit(solution)/shard_map/dot_general | solution.py:21
  86.2 1.5 reduce-precision_convert_fusion.2
  88.4 1.4 copy-done.8
  89.8 4.5 %all-to-all-start.1 = ((f32[8,136,512]{2,1,0:T(8,128)}), f32[8,136,512]{2,1,0:T(8,128)}, u32[]{:S(2)}, u32[]{:S(2)}) async-start(f32[8,136,512]{2,1,0:T(8,128)} %bitcast.228), calls=%async_computation.1 | async-start | bytes 4456448 | tf_op jit(solution)/shard_map/all_to_all | solution.py:83
  95.4 3.4 %fusion.28 = f32[4,128,512]{2,1,0:T(8,128)} fusion(bf16[4,64,512]{2,1,0:T(8,128)(2,1)S(1)} %fusion.13, bf16[4,64,512]{2,1,0:T(8,128)(2,1)S(1)} %get-tuple-element.11, bf16[10,512,512]{2,1,0:T(8,128)(2,1)} %param.8), kind=kOutput, calls=%fused_computation.50 | convolution fusion | flops 269484032 | bytes 3670016 | tf_op jit(solution)/shard_map/dot_general | solution.py:21
  98.8 46.0 %all-to-all-done.1 = f32[8,136,512]{2,1,0:T(8,128)} async-done(((f32[8,136,512]{2,1,0:T(8,128)}), f32[8,136,512]{2,1,0:T(8,128)}, u32[]{:S(2)}, u32[]{:S(2)}) %all-to-all-start.1) | async-done | bytes 2228256 | tf_op jit(solution)/shard_map/all_to_all | solution.py:83
  148.8 0.9 bitcast_dynamic-update-slice_fusion.2
  149.7 0.9 bitcast_dynamic-update-slice_fusion.1
  151.7 3.0 %fusion = f32[6,128,512]{2,1,0:T(8,128)S(1)} fusion(bf16[10,512,512]{2,1,0:T(8,128)(2,1)} %param.8, bf16[6,64,512]{2,1,0:T(8,128)(2,1)S(1)} %get-tuple-element.23, bf16[6,64,512]{2,1,0:T(8,128)(2,1)S(1)} %get-tuple-element.22), kind=kOutput, calls=%fused_computation.2 | convolution fusion | flops 404226048 | bytes 5505024 | tf_op jit(solution)/shard_map/dot_general | solution.py:21
  156.2 1.7 fusion.22
  161.0 3.6 %all-to-all-start.2 = ((f32[32,1,832]{2,1,0:T(1,128)}), f32[32,1,832]{2,1,0:T(1,128)S(1)}, u32[]{:S(2)}, u32[]{:S(2)}) async-start(f32[32,1,832]{2,1,0:T(1,128)} %reshape.195), calls=%async_computation.2 | async-start | bytes 229376 | tf_op jit(solution)/shard_map/all_to_all | solution.py:138
  164.6 8.0 %all-to-all-done.2 = f32[32,1,832]{2,1,0:T(1,128)S(1)} async-done(((f32[32,1,832]{2,1,0:T(1,128)}), f32[32,1,832]{2,1,0:T(1,128)S(1)}, u32[]{:S(2)}, u32[]{:S(2)}) %all-to-all-start.2) | async-done | bytes 106528 | tf_op jit(solution)/shard_map/all_to_all | solution.py:138
  (126 shorter events, 25.1 us)
Async XLA Ops:
  7.2 1.6 slice-start
  10.9 4.2 %copy-start = (f32[64,2048]{1,0:T(8,128)S(1)}, f32[64,2048]{1,0:T(8,128)}, u32[]{:S(2)}) copy-start(f32[64,2048]{1,0:T(8,128)} %param.6) | copy-start | bytes 1572868
  17.5 8.2 %copy-start.10 = (s32[10]{0:T(128)S(1)}, s32[10]{0:T(128)}, u32[]{:S(2)}) copy-start(s32[10]{0:T(128)} %param.10) | copy-start | bytes 124
  17.5 25.1 %copy-start.11 = (s32[10]{0:T(128)S(1)}, s32[10]{0:T(128)}, u32[]{:S(2)}) copy-start(s32[10]{0:T(128)} %param.9) | copy-start | bytes 124
  17.5 58.6 %all-to-all-start = ((f32[8,136,512]{2,1,0:T(8,128)}), f32[8,136,512]{2,1,0:T(8,128)}, u32[]{:S(2)}, u32[]{:S(2)}) async-start(f32[8,136,512]{2,1,0:T(8,128)} %pad_maximum_fusion), calls=%async_computation | async-start | bytes 4456448 | tf_op jit(solution)/shard_map/all_to_all | solution.py:83
  24.9 26.4 %all-gather.2.cloned.1.call-start = ((), (), s32[]{:S(2)}) async-start(), calls=%async_computation.3 | async-start | bytes 2621440 | tf_op jit(solution)/shard_map/all_gather | solution.py:102
  54.1 24.8 %copy-start.2 = (f32[64,4,512]{2,1,0:T(4,128)}, f32[64,4,512]{2,1,0:T(4,128)S(1)}, u32[]{:S(2)}) copy-start(f32[64,4,512]{2,1,0:T(4,128)S(1)} %reshape.178) | copy-start | bytes 1572868
  54.5 27.3 %copy-start.4 = (f32[64,4,512]{2,1,0:T(4,128)}, f32[64,4,512]{2,1,0:T(4,128)S(1)}, u32[]{:S(2)}) copy-start(f32[64,4,512]{2,1,0:T(4,128)S(1)} %reshape.177) | copy-start | bytes 1572868
  84.8 1.0 copy-start.1
  84.8 1.4 copy-start.6
  88.4 1.4 copy-start.8
  89.8 55.1 %all-to-all-start.1 = ((f32[8,136,512]{2,1,0:T(8,128)}), f32[8,136,512]{2,1,0:T(8,128)}, u32[]{:S(2)}, u32[]{:S(2)}) async-start(f32[8,136,512]{2,1,0:T(8,128)} %bitcast.228), calls=%async_computation.1 | async-start | bytes 4456448 | tf_op jit(solution)/shard_map/all_to_all | solution.py:83
  154.7 1.2 copy-start.7
  154.7 1.5 copy-start.9
  158.0 1.0 copy-start.3
  158.0 1.2 copy-start.5
  161.0 11.6 %all-to-all-start.2 = ((f32[32,1,832]{2,1,0:T(1,128)}), f32[32,1,832]{2,1,0:T(1,128)S(1)}, u32[]{:S(2)}, u32[]{:S(2)}) async-start(f32[32,1,832]{2,1,0:T(1,128)} %reshape.195), calls=%async_computation.2 | async-start | bytes 229376 | tf_op jit(solution)/shard_map/all_to_all | solution.py:138
Sparse Core Ops, SparseCore 0:
  27.3 24.0 all-gather.1

commit v13 on v10

--- a/solution.py
+++ b/solution.py
@@ -119,11 +119,15 @@
         kw = kprod(w, tiles1)
         kz1 = kz0 - alpha0[None, :, None] * kw
         az1 = tau0 * z1 + tau1 * kz1
+        pw_local = jnp.sum(geno_sub * w[None], axis=(1, 3))
+        p1_local = p0_local - alpha0[None] * pw_local
         red_local = jnp.concatenate(
             [colsum(resid1 * z1)[None], colsum(z1 * az1)[None],
-             colsum(z1 * image0 + z0 * az1)[None], jnp.sum(geno_sub * z1[None], axis=(1, 3))],
+             colsum(z1 * image0 + z0 * az1)[None], p1_local],
             axis=0,
         )
+        z0_rows = from_tiles(z0)
+        z1_rows = from_tiles(z1)
         lead = (me == 0).astype(jnp.float32)
         payload = jnp.concatenate(
             [red_local, lead * rz0[None], lead * dad0[None], lead * p0], axis=0)
@@ -143,8 +147,8 @@
         mine = lambda t: lax.dynamic_index_in_dim(t, v, 0, keepdims=False)
         beta = mine(beta_all)
         alpha1 = mine(alpha1_all)
-        dir1 = z1 + beta[None, :, None] * z0
-        sol = alpha0[None, :, None] * z0 + alpha1[None, :, None] * dir1
+        dir1 = z1_rows + beta[:, None] * z0_rows
+        sol = alpha0[:, None] * z0_rows + alpha1[:, None] * dir1
         part = alpha0_all[:, None] * p0_all + alpha1_all[:, None] * (p1_all + beta_all[:, None] * p0_all)
         return sol, part
 
@@ -152,13 +156,13 @@
     width = cols_here // CHUNKS
     outs = [chunk(g_all[:, k * width:(k + 1) * width], geno_sub[:, :, k * width:(k + 1) * width])
             for k in range(CHUNKS)]
-    solution = jnp.concatenate([o[0] for o in outs], axis=1)
+    solution = jnp.concatenate([o[0] for o in outs], axis=0)
     gram_part = jnp.concatenate([o[1] for o in outs], axis=2)
     full = jnp.transpose(gram_part, (1, 0, 2)).reshape(VARS_GENE, ncol)
     gram_cols = lax.dynamic_index_in_dim(full, a_out, 0, keepdims=False)
     gram_cols = lax.dynamic_slice_in_dim(gram_cols.reshape(VARS_GENE, genes), g0, cols_here, 1)
     gene_gram = jnp.transpose(gram_cols) / total_ind
-    return (from_tiles(solution), gene_gram)
+    return (solution, gene_gram)
 
 
 def solution(mesh):

time: 175 us -> 190 us (1.086)
  local copies, waits for them, and re-layouts: 25.4 us -> 38.6 us
    unnamed x75 -> x90, local copies, waits for them, and re-layouts: 7.69 us -> 19.8 us
    all_to_all x2, waiting for transfers between devices: 59.9 us -> 62.3 us  [exchange(): lax.all_to_all(pieces, 'ind', split_axis=0, concat_axis=0, tiled=True)]
  transfers between devices with their start and end apart: 4 -> 4, of which waited for: 4 -> 4; matrix products, arithmetic and copies ran while one was open for 12% -> 10% of each run, Pallas kernels for 0% -> 0%
where the time goes in v13:
time: 190 us; the launch traced here: 189 us
  waiting for transfers between devices  77.4 us (41%)
  local copies, waits for them, and re-layouts  38.6 us (20%)
  between operations  27.1 us (14%)
  other arithmetic  17.1 us (9%)
  starting transfers between devices  15.5 us (8%)
  matrix products  12.9 us (7%)
    all_to_all x2, waiting for transfers between devices, exchange(): lax.all_to_all(pieces, 'ind', split_axis=0, concat_axis=0, tiled=True)  62.3 us
    unnamed x90, local copies, waits for them, and re-layouts  19.8 us
    dot_general x4, matrix products, batched_tile_dot(): lax.dot_general(parts, tiles, (((2,), (2,)), ((0,), (0,))), preferred_ele...  12.9 us
    all_to_all x2, starting transfers between devices, exchange(): lax.all_to_all(pieces, 'ind', split_axis=0, concat_axis=0, tiled=True)  11.8 us
    all_gather x1, waiting for transfers between devices, local(): geno_all = lax.all_gather(genotypes, 'var', axis=0, tiled=True)  7.74 us
    reshape x4, local copies, waits for them, and re-layouts, to_tiles(): return jnp.transpose(x.reshape(cols_here, row_tiles, tile_size), (1, 0, 2))  6.7 us
    all_to_all x1, waiting for transfers between devices, chunk(): lax.all_to_all(spread, ('ind', 'var'), split_axis=0, concat_axis=0, tiled...  6.69 us
  transfers between devices with their start and end apart: 4, of which 4 were waited for; matrix products, arithmetic and copies ran while one was open for 10% of the time, Pallas kernels for 0%

profile of v13, /device:TPU:0, one launch (start us, length us, event | category | flops | bytes accessed | tf_op | source)
XLA Modules:
  0.0 188.5 jit_solution(8852233411588303155)
XLA Ops:
  7.3 1.3 fusion.69
  8.6 2.4 %select_reduce_fusion = f32[4,512]{1,0:T(4,128)S(1)} fusion(pred[512,512]{1,0:T(8,128)(4,1)S(1)} %iota_compare_fusion, bf16[10,512,512]{2,1,0:T(8,128)(2,1)} %param.8), kind=kLoop, calls=%fused_computation | loop fusion | flops 3143680 | bytes 2367488 | tf_op jit(solution)/shard_map/reduce_sum | solution.py:45
  11.0 1.2 multiply_add_fusion.2
  13.1 1.6 pad_maximum_fusion
  14.7 7.4 %all-to-all-start = ((f32[8,136,512]{2,1,0:T(8,128)}), f32[8,136,512]{2,1,0:T(8,128)S(1)}, u32[]{:S(2)}, u32[]{:S(2)}) async-start(f32[8,136,512]{2,1,0:T(8,128)} %pad_maximum_fusion), calls=%async_computation | async-start | bytes 4456448 | tf_op jit(solution)/shard_map/all_to_all | solution.py:79
  31.4 1.2 copy.37
  37.3 3.4 %fusion.6 = f32[4,128,512]{2,1,0:T(8,128)} fusion(bf16[10,512,512]{2,1,0:T(8,128)(2,1)} %param.8, bf16[4,64,512]{2,1,0:T(8,128)(2,1)S(1)} %get-tuple-element.24, bf16[4,64,512]{2,1,0:T(8,128)(2,1)S(1)} %get-tuple-element.23), kind=kOutput, calls=%fused_computation.13 | convolution fusion | flops 269484032 | bytes 3670016 | tf_op jit(solution)/shard_map/dot_general | solution.py:21
  40.7 7.7 %all-gather.2.cloned.1.call-done = f32[256,2048]{1,0:T(8,128)} async-done(((f32[64,2048]{1,0:T(8,128)}), f32[256,2048]{1,0:T(8,128)}) %all-gather.2.cloned.1.call-update) | async-done | bytes 2097168 | tf_op jit(solution)/shard_map/all_gather | solution.py:95
  48.5 2.7 %constant_dynamic-slice_fusion.6 = (f32[64,2048]{1,0:T(8,128)}, f32[64,2048]{1,0:T(8,128)}, f32[64,2048]{1,0:T(8,128)S(1)}, f32[64,2048]{1,0:T(8,128)S(1)}) fusion(f32[256,2048]{1,0:T(8,128)} %all-gather.2.cloned.1.call-done, s32[]{:T(128)S(6)} %select_n.88, s32[]{:T(128)S(6)} %select_n.91, s32[]{:T(128)S(6)} %select_n.90, s32[]{:T(128)S(6)} %select_n.89), kind=kLoop, calls=%fused_computation.119 | loop fusion | bytes 4194320 | tf_op jit(solution)/shard_map/dynamic_slice | solution.py:100
  51.2 2.2 %reshape.180 = f32[64,4,512]{2,1,0:T(4,128)} reshape(f32[64,2048]{1,0:T(8,128)} %get-tuple-element.14) | data formatting | bytes 1048576 | tf_op jit(solution)/shard_map/reshape | solution.py:58
  53.3 2.2 %reshape.183 = f32[64,4,512]{2,1,0:T(4,128)} reshape(f32[64,2048]{1,0:T(8,128)} %get-tuple-element.15) | data formatting | bytes 1048576 | tf_op jit(solution)/shard_map/reshape | solution.py:58
  57.9 15.3 %all-to-all-done = f32[8,136,512]{2,1,0:T(8,128)S(1)} async-done(((f32[8,136,512]{2,1,0:T(8,128)}), f32[8,136,512]{2,1,0:T(8,128)S(1)}, u32[]{:S(2)}, u32[]{:S(2)}) %all-to-all-start) | async-done | bytes 2228256 | tf_op jit(solution)/shard_map/all_to_all | solution.py:79
  73.6 3.0 %fusion.2 = f32[6,128,512]{2,1,0:T(8,128)S(1)} fusion(bf16[10,512,512]{2,1,0:T(8,128)(2,1)} %param.8, bf16[6,64,512]{2,1,0:T(8,128)(2,1)S(1)} %get-tuple-element.22, bf16[6,64,512]{2,1,0:T(8,128)(2,1)S(1)} %get-tuple-element.21), kind=kOutput, calls=%fused_computation.5 | convolution fusion | flops 404226048 | bytes 5505024 | tf_op jit(solution)/shard_map/dot_general | solution.py:21
  78.1 1.9 %reduce-precision_convert_fusion.2 = (bf16[4,64,512]{2,1,0:T(8,128)(2,1)S(1)}, f32[4,64,512]{2,1,0:T(8,128)S(1)}, f32[4,64,512]{2,1,0:T(8,128)S(1)}) fusion(f32[4,512]{1,0:T(4,128)S(1)} %multiply_add_fusion.2, f32[4,64,512]{2,1,0:T(8,128)S(1)} %multiply_reduce_fusion.1, f32[4,128,512]{2,1,0:T(8,128)S(1)} %copy-done.6, f32[]{:T(128)} %bitcast.2, ...), kind=kLoop, calls=%fused_computation.32 | loop fusion | flops 1179648 | bytes 3416072 | tf_op jit(solution)/shard_map/convert_element_type | solution.py:15
  81.2 2.7 %multiply_reduce_fusion.2 = (f32[4,64]{1,0:T(4,128)}, f32[4,64]{1,0:T(4,128)S(1)}) fusion(f32[4,64,512]{2,0,1:T(4,128)S(1)} %copy.38, f32[1,4,64,512]{3,1,2,0:T(4,128)S(1)} %bitcast.220, f32[1,4,64,512]{3,1,2,0:T(4,128)S(1)} %bitcast.221, f32[1,4,64,512]{3,1,2,0:T(4,128)S(1)} %bitcast.222, f32[1,4,64,512]{3,1,2,0:T(4,128)S(1)} %bitcast.219, ...), kind=kLoop, calls=%fused_computation.9 | loop fusion | flops 3669504 | bytes 3147776 | tf_op jit(solution)/shard_map/reduce_sum | solution.py:122
  100.6 4.3 %all-to-all-start.1 = ((f32[8,136,512]{2,1,0:T(8,128)}), f32[8,136,512]{2,1,0:T(8,128)}, u32[]{:S(2)}, u32[]{:S(2)}) async-start(f32[8,136,512]{2,1,0:T(8,128)} %bitcast.217), calls=%async_computation.1 | async-start | bytes 4456448 | tf_op jit(solution)/shard_map/all_to_all | solution.py:79
  105.2 3.4 %fusion.4 = f32[4,128,512]{2,1,0:T(8,128)} fusion(bf16[10,512,512]{2,1,0:T(8,128)(2,1)} %param.8, bf16[4,64,512]{2,1,0:T(8,128)(2,1)S(1)} %fusion.17, bf16[4,64,512]{2,1,0:T(8,128)(2,1)S(1)} %get-tuple-element.11), kind=kOutput, calls=%fused_computation.11 | convolution fusion | flops 269484032 | bytes 3670016 | tf_op jit(solution)/shard_map/dot_general | solution.py:21
  108.6 47.0 %all-to-all-done.1 = f32[8,136,512]{2,1,0:T(8,128)} async-done(((f32[8,136,512]{2,1,0:T(8,128)}), f32[8,136,512]{2,1,0:T(8,128)}, u32[]{:S(2)}, u32[]{:S(2)}) %all-to-all-start.1) | async-done | bytes 2228256 | tf_op jit(solution)/shard_map/all_to_all | solution.py:79
  156.8 1.8 slice.214
  158.8 3.0 %fusion = f32[6,128,512]{2,1,0:T(8,128)S(1)} fusion(bf16[10,512,512]{2,1,0:T(8,128)(2,1)} %param.8, bf16[6,64,512]{2,1,0:T(8,128)(2,1)S(1)} %get-tuple-element.20, bf16[6,64,512]{2,1,0:T(8,128)(2,1)S(1)} %get-tuple-element.19), kind=kOutput, calls=%fused_computation.3 | convolution fusion | flops 404226048 | bytes 5505024 | tf_op jit(solution)/shard_map/dot_general | solution.py:21
  163.8 1.9 %add_reduce_fusion = (f32[64]{0:T(128)S(1)}, f32[64]{0:T(128)S(1)}, f32[64]{0:T(128)S(1)}, f32[4,8,8,512]{3,2,1,0:T(8,128)S(1)}) fusion(f32[4,64,512]{2,1,0:T(8,128)S(1)} %copy-done.5, f32[4,512]{1,0:T(4,128)S(1)} %copy-done.15, f32[64]{0:T(128)S(1)} %get-tuple-element.35, f32[8,4,8,512]{3,2,1,0:T(8,128)S(1)} %bitcast.202, ...), kind=kLoop, calls=%fused_computation.58 | loop fusion | flops 2752320 | bytes 4727816 | tf_op jit(solution)/shard_map/reduce_sum | solution.py:93
  166.6 3.7 %all-to-all-start.2 = ((f32[32,1,832]{2,1,0:T(1,128)}), f32[32,1,832]{2,1,0:T(1,128)S(1)}, u32[]{:S(2)}, u32[]{:S(2)}) async-start(f32[32,1,832]{2,1,0:T(1,128)} %reshape.199), calls=%async_computation.2 | async-start | bytes 229376 | tf_op jit(solution)/shard_map/all_to_all | solution.py:135
  170.3 1.2 fusion.70
  171.6 6.7 %all-to-all-done.2 = f32[32,1,832]{2,1,0:T(1,128)S(1)} async-done(((f32[32,1,832]{2,1,0:T(1,128)}), f32[32,1,832]{2,1,0:T(1,128)S(1)}, u32[]{:S(2)}, u32[]{:S(2)}) %all-to-all-start.2) | async-done | bytes 106528 | tf_op jit(solution)/shard_map/all_to_all | solution.py:135
  (148 shorter events, 32.1 us)
Async XLA Ops:
  7.2 5.1 %copy-start = (f32[64,2048]{1,0:T(8,128)S(1)}, f32[64,2048]{1,0:T(8,128)}, u32[]{:S(2)}) copy-start(f32[64,2048]{1,0:T(8,128)} %param.6) | copy-start | bytes 1572868
  11.0 1.3 copy-start.16
  12.2 68.8 %copy-start.14 = (f32[4,512]{1,0:T(4,128)}, f32[4,512]{1,0:T(4,128)S(1)}, u32[]{:S(2)}) copy-start(f32[4,512]{1,0:T(4,128)S(1)} %multiply_add_fusion.2) | copy-start | bytes 24580
  14.7 8.2 %copy-start.23 = (s32[10]{0:T(128)S(1)}, s32[10]{0:T(128)}, u32[]{:S(2)}) copy-start(s32[10]{0:T(128)} %param.10) | copy-start | bytes 124
  14.7 18.6 %copy-start.24 = (s32[10]{0:T(128)S(1)}, s32[10]{0:T(128)}, u32[]{:S(2)}) copy-start(s32[10]{0:T(128)} %param.9) | copy-start | bytes 124
  14.7 58.5 %all-to-all-start = ((f32[8,136,512]{2,1,0:T(8,128)}), f32[8,136,512]{2,1,0:T(8,128)S(1)}, u32[]{:S(2)}, u32[]{:S(2)}) async-start(f32[8,136,512]{2,1,0:T(8,128)} %pad_maximum_fusion), calls=%async_computation | async-start | bytes 4456448 | tf_op jit(solution)/shard_map/all_to_all | solution.py:79
  22.1 26.4 %all-gather.2.cloned.1.call-start = ((), (), s32[]{:S(2)}) async-start(), calls=%async_computation.3 | async-start | bytes 2621440 | tf_op jit(solution)/shard_map/all_gather | solution.py:95
  37.3 39.5 %copy-start.18 = (f32[6,4]{1,0:T(8,128)}, f32[6,4]{1,0:T(8,128)S(1)}, u32[]{:S(2)}) copy-start(f32[6,4]{1,0:T(8,128)S(1)} %fusion.53) | copy-start | bytes 292
  76.7 1.4 copy-start.6
  78.1 2.3 %copy-start.2 = (f32[4,64,512]{2,1,0:T(8,128)}, f32[4,64,512]{2,1,0:T(8,128)S(1)}, u32[]{:S(2)}) copy-start(f32[4,64,512]{2,1,0:T(8,128)S(1)} %multiply_reduce_fusion.1) | copy-start | bytes 1572868
  78.1 3.1 %copy-start.8 = (f32[4,64,512]{2,0,1:T(4,128)S(1)}, f32[4,64,512]{2,0,1:T(4,128)}, u32[]{:S(2)}) copy-start(f32[4,64,512]{2,0,1:T(4,128)} %copy.37) | copy-start | bytes 1572868
  78.1 3.1 %copy-start.9 = (f32[64,4,512]{2,1,0:T(4,128)S(1)}, f32[64,4,512]{2,1,0:T(4,128)}, u32[]{:S(2)}) copy-start(f32[64,4,512]{2,1,0:T(4,128)} %reshape.180) | copy-start | bytes 1572868
  78.1 3.1 %copy-start.10 = (f32[64,4,512]{2,1,0:T(4,128)S(1)}, f32[64,4,512]{2,1,0:T(4,128)}, u32[]{:S(2)}) copy-start(f32[64,4,512]{2,1,0:T(4,128)} %reshape.183) | copy-start | bytes 1572868
  78.1 3.1 %copy-start.11 = (f32[64,4,512]{2,1,0:T(4,128)S(1)}, f32[64,4,512]{2,1,0:T(4,128)}, u32[]{:S(2)}) copy-start(f32[64,4,512]{2,1,0:T(4,128)} %reshape.182) | copy-start | bytes 1572868
  78.1 3.1 %copy-start.12 = (f32[64,4,512]{2,1,0:T(4,128)S(1)}, f32[64,4,512]{2,1,0:T(4,128)}, u32[]{:S(2)}) copy-start(f32[64,4,512]{2,1,0:T(4,128)} %reshape.181) | copy-start | bytes 1572868
  80.0 4.0 %copy-start.4 = (f32[4,64,512]{2,1,0:T(8,128)}, f32[4,64,512]{2,1,0:T(8,128)S(1)}, u32[]{:S(2)}) copy-start(f32[4,64,512]{2,1,0:T(8,128)S(1)} %get-tuple-element.13) | copy-start | bytes 1572868
  100.6 55.0 %all-to-all-start.1 = ((f32[8,136,512]{2,1,0:T(8,128)}), f32[8,136,512]{2,1,0:T(8,128)}, u32[]{:S(2)}, u32[]{:S(2)}) async-start(f32[8,136,512]{2,1,0:T(8,128)} %bitcast.217), calls=%async_computation.1 | async-start | bytes 4456448 | tf_op jit(solution)/shard_map/all_to_all | solution.py:79
  158.8 3.3 %copy-start.19 = (f32[6,4]{1,0:T(8,128)S(1)}, f32[6,4]{1,0:T(8,128)}, u32[]{:S(2)}) copy-start(f32[6,4]{1,0:T(8,128)} %copy-done.18) | copy-start | bytes 292
  161.9 1.2 copy-start.5
  161.9 1.5 copy-start.7
  161.9 1.8 copy-start.13
  161.9 1.8 copy-start.15
  163.8 6.5 %copy-start.17 = (f32[4,512]{1,0:T(4,128)S(1)}, f32[4,512]{1,0:T(4,128)}, u32[]{:S(2)}) copy-start(f32[4,512]{1,0:T(4,128)} %copy-done.16) | copy-start | bytes 24580
  166.6 11.7 %all-to-all-start.2 = ((f32[32,1,832]{2,1,0:T(1,128)}), f32[32,1,832]{2,1,0:T(1,128)S(1)}, u32[]{:S(2)}, u32[]{:S(2)}) async-start(f32[32,1,832]{2,1,0:T(1,128)} %reshape.199), calls=%async_computation.2 | async-start | bytes 229376 | tf_op jit(solution)/shard_map/all_to_all | solution.py:135
  (5 other events, 4.0 us)
Sparse Core Ops, SparseCore 0:
  24.5 23.9 all-gather.1

commit v14 on v10

--- a/solution.py
+++ b/solution.py
@@ -2,6 +2,8 @@
 import jax.numpy as jnp
 from jax import lax
 from jax.sharding import PartitionSpec as P
+from jax.experimental import pallas as pl
+from jax.experimental.pallas import tpu as pltpu
 
 VARS_GENE = 4
 NEED = 2
@@ -24,6 +26,29 @@
     return prod[:, :cols] + prod[:, cols:]
 
 
+def diag_kernel(t_ref, o_ref):
+    tile = t_ref[0].astype(jnp.float32)
+    size = tile.shape[0]
+    rows = lax.broadcasted_iota(jnp.int32, (size, size), 0)
+    cols = lax.broadcasted_iota(jnp.int32, (size, size), 1)
+    o_ref[0] = jnp.sum(jnp.where(rows == cols, tile, 0.0), axis=0, keepdims=True)
+
+
+def tile_diagonals(tiles, count):
+    size = tiles.shape[1]
+    out = pl.pallas_call(
+        diag_kernel,
+        grid=(count,),
+        in_specs=[pl.BlockSpec((1, size, size), lambda i: (i, 0, 0))],
+        out_specs=pl.BlockSpec((1, 1, size), lambda i: (i, 0, 0)),
+        out_shape=jax.ShapeDtypeStruct((count, 1, size), jnp.float32),
+        cost_estimate=pl.CostEstimate(
+            flops=count * size * size, transcendentals=0,
+            bytes_accessed=count * size * size * 2 + count * size * 4),
+    )(tiles)
+    return out.reshape(count, size)
+
+
 def local(genotypes, variance_comp, grm_tiles, tile_rows, tile_cols, tile_live):
     cols_here, rows_here = genotypes.shape
     tile_size = grm_tiles.shape[1]
@@ -41,10 +66,7 @@
     tau1 = variance_comp[1]
     live = tile_live[0]
 
-    eye = jnp.arange(tile_size)[:, None] == jnp.arange(tile_size)[None, :]
-    diag_values = jnp.sum(
-        jnp.where(eye[None], grm_tiles[:row_tiles].astype(jnp.float32), 0.0), axis=2
-    )
+    diag_values = tile_diagonals(grm_tiles, row_tiles)
     precond = (tau0 + tau1 * diag_values)[:, None, :]
     off_rows = tile_rows[row_tiles:]
     off_cols = tile_cols[row_tiles:]

time: 175 us -> 176 us (level)
  Pallas kernels: 0 us -> 3.48 us
  other arithmetic: 16.2 us -> 14.4 us
    pallas_call x0 -> x1, Pallas kernels: none -> 3.48 us  [tile_diagonals(): pl.pallas_call(diag_kernel, grid=(count,), in_specs=[pl.BlockSpec((1, siz...]
    reduce_sum x1 -> x0, other arithmetic: 2.42 us -> none  [local(): jnp.sum(jnp.where(eye[None], grm_tiles[:row_tiles].astype(jnp.float32), 0...]
    unnamed x75 -> x76, local copies, waits for them, and re-layouts: 7.69 us -> 7.69 us
where the time goes in v14:
time: 176 us; the launch traced here: 175 us
  waiting for transfers between devices  77 us (44%)
  between operations  26.6 us (15%)
  local copies, waits for them, and re-layouts  25.4 us (14%)
  starting transfers between devices  15.5 us (9%)
  other arithmetic  14.4 us (8%)
  matrix products  12.9 us (7%)
  Pallas kernels  3.48 us (2%)
    all_to_all x2, waiting for transfers between devices, exchange(): lax.all_to_all(pieces, 'ind', split_axis=0, concat_axis=0, tiled=True)  60 us
    dot_general x4, matrix products, batched_tile_dot(): lax.dot_general(parts, tiles, (((2,), (2,)), ((0,), (0,))), preferred_ele...  12.9 us
    all_to_all x2, starting transfers between devices, exchange(): lax.all_to_all(pieces, 'ind', split_axis=0, concat_axis=0, tiled=True)  11.8 us
    all_gather x1, waiting for transfers between devices, local(): geno_all = lax.all_gather(genotypes, 'var', axis=0, tiled=True)  8.36 us
    all_to_all x1, waiting for transfers between devices, chunk(): lax.all_to_all(spread, ('ind', 'var'), split_axis=0, concat_axis=0, tiled...  7.98 us
    unnamed x76, local copies, waits for them, and re-layouts  7.69 us
    reshape x4, local copies, waits for them, and re-layouts, to_tiles(): return jnp.transpose(x.reshape(cols_here, row_tiles, tile_size), (1, 0, 2))  6.53 us
    all_to_all x1, starting transfers between devices, chunk(): lax.all_to_all(spread, ('ind', 'var'), split_axis=0, concat_axis=0, tiled...  3.66 us
  transfers between devices with their start and end apart: 4, of which 4 were waited for; matrix products, arithmetic and copies ran while one was open for 12% of the time, Pallas kernels for 0%

profile of v14, /device:TPU:0, one launch (start us, length us, event | category | flops | bytes accessed | tf_op | source)
XLA Modules:
  0.0 175.3 jit_solution(17632543655994016022)
XLA Ops:
  7.2 1.4 fusion.68
  8.5 3.5 %shard_map.77 = f32[4,1,512]{2,1,0:T(1,128)} custom-call(bf16[10,512,512]{2,1,0:T(8,128)(2,1)} %t_ref.1), custom_call_target="tpu_custom_call" | custom-call | flops 1048576 | bytes 2105344 | tf_op jit(solution)/shard_map/pallas_call | solution.py:39
  12.0 2.0 %multiply_add_fusion.1 = f32[4,1,512]{2,1,0:T(1,128)S(1)} fusion(f32[4,1,512]{2,1,0:T(1,128)} %shard_map.77, f32[]{:T(128)} %bitcast.2, f32[]{:T(128)} %bitcast.1), kind=kLoop, calls=%fused_computation.111 | loop fusion | flops 4096 | bytes 16392 | tf_op jit(solution)/shard_map/add | solution.py:70
  14.9 1.6 pad_maximum_fusion
  16.5 7.4 %all-to-all-start = ((f32[8,136,512]{2,1,0:T(8,128)}), f32[8,136,512]{2,1,0:T(8,128)S(1)}, u32[]{:S(2)}, u32[]{:S(2)}) async-start(f32[8,136,512]{2,1,0:T(8,128)} %pad_maximum_fusion), calls=%async_computation | async-start | bytes 4456448 | tf_op jit(solution)/shard_map/all_to_all | solution.py:101
  38.6 3.4 %fusion.6 = f32[4,128,512]{2,1,0:T(8,128)} fusion(bf16[10,512,512]{2,1,0:T(8,128)(2,1)} %t_ref.1, bf16[4,64,512]{2,1,0:T(8,128)(2,1)S(1)} %get-tuple-element.25, bf16[4,64,512]{2,1,0:T(8,128)(2,1)S(1)} %get-tuple-element.22), kind=kOutput, calls=%fused_computation.12 | convolution fusion | flops 269484032 | bytes 3670016 | tf_op jit(solution)/shard_map/dot_general | solution.py:23
  41.9 8.4 %all-gather.2.cloned.1.call-done = f32[256,2048]{1,0:T(8,128)} async-done(((f32[64,2048]{1,0:T(8,128)}), f32[256,2048]{1,0:T(8,128)}) %all-gather.2.cloned.1.call-update) | async-done | bytes 2097168 | tf_op jit(solution)/shard_map/all_gather | solution.py:117
  50.3 2.7 %constant_dynamic-slice_fusion.6 = (f32[64,2048]{1,0:T(8,128)S(1)}, f32[64,2048]{1,0:T(8,128)}, f32[64,2048]{1,0:T(8,128)}, f32[64,2048]{1,0:T(8,128)}) fusion(f32[256,2048]{1,0:T(8,128)} %all-gather.2.cloned.1.call-done, s32[]{:T(128)S(6)} %select_n.83, s32[]{:T(128)S(6)} %select_n.86, s32[]{:T(128)S(6)} %select_n.85, s32[]{:T(128)S(6)} %select_n.84), kind=kLoop, calls=%fused_computation.118 | loop fusion | bytes 4194320 | tf_op jit(solution)/shard_map/dynamic_slice | solution.py:122
  53.4 1.6 reshape.153
  55.0 2.4 %reshape.152 = f32[64,4,512]{2,1,0:T(4,128)} reshape(f32[64,2048]{1,0:T(8,128)} %get-tuple-element.16) | data formatting | bytes 1048576 | tf_op jit(solution)/shard_map/reshape | solution.py:80
  57.4 2.2 %reshape.151 = f32[64,4,512]{2,1,0:T(4,128)} reshape(f32[64,2048]{1,0:T(8,128)} %get-tuple-element.17) | data formatting | bytes 1048576 | tf_op jit(solution)/shard_map/reshape | solution.py:80
  59.6 2.2 %multiply_reduce_fusion.3 = f32[4,64]{1,0:T(4,128)S(1)} fusion(f32[4,64,512]{2,0,1:T(4,128)} %copy.37, f32[1,4,64,512]{3,1,2,0:T(4,128)S(1)} %bitcast.190, f32[1,4,64,512]{3,1,2,0:T(4,128)} %bitcast.192, f32[1,4,64,512]{3,1,2,0:T(4,128)} %bitcast.194, f32[1,4,64,512]{3,1,2,0:T(4,128)S(1)} %bitcast.188), kind=kLoop, calls=%fused_computation.9 | loop fusion | flops 2621184 | bytes 2622464 | tf_op jit(solution)/shard_map/reduce_sum | solution.py:133
  61.9 13.1 %all-to-all-done = f32[8,136,512]{2,1,0:T(8,128)S(1)} async-done(((f32[8,136,512]{2,1,0:T(8,128)}), f32[8,136,512]{2,1,0:T(8,128)S(1)}, u32[]{:S(2)}, u32[]{:S(2)}) %all-to-all-start) | async-done | bytes 2228256 | tf_op jit(solution)/shard_map/all_to_all | solution.py:101
  75.5 3.0 %fusion.2 = f32[6,128,512]{2,1,0:T(8,128)S(1)} fusion(bf16[10,512,512]{2,1,0:T(8,128)(2,1)} %t_ref.1, bf16[6,64,512]{2,1,0:T(8,128)(2,1)S(1)} %get-tuple-element.21, bf16[6,64,512]{2,1,0:T(8,128)(2,1)S(1)} %get-tuple-element.20), kind=kOutput, calls=%fused_computation.4 | convolution fusion | flops 404226048 | bytes 5505024 | tf_op jit(solution)/shard_map/dot_general | solution.py:23
  79.9 2.3 %reduce-precision_convert_fusion.2 = (bf16[4,64,512]{2,1,0:T(8,128)(2,1)}, f32[4,64,512]{2,1,0:T(8,128)S(1)}, f32[4,64,512]{2,1,0:T(8,128)S(1)}) fusion(f32[4,512]{1,0:T(4,128)S(1)} %bitcast.213, f32[4,64,512]{2,1,0:T(8,128)S(1)} %multiply_reduce_fusion.1, f32[4,128,512]{2,1,0:T(8,128)S(1)} %copy-done.12, f32[]{:T(128)} %bitcast.2, ...), kind=kLoop, calls=%fused_computation.30 | loop fusion | flops 1179648 | bytes 3416072 | tf_op jit(solution)/shard_map/convert_element_type | solution.py:17
  83.7 1.4 copy-done.14
  85.0 4.4 %all-to-all-start.1 = ((f32[8,136,512]{2,1,0:T(8,128)}), f32[8,136,512]{2,1,0:T(8,128)}, u32[]{:S(2)}, u32[]{:S(2)}) async-start(f32[8,136,512]{2,1,0:T(8,128)} %bitcast.209), calls=%async_computation.1 | async-start | bytes 4456448 | tf_op jit(solution)/shard_map/all_to_all | solution.py:101
  89.6 3.5 %fusion.4 = f32[4,128,512]{2,1,0:T(8,128)} fusion(bf16[10,512,512]{2,1,0:T(8,128)(2,1)} %t_ref.1, bf16[4,64,512]{2,1,0:T(8,128)(2,1)S(1)} %fusion.17, bf16[4,64,512]{2,1,0:T(8,128)(2,1)} %get-tuple-element.11), kind=kOutput, calls=%fused_computation.10 | convolution fusion | flops 269484032 | bytes 3670016 | tf_op jit(solution)/shard_map/dot_general | solution.py:23
  93.1 46.9 %all-to-all-done.1 = f32[8,136,512]{2,1,0:T(8,128)} async-done(((f32[8,136,512]{2,1,0:T(8,128)}), f32[8,136,512]{2,1,0:T(8,128)}, u32[]{:S(2)}, u32[]{:S(2)}) %all-to-all-start.1) | async-done | bytes 2228256 | tf_op jit(solution)/shard_map/all_to_all | solution.py:101
  141.2 1.8 %slice.213 = f32[8,128,512]{2,1,0:T(8,128)S(1)} slice(f32[8,136,512]{2,1,0:T(8,128)} %all-to-all-done.1), slice={[0:8], [0:128], [0:512]} | slice | bytes 4194304 | tf_op jit(solution)/shard_map/slice | solution.py:102
  143.3 3.0 %fusion = f32[6,128,512]{2,1,0:T(8,128)S(1)} fusion(bf16[10,512,512]{2,1,0:T(8,128)(2,1)} %t_ref.1, bf16[6,64,512]{2,1,0:T(8,128)(2,1)S(1)} %get-tuple-element.19, bf16[6,64,512]{2,1,0:T(8,128)(2,1)S(1)} %get-tuple-element.18), kind=kOutput, calls=%fused_computation.2 | convolution fusion | flops 404226048 | bytes 5505024 | tf_op jit(solution)/shard_map/dot_general | solution.py:23
  148.3 1.8 %fusion.26 = (f32[4,64,512]{2,1,0:T(8,128)S(1)}, f32[4,64,512]{2,1,0:T(8,128)S(1)}) fusion(f32[4,64,512]{2,1,0:T(8,128)S(1)} %multiply_reduce_fusion, f32[4,128,512]{2,1,0:T(8,128)S(1)} %copy-done.15, f32[64]{0:T(128)S(1)} %get-tuple-element.34, f32[]{:T(128)} %bitcast.2, f32[]{:T(128)} %bitcast.1, f32[4,64,512]{2,1,0:T(8,128)S(1)} %copy-done.5, ...), kind=kLoop, calls=%fused_computation.45 | loop fusion | flops 1572864 | bytes 5251336 | tf_op jit(solution)/shard_map/add | solution.py:143
  153.3 3.7 %all-to-all-start.2 = ((f32[32,1,832]{2,1,0:T(1,128)}), f32[32,1,832]{2,1,0:T(1,128)S(1)}, u32[]{:S(2)}, u32[]{:S(2)}) async-start(f32[32,1,832]{2,1,0:T(1,128)} %reshape.169), calls=%async_computation.2 | async-start | bytes 229376 | tf_op jit(solution)/shard_map/all_to_all | solution.py:153
  157.0 8.0 %all-to-all-done.2 = f32[32,1,832]{2,1,0:T(1,128)S(1)} async-done(((f32[32,1,832]{2,1,0:T(1,128)}), f32[32,1,832]{2,1,0:T(1,128)S(1)}, u32[]{:S(2)}, u32[]{:S(2)}) %all-to-all-start.2) | async-done | bytes 106528 | tf_op jit(solution)/shard_map/all_to_all | solution.py:153
  (133 shorter events, 17.1 us)
Async XLA Ops:
  8.5 5.5 %copy-start = (f32[64,2048]{1,0:T(8,128)S(1)}, f32[64,2048]{1,0:T(8,128)}, u32[]{:S(2)}) copy-start(f32[64,2048]{1,0:T(8,128)} %param.6) | copy-start | bytes 1572868
  16.5 8.2 %copy-start.16 = (s32[10]{0:T(128)S(1)}, s32[10]{0:T(128)}, u32[]{:S(2)}) copy-start(s32[10]{0:T(128)} %param.10) | copy-start | bytes 124
  16.5 18.2 %copy-start.17 = (s32[10]{0:T(128)S(1)}, s32[10]{0:T(128)}, u32[]{:S(2)}) copy-start(s32[10]{0:T(128)} %param.9) | copy-start | bytes 124
  16.5 58.5 %all-to-all-start = ((f32[8,136,512]{2,1,0:T(8,128)}), f32[8,136,512]{2,1,0:T(8,128)S(1)}, u32[]{:S(2)}, u32[]{:S(2)}) async-start(f32[8,136,512]{2,1,0:T(8,128)} %pad_maximum_fusion), calls=%async_computation | async-start | bytes 4456448 | tf_op jit(solution)/shard_map/all_to_all | solution.py:101
  23.9 26.4 %all-gather.2.cloned.1.call-start = ((), (), s32[]{:S(2)}) async-start(), calls=%async_computation.3 | async-start | bytes 2621440 | tf_op jit(solution)/shard_map/all_gather | solution.py:117
  53.4 8.5 %copy-start.6 = (f32[64,4,512]{2,1,0:T(4,128)}, f32[64,4,512]{2,1,0:T(4,128)S(1)}, u32[]{:S(2)}) copy-start(f32[64,4,512]{2,1,0:T(4,128)S(1)} %reshape.150) | copy-start | bytes 1572868
  55.0 6.9 %copy-start.8 = (f32[64,4,512]{2,1,0:T(4,128)}, f32[64,4,512]{2,1,0:T(4,128)S(1)}, u32[]{:S(2)}) copy-start(f32[64,4,512]{2,1,0:T(4,128)S(1)} %reshape.153) | copy-start | bytes 1572868
  78.5 1.0 copy-start.1
  78.5 1.4 copy-start.12
  79.9 3.3 %copy-start.4 = (f32[4,64,512]{2,1,0:T(8,128)}, f32[4,64,512]{2,1,0:T(8,128)S(1)}, u32[]{:S(2)}) copy-start(f32[4,64,512]{2,1,0:T(8,128)S(1)} %multiply_reduce_fusion.1) | copy-start | bytes 1572868
  82.2 0.8 copy-start.2
  83.7 1.4 copy-start.14
  85.0 55.0 %all-to-all-start.1 = ((f32[8,136,512]{2,1,0:T(8,128)}), f32[8,136,512]{2,1,0:T(8,128)}, u32[]{:S(2)}, u32[]{:S(2)}) async-start(f32[8,136,512]{2,1,0:T(8,128)} %bitcast.209), calls=%async_computation.1 | async-start | bytes 4456448 | tf_op jit(solution)/shard_map/all_to_all | solution.py:101
  146.4 1.0 copy-start.3
  146.4 1.2 copy-start.5
  146.4 1.5 copy-start.13
  146.4 1.8 %copy-start.15 = (f32[4,128,512]{2,1,0:T(8,128)S(1)}, f32[4,128,512]{2,1,0:T(8,128)}, u32[]{:S(2)}) copy-start(f32[4,128,512]{2,1,0:T(8,128)} %fusion.4) | copy-start | bytes 3145732
  150.0 1.0 copy-start.7
  150.1 1.2 copy-start.9
  150.1 1.3 copy-start.10
  150.1 1.5 copy-start.11
  153.3 11.7 %all-to-all-start.2 = ((f32[32,1,832]{2,1,0:T(1,128)}), f32[32,1,832]{2,1,0:T(1,128)S(1)}, u32[]{:S(2)}, u32[]{:S(2)}) async-start(f32[32,1,832]{2,1,0:T(1,128)} %reshape.169), calls=%async_computation.2 | async-start | bytes 229376 | tf_op jit(solution)/shard_map/all_to_all | solution.py:153
Sparse Core Ops, SparseCore 0:
  26.3 23.9 all-gather.1

commit v15 on v10

--- a/solution.py
+++ b/solution.py
@@ -62,14 +62,17 @@
 
     def exchange(x, extra, by_concat=False):
         width = x.shape[1]
-        flat = extra.reshape(-1)
-        flat = jnp.pad(flat, (0, PAD_ROWS * tile_size - flat.shape[0]))
         if by_concat:
             rows = []
             for p in range(peers):
                 rows += [x[(p + t) % row_tiles] for t in range(NEED)]
-                rows.append(flat.reshape(PAD_ROWS, tile_size))
-            pieces = jnp.concatenate(rows, axis=0).reshape(peers, -1, tile_size)
+            pieces = jnp.concatenate(rows, axis=0).reshape(peers * NEED, width, tile_size)
+            arrived = lax.all_to_all(pieces, "ind", split_axis=0, concat_axis=0, tiled=True)
+            return arrived, None
+        flat = extra.reshape(-1)
+        flat = jnp.pad(flat, (0, PAD_ROWS * tile_size - flat.shape[0]))
+        if by_concat:
+            pieces = None
         else:
             rolled = jnp.stack([jnp.roll(x, -t, axis=0) for t in range(NEED)], axis=1)
             rolled = rolled.reshape(row_tiles, NEED * width, tile_size)
@@ -81,10 +84,13 @@
         sums = jnp.sum(arrived[:, NEED * width:].reshape(peers, -1)[:, :extra.size], axis=0)
         return tiles_in, sums.reshape(extra.shape)
 
-    def kprod(x, arrived):
+    def kprod(x, arrived, gather=False):
         width = x.shape[1]
-        picked = jnp.stack([lax.dynamic_index_in_dim(arrived, position[s], 0, keepdims=False)
-                            for s in range(off_count)])
+        if gather:
+            picked = jnp.take(arrived, position, axis=0, mode="clip")
+        else:
+            picked = jnp.stack([lax.dynamic_index_in_dim(arrived, position[s], 0, keepdims=False)
+                                for s in range(off_count)])
         near = batched_tile_dot(x, grm_tiles[:row_tiles])
         far = batched_tile_dot(picked, grm_tiles[row_tiles:])
         return near + jnp.sum(weight[:, :, None, None] * far[:, None], axis=0)
@@ -109,14 +115,12 @@
         image0 = tau0 * z0 + tau1 * kz0
         w = image0 / precond
         p0_local = jnp.sum(geno_sub * z0[None], axis=(1, 3))
-        extra1 = jnp.concatenate([colsum(z0 * image0)[None], p0_local], axis=0)
-        tiles1, sums1 = exchange(w, extra1, by_concat=True)
-        dad0 = sums1[0]
-        p0 = sums1[1:]
+        dad0 = lax.psum(colsum(z0 * image0), "ind")
+        tiles1, _ = exchange(w, None, by_concat=True)
         alpha0 = rz0 / dad0
         resid1 = g - alpha0[None, :, None] * image0
         z1 = resid1 / precond
-        kw = kprod(w, tiles1)
+        kw = kprod(w, tiles1, gather=True)
         kz1 = kz0 - alpha0[None, :, None] * kw
         az1 = tau0 * z1 + tau1 * kz1
         red_local = jnp.concatenate(
@@ -126,7 +130,7 @@
         )
         lead = (me == 0).astype(jnp.float32)
         payload = jnp.concatenate(
-            [red_local, lead * rz0[None], lead * dad0[None], lead * p0], axis=0)
+            [red_local, lead * rz0[None], lead * dad0[None], p0_local], axis=0)
         spread = jnp.broadcast_to(payload[None], (peers * nvar,) + payload.shape)
         got = lax.all_to_all(spread, ("ind", "var"), split_axis=0, concat_axis=0, tiled=True)
         tot = jnp.sum(got.reshape((peers, nvar) + payload.shape), axis=0)

time: 175 us -> 183 us (1.046)
  waiting for transfers between devices: 76.9 us -> 42.7 us
  blocking collectives: 0 us -> 33.3 us
  starting transfers between devices: 15.6 us -> 22.4 us
  local copies, waits for them, and re-layouts: 25.4 us -> 27.6 us
    psum x0 -> x1, blocking collectives: none -> 33.3 us  [chunk(): dad0 = lax.psum(colsum(z0 * image0), 'ind')]
    all_to_all x2, waiting for transfers between devices: 59.9 us -> 34.1 us  [exchange(): lax.all_to_all(pieces, 'ind', split_axis=0, concat_axis=0, tiled=True)]
    all_gather x1, waiting for transfers between devices: 8.36 us -> 0.01 us  [local(): geno_all = lax.all_gather(genotypes, 'var', axis=0, tiled=True)]
    all_to_all x1, starting transfers between devices: 3.6 us -> 10.6 us  [chunk(): lax.all_to_all(spread, ('ind', 'var'), split_axis=0, concat_axis=0, tiled...]
    gather x0 -> x1, local copies, waits for them, and re-layouts: none -> 2.31 us  [kprod(): picked = jnp.take(arrived, position, axis=0, mode='clip')]
    reshape x4, local copies, waits for them, and re-layouts: 6.53 us -> 8.77 us  [to_tiles(): return jnp.transpose(x.reshape(cols_here, row_tiles, tile_size), (1, 0, 2))]
    unnamed x75 -> x60, local copies, waits for them, and re-layouts: 7.69 us -> 6.14 us
  transfers between devices with their start and end apart: 4 -> 4, of which waited for: 4 -> 2; matrix products, arithmetic and copies ran while one was open for 12% -> 16% of each run, Pallas kernels for 0% -> 0%
where the time goes in v15:
time: 183 us; the launch traced here: 182 us
  waiting for transfers between devices  42.7 us (23%)
  blocking collectives  33.3 us (18%)
  local copies, waits for them, and re-layouts  27.6 us (15%)
  between operations  26.6 us (15%)
  starting transfers between devices  22.4 us (12%)
  other arithmetic  17.4 us (10%)
  matrix products  11.8 us (6%)
    all_to_all x2, waiting for transfers between devices, exchange(): lax.all_to_all(pieces, 'ind', split_axis=0, concat_axis=0, tiled=True)  34.1 us
    psum x1, blocking collectives, chunk(): dad0 = lax.psum(colsum(z0 * image0), 'ind')  33.3 us
    dot_general x4, matrix products, batched_tile_dot(): lax.dot_general(parts, tiles, (((2,), (2,)), ((0,), (0,))), preferred_ele...  11.8 us
    all_to_all x2, starting transfers between devices, exchange(): lax.all_to_all(pieces, 'ind', split_axis=0, concat_axis=0, tiled=True)  11.8 us
    all_to_all x1, starting transfers between devices, chunk(): lax.all_to_all(spread, ('ind', 'var'), split_axis=0, concat_axis=0, tiled...  10.6 us
    reshape x4, local copies, waits for them, and re-layouts, to_tiles(): return jnp.transpose(x.reshape(cols_here, row_tiles, tile_size), (1, 0, 2))  8.77 us
    all_to_all x1, waiting for transfers between devices, chunk(): lax.all_to_all(spread, ('ind', 'var'), split_axis=0, concat_axis=0, tiled...  7.98 us
    unnamed x60, local copies, waits for them, and re-layouts  6.14 us
  transfers between devices with their start and end apart: 4, of which 2 were waited for; matrix products, arithmetic and copies ran while one was open for 16% of the time, Pallas kernels for 0%

profile of v15, /device:TPU:0, one launch (start us, length us, event | category | flops | bytes accessed | tf_op | source)
XLA Modules:
  0.0 181.9 jit_solution(9272789361395929292)
XLA Ops:
  7.3 1.3 fusion.68
  8.6 2.4 %select_reduce_fusion = f32[4,512]{1,0:T(4,128)S(1)} fusion(pred[512,512]{1,0:T(8,128)(4,1)S(1)} %iota_compare_fusion, bf16[10,512,512]{2,1,0:T(8,128)(2,1)} %param.8), kind=kLoop, calls=%fused_computation.1 | loop fusion | flops 3143680 | bytes 2367488 | tf_op jit(solution)/shard_map/reduce_sum | solution.py:45
  13.8 1.6 pad_maximum_fusion
  15.4 7.4 %all-to-all-start = ((f32[8,136,512]{2,1,0:T(8,128)}), f32[8,136,512]{2,1,0:T(8,128)S(1)}, u32[]{:S(2)}, u32[]{:S(2)}) async-start(f32[8,136,512]{2,1,0:T(8,128)} %pad_maximum_fusion), calls=%async_computation | async-start | bytes 4456448 | tf_op jit(solution)/shard_map/all_to_all | solution.py:82
  36.4 3.4 %fusion.6 = f32[4,128,512]{2,1,0:T(8,128)} fusion(bf16[10,512,512]{2,1,0:T(8,128)(2,1)} %param.8, bf16[4,64,512]{2,1,0:T(8,128)(2,1)S(1)} %get-tuple-element.27, bf16[4,64,512]{2,1,0:T(8,128)(2,1)S(1)} %get-tuple-element.24), kind=kOutput, calls=%fused_computation.14 | convolution fusion | flops 269484032 | bytes 3670016 | tf_op jit(solution)/shard_map/dot_general | solution.py:21
  39.8 34.1 %all-to-all-done = f32[8,136,512]{2,1,0:T(8,128)S(1)} async-done(((f32[8,136,512]{2,1,0:T(8,128)}), f32[8,136,512]{2,1,0:T(8,128)S(1)}, u32[]{:S(2)}, u32[]{:S(2)}) %all-to-all-start) | async-done | bytes 2228256 | tf_op jit(solution)/shard_map/all_to_all | solution.py:82
  74.4 3.0 %fusion.2 = f32[6,128,512]{2,1,0:T(8,128)S(1)} fusion(bf16[10,512,512]{2,1,0:T(8,128)(2,1)} %param.8, bf16[6,64,512]{2,1,0:T(8,128)(2,1)S(1)} %get-tuple-element.23, bf16[6,64,512]{2,1,0:T(8,128)(2,1)S(1)} %get-tuple-element.22), kind=kOutput, calls=%fused_computation.6 | convolution fusion | flops 404226048 | bytes 5505024 | tf_op jit(solution)/shard_map/dot_general | solution.py:21
  78.8 2.3 %reduce-precision_convert_fusion.2 = (bf16[4,64,512]{2,1,0:T(8,128)(2,1)S(1)}, f32[4,64,512]{2,1,0:T(8,128)S(1)}, f32[4,64,512]{2,1,0:T(8,128)}) fusion(f32[4,512]{1,0:T(4,128)S(1)} %multiply_add_fusion.1, f32[4,64,512]{2,1,0:T(8,128)S(1)} %multiply_reduce_fusion.1, f32[4,128,512]{2,1,0:T(8,128)S(1)} %copy-done.6, f32[]{:T(128)} %bitcast.2, ...), kind=kLoop, calls=%fused_computation.33 | loop fusion | flops 1179648 | bytes 3416072 | tf_op jit(solution)/shard_map/convert_element_type | solution.py:15
  81.5 1.3 copy-done.8
  82.8 4.3 %all-to-all-start.1 = ((f32[16,64,512]{2,1,0:T(8,128)}), f32[16,64,512]{2,1,0:T(8,128)}, u32[]{:S(2)}, u32[]{:S(2)}) async-start(f32[16,64,512]{2,1,0:T(8,128)} %bitcast.187), calls=%async_computation.1 | async-start | bytes 4194304 | tf_op jit(solution)/shard_map/all_to_all | solution.py:70
  87.1 2.2 %copy.38 = f32[4,64,512]{2,0,1:T(4,128)} copy(f32[4,64,512]{2,1,0:T(8,128)} %copy-done.5) | data formatting | bytes 1048576 | tf_op jit(solution)/shard_map/div | solution.py:111
  90.0 2.9 %constant_dynamic-slice_fusion.6 = (f32[64,2048]{1,0:T(8,128)}, f32[64,2048]{1,0:T(8,128)}, f32[64,2048]{1,0:T(8,128)}, f32[64,2048]{1,0:T(8,128)}) fusion(f32[256,2048]{1,0:T(8,128)} %all-gather.2.cloned.1.call-done, s32[]{:T(128)S(6)} %select_n.82, s32[]{:T(128)S(6)} %select_n.85, s32[]{:T(128)S(6)} %select_n.84, s32[]{:T(128)S(6)} %select_n.83), kind=kLoop, calls=%fused_computation.108 | loop fusion | bytes 4194320 | tf_op jit(solution)/shard_map/dynamic_slice | solution.py:106
  92.9 2.2 %reshape.130 = f32[64,4,512]{2,1,0:T(4,128)} reshape(f32[64,2048]{1,0:T(8,128)} %get-tuple-element.16) | data formatting | bytes 1048576 | tf_op jit(solution)/shard_map/reshape | solution.py:58
  95.1 2.2 %reshape.131 = f32[64,4,512]{2,1,0:T(4,128)} reshape(f32[64,2048]{1,0:T(8,128)} %get-tuple-element.19) | data formatting | bytes 1048576 | tf_op jit(solution)/shard_map/reshape | solution.py:58
  97.3 2.2 %reshape.132 = f32[64,4,512]{2,1,0:T(4,128)} reshape(f32[64,2048]{1,0:T(8,128)} %get-tuple-element.18) | data formatting | bytes 1048576 | tf_op jit(solution)/shard_map/reshape | solution.py:58
  99.4 2.2 %reshape.133 = f32[64,4,512]{2,1,0:T(4,128)} reshape(f32[64,2048]{1,0:T(8,128)} %get-tuple-element.17) | data formatting | bytes 1048576 | tf_op jit(solution)/shard_map/reshape | solution.py:58
  103.0 33.3 %psum.7 = f32[64]{0:T(128)S(1)} all-reduce(f32[64]{0:T(128)S(1)} %multiply_reduce_fusion.6), channel_id=1, replica_groups=mesh['ind'=8,'var'=4] {'ind'}, use_global_device_ids=true, to_apply=%region_5.6 | all-reduce | flops 64 | bytes 512 | tf_op jit(solution)/shard_map/psum | solution.py:118
  136.9 2.4 %fusion.4 = f32[4,128,512]{2,1,0:T(8,128)S(1)} fusion(bf16[10,512,512]{2,1,0:T(8,128)(2,1)} %param.8, bf16[4,64,512]{2,1,0:T(8,128)(2,1)S(1)} %fusion.17, bf16[4,64,512]{2,1,0:T(8,128)(2,1)S(1)} %get-tuple-element.13), kind=kOutput, calls=%fused_computation.12 | convolution fusion | flops 269484032 | bytes 3670016 | tf_op jit(solution)/shard_map/dot_general | solution.py:21
  139.3 2.3 %gather_fusion = f32[6,64,512]{2,1,0:T(8,128)S(1)} fusion(f32[16,64,512]{2,1,0:T(8,128)} %all-to-all-done.1, s32[1024]{0:T(1024)} %pad_clamp_fusion), kind=kCustom, calls=%fused_computation | custom fusion | bytes 1572888 | tf_op jit(solution)/shard_map/jit(_take)/gather | solution.py:90
  141.8 3.0 %fusion = f32[6,128,512]{2,1,0:T(8,128)S(1)} fusion(bf16[10,512,512]{2,1,0:T(8,128)(2,1)} %param.8, bf16[6,64,512]{2,1,0:T(8,128)(2,1)S(1)} %get-tuple-element.21, bf16[6,64,512]{2,1,0:T(8,128)(2,1)S(1)} %get-tuple-element.20), kind=kOutput, calls=%fused_computation.4 | convolution fusion | flops 404226048 | bytes 5505024 | tf_op jit(solution)/shard_map/dot_general | solution.py:21
  146.4 1.8 fusion.26
  149.8 2.2 %multiply_reduce_fusion.2 = (f32[4,64]{1,0:T(4,128)S(1)}, f32[4,64]{1,0:T(4,128)S(1)}) fusion(f32[4,64,512]{2,0,1:T(4,128)S(1)} %copy-done.9, f32[1,4,64,512]{3,1,2,0:T(4,128)S(1)} %bitcast.191, f32[1,4,64,512]{3,1,2,0:T(4,128)S(1)} %bitcast.190, f32[1,4,64,512]{3,1,2,0:T(4,128)S(1)} %bitcast.189, f32[1,4,64,512]{3,1,2,0:T(4,128)S(1)} %bitcast.188, ...), kind=kLoop, calls=%fused_computation.10 | loop fusion | flops 3669504 | bytes 3147776 | tf_op jit(solution)/shard_map/reduce_sum | solution.py:117
  152.9 10.6 %all-to-all-start.2 = ((f32[32,1,832]{2,1,0:T(1,128)}), f32[32,1,832]{2,1,0:T(1,128)S(1)}, u32[]{:S(2)}, u32[]{:S(2)}) async-start(f32[32,1,832]{2,1,0:T(1,128)} %reshape.153), calls=%async_computation.2 | async-start | bytes 229376 | tf_op jit(solution)/shard_map/all_to_all | solution.py:135
  163.6 8.0 %all-to-all-done.2 = f32[32,1,832]{2,1,0:T(1,128)S(1)} async-done(((f32[32,1,832]{2,1,0:T(1,128)}), f32[32,1,832]{2,1,0:T(1,128)S(1)}, u32[]{:S(2)}, u32[]{:S(2)}) %all-to-all-start.2) | async-done | bytes 106528 | tf_op jit(solution)/shard_map/all_to_all | solution.py:135
  (111 shorter events, 16.5 us)
Async XLA Ops:
  7.2 5.1 %copy-start = (f32[64,2048]{1,0:T(8,128)S(1)}, f32[64,2048]{1,0:T(8,128)}, u32[]{:S(2)}) copy-start(f32[64,2048]{1,0:T(8,128)} %param.6) | copy-start | bytes 1572868
  12.5 0.8 copy-start.5
  15.4 8.2 %copy-start.16 = (s32[10]{0:T(128)S(1)}, s32[10]{0:T(128)}, u32[]{:S(2)}) copy-start(s32[10]{0:T(128)} %param.10) | copy-start | bytes 124
  15.4 17.1 %copy-start.17 = (s32[10]{0:T(128)S(1)}, s32[10]{0:T(128)}, u32[]{:S(2)}) copy-start(s32[10]{0:T(128)} %param.9) | copy-start | bytes 124
  15.4 58.5 %all-to-all-start = ((f32[8,136,512]{2,1,0:T(8,128)}), f32[8,136,512]{2,1,0:T(8,128)S(1)}, u32[]{:S(2)}, u32[]{:S(2)}) async-start(f32[8,136,512]{2,1,0:T(8,128)} %pad_maximum_fusion), calls=%async_computation | async-start | bytes 4456448 | tf_op jit(solution)/shard_map/all_to_all | solution.py:82
  22.8 67.1 %all-gather.2.cloned.1.call-start = ((), (), s32[]{:S(2)}) async-start(), calls=%async_computation.3 | async-start | bytes 2621440 | tf_op jit(solution)/shard_map/all_gather | solution.py:101
  77.4 1.0 copy-start.1
  77.4 1.4 copy-start.6
  78.8 2.4 %copy-start.3 = (f32[4,64,512]{2,1,0:T(8,128)}, f32[4,64,512]{2,1,0:T(8,128)S(1)}, u32[]{:S(2)}) copy-start(f32[4,64,512]{2,1,0:T(8,128)S(1)} %multiply_reduce_fusion.1) | copy-start | bytes 1572868
  81.4 1.3 copy-start.8
  82.8 56.5 %all-to-all-start.1 = ((f32[16,64,512]{2,1,0:T(8,128)}), f32[16,64,512]{2,1,0:T(8,128)}, u32[]{:S(2)}, u32[]{:S(2)}) async-start(f32[16,64,512]{2,1,0:T(8,128)} %bitcast.187), calls=%async_computation.1 | async-start | bytes 4194304 | tf_op jit(solution)/shard_map/all_to_all | solution.py:70
  144.8 1.0 copy-start.2
  144.8 1.2 copy-start.4
  144.8 1.5 copy-start.7
  148.1 1.0 copy-start.9
  148.2 1.2 copy-start.10
  148.2 1.3 copy-start.11
  148.2 1.5 copy-start.12
  148.2 1.6 copy-start.13
  149.0 3.1 %copy-start.14 = (f32[1,64]{1,0:T(1,128)S(1)}, f32[1,64]{1,0:T(1,128)}, u32[]{:S(2)}) copy-start(f32[1,64]{1,0:T(1,128)} %get-tuple-element.35) | copy-start | bytes 772
  149.0 3.1 %copy-start.15 = (f32[1,64]{1,0:T(1,128)S(1)}, f32[1,64]{1,0:T(1,128)}, u32[]{:S(2)}) copy-start(f32[1,64]{1,0:T(1,128)} %get-tuple-element.37) | copy-start | bytes 772
  152.9 18.7 %all-to-all-start.2 = ((f32[32,1,832]{2,1,0:T(1,128)}), f32[32,1,832]{2,1,0:T(1,128)S(1)}, u32[]{:S(2)}, u32[]{:S(2)}) async-start(f32[32,1,832]{2,1,0:T(1,128)} %reshape.153), calls=%async_computation.2 | async-start | bytes 229376 | tf_op jit(solution)/shard_map/all_to_all | solution.py:135
Sparse Core Ops, SparseCore 0:
  25.2 23.9 all-gather.1

commit v16 on v10

--- a/solution.py
+++ b/solution.py
@@ -92,7 +92,12 @@
     def colsum(x):
         return jnp.sum(x, axis=(0, 2))
 
-    geno_all = lax.all_gather(genotypes, "var", axis=0, tiled=True)
+    parts = [genotypes] + [
+        lax.ppermute(genotypes, "var", [(j, (j + k) % nvar) for j in range(nvar)])
+        for k in range(1, nvar)]
+    parts = jnp.stack(parts)
+    order = (v - jnp.arange(nvar, dtype=jnp.int32)) % nvar
+    geno_all = jnp.take(parts, order, axis=0, mode="clip").reshape(ncol, rows_here)
     first = v * cols_here
     a_out = first // genes
     g0 = first % genes

time: 175 us -> 162 us (0.926)
  between operations: 26.7 us -> 13.2 us
  waiting for transfers between devices: 76.9 us -> 65.1 us
  local copies, waits for them, and re-layouts: 25.4 us -> 30.6 us
  other arithmetic: 16.2 us -> 20.3 us
  starting transfers between devices: 15.6 us -> 18.8 us
    all_gather x1 -> x0, waiting for transfers between devices: 8.36 us -> none  [local(): geno_all = lax.all_gather(genotypes, 'var', axis=0, tiled=True)]
    all_to_all x2, waiting for transfers between devices: 59.9 us -> 52.3 us  [exchange(): lax.all_to_all(pieces, 'ind', split_axis=0, concat_axis=0, tiled=True)]
    ppermute x0 -> x3, waiting for transfers between devices: none -> 4.8 us  [local(): lax.ppermute(genotypes, 'var', [(j, (j + k) % nvar) for j in range(nvar)])]
    gather x0 -> x1, local copies, waits for them, and re-layouts: none -> 3.58 us  [local(): jnp.take(parts, order, axis=0, mode='clip').reshape(ncol, rows_here)]
    ppermute x0 -> x3, starting transfers between devices: none -> 3.26 us  [local(): lax.ppermute(genotypes, 'var', [(j, (j + k) % nvar) for j in range(nvar)])]
    another operation x0 -> x1, other arithmetic: none -> 2.91 us  [local(): parts = jnp.stack(parts)]
    unnamed x75 -> x71, local copies, waits for them, and re-layouts: 7.69 us -> 7.52 us
  transfers between devices with their start and end apart: 4 -> 6, of which waited for: 4 -> 4; matrix products, arithmetic and copies ran while one was open for 12% -> 18% of each run, Pallas kernels for 0% -> 0%
where the time goes in v16:
time: 162 us; the launch traced here: 161 us
  waiting for transfers between devices  65.1 us (40%)
  local copies, waits for them, and re-layouts  30.6 us (19%)
  other arithmetic  20.3 us (13%)
  starting transfers between devices  18.8 us (12%)
  between operations  13.2 us (8%)
  matrix products  13.1 us (8%)
    all_to_all x2, waiting for transfers between devices, exchange(): lax.all_to_all(pieces, 'ind', split_axis=0, concat_axis=0, tiled=True)  52.3 us
    dot_general x4, matrix products, batched_tile_dot(): lax.dot_general(parts, tiles, (((2,), (2,)), ((0,), (0,))), preferred_ele...  13.1 us
    all_to_all x2, starting transfers between devices, exchange(): lax.all_to_all(pieces, 'ind', split_axis=0, concat_axis=0, tiled=True)  11.9 us
    reshape x4, local copies, waits for them, and re-layouts, to_tiles(): return jnp.transpose(x.reshape(cols_here, row_tiles, tile_size), (1, 0, 2))  8.25 us
    all_to_all x1, waiting for transfers between devices, chunk(): lax.all_to_all(spread, ('ind', 'var'), split_axis=0, concat_axis=0, tiled...  7.98 us
    unnamed x71, local copies, waits for them, and re-layouts  7.52 us
    ppermute x3, waiting for transfers between devices, local(): lax.ppermute(genotypes, 'var', [(j, (j + k) % nvar) for j in range(nvar)])  4.8 us
    convert_element_type x5, other arithmetic, split2(): return (hi.astype(jnp.bfloat16), lo.astype(jnp.bfloat16))  3.72 us
  transfers between devices with their start and end apart: 6, of which 4 were waited for; matrix products, arithmetic and copies ran while one was open for 18% of the time, Pallas kernels for 0%

profile of v16, /device:TPU:0, one launch (start us, length us, event | category | flops | bytes accessed | tf_op | source)
XLA Modules:
  0.0 161.1 jit_solution(989255397720290593)
XLA Ops:
  2.1 2.4 %select_reduce_fusion = f32[4,512]{1,0:T(4,128)S(1)} fusion(pred[512,512]{1,0:T(8,128)(4,1)S(1)} %iota_compare_fusion, bf16[10,512,512]{2,1,0:T(8,128)(2,1)} %param.8), kind=kLoop, calls=%fused_computation.1 | loop fusion | flops 3143680 | bytes 2367488 | tf_op jit(solution)/shard_map/reduce_sum | solution.py:45
  7.6 1.7 %pad_maximum_fusion = f32[8,136,512]{2,1,0:T(8,128)} fusion(f32[8,8,512]{2,1,0:T(8,128)S(1)} %broadcast_in_dim.31, f32[8,128,512]{2,1,0:T(8,128)S(1)} %bitcast.193), kind=kLoop, calls=%fused_computation.8 | loop fusion | flops 557056 | bytes 4456448 | tf_op jit(solution)/shard_map/concatenate | solution.py:78
  9.2 7.4 %all-to-all-start = ((f32[8,136,512]{2,1,0:T(8,128)}), f32[8,136,512]{2,1,0:T(8,128)S(1)}, u32[]{:S(2)}, u32[]{:S(2)}) async-start(f32[8,136,512]{2,1,0:T(8,128)} %pad_maximum_fusion), calls=%async_computation | async-start | bytes 4456448 | tf_op jit(solution)/shard_map/all_to_all | solution.py:79
  16.7 1.7 %collective-permute-start.2 = (f32[64,2048]{1,0:T(8,128)S(1)}, f32[64,2048]{1,0:T(8,128)}, u32[]{:S(2)}, u32[]{:S(2)}) collective-permute-start(f32[64,2048]{1,0:T(8,128)S(1)} %copy-done), channel_id=1, source_target_pairs={{0,3},{1,0},{2,1},{3,2},{4,7},{5,4},{6,5},{7,6},{8,11},{9,8},{10,9... | collective-permute-start | bytes 1572872 | tf_op jit(solution)/shard_map/ppermute | solution.py:96
  33.8 3.6 %fusion.6 = f32[4,128,512]{2,1,0:T(8,128)} fusion(bf16[10,512,512]{2,1,0:T(8,128)(2,1)} %param.8, bf16[4,64,512]{2,1,0:T(8,128)(2,1)} %get-tuple-element.25, bf16[4,64,512]{2,1,0:T(8,128)(2,1)} %get-tuple-element.22), kind=kOutput, calls=%fused_computation.15 | convolution fusion | flops 269484032 | bytes 3670016 | tf_op jit(solution)/shard_map/dot_general | solution.py:21
  37.4 4.8 %collective-permute-done.1 = f32[64,2048]{1,0:T(8,128)} collective-permute-done((f32[64,2048]{1,0:T(8,128)S(1)}, f32[64,2048]{1,0:T(8,128)}, u32[]{:S(2)}, u32[]{:S(2)}) %collective-permute-start.1) | collective-permute-done | bytes 524320 | tf_op jit(solution)/shard_map/ppermute | solution.py:96
  42.2 2.9 %pad_maximum_fusion.1 = f32[4,64,2048]{2,1,0:T(8,128)} fusion(f32[1,64,2048]{2,1,0:T(8,128)} %bitcast.21, f32[1,64,2048]{2,1,0:T(8,128)} %bitcast.20, f32[1,64,2048]{2,1,0:T(8,128)} %bitcast.19, f32[1,64,2048]{2,1,0:T(8,128)S(1)} %bitcast.186), kind=kLoop, calls=%fused_computation.9 | loop fusion | flops 1572864 | bytes 4194304 | tf_op jit(solution)/shard_map/stack | solution.py:98
  45.1 3.6 %gather_fusion = f32[4,64,2048]{2,1,0:T(8,128)} fusion(f32[4,64,2048]{2,1,0:T(8,128)} %pad_maximum_fusion.1, s32[1024]{0:T(1024)S(1)} %pad_clamp_fusion), kind=kCustom, calls=%fused_computation | custom fusion | bytes 4194320 | tf_op jit(solution)/shard_map/jit(_take)/gather | solution.py:100
  48.7 2.9 %constant_dynamic-slice_fusion.6 = (f32[64,2048]{1,0:T(8,128)}, f32[64,2048]{1,0:T(8,128)}, f32[64,2048]{1,0:T(8,128)}, f32[64,2048]{1,0:T(8,128)}) fusion(f32[256,2048]{1,0:T(8,128)} %bitcast.192, s32[]{:T(128)S(6)} %select_n.102, s32[]{:T(128)S(6)} %select_n.105, s32[]{:T(128)S(6)} %select_n.104, s32[]{:T(128)S(6)} %select_n.103), kind=kLoop, calls=%fused_computation.121 | loop fusion | bytes 4194320 | tf_op jit(solution)/shard_map/dynamic_slice | solution.py:105
  53.0 2.4 %reshape.212 = f32[64,4,512]{2,1,0:T(4,128)} reshape(f32[64,2048]{1,0:T(8,128)} %get-tuple-element.15) | data formatting | bytes 1048576 | tf_op jit(solution)/shard_map/reshape | solution.py:58
  55.4 2.2 %reshape.211 = f32[64,4,512]{2,1,0:T(4,128)} reshape(f32[64,2048]{1,0:T(8,128)} %get-tuple-element.16) | data formatting | bytes 1048576 | tf_op jit(solution)/shard_map/reshape | solution.py:58
  57.6 2.2 %reshape.210 = f32[64,4,512]{2,1,0:T(4,128)} reshape(f32[64,2048]{1,0:T(8,128)} %get-tuple-element.17) | data formatting | bytes 1048576 | tf_op jit(solution)/shard_map/reshape | solution.py:58
  59.9 2.4 %multiply_reduce_fusion.3 = f32[4,64]{1,0:T(4,128)S(1)} fusion(f32[4,64,512]{2,0,1:T(4,128)} %copy.37, f32[1,4,64,512]{3,1,2,0:T(4,128)} %bitcast.196, f32[1,4,64,512]{3,1,2,0:T(4,128)} %bitcast.198, f32[1,4,64,512]{3,1,2,0:T(4,128)} %bitcast.200, f32[1,4,64,512]{3,1,2,0:T(4,128)S(1)} %bitcast.194), kind=kLoop, calls=%fused_computation.12 | loop fusion | flops 2621184 | bytes 2622464 | tf_op jit(solution)/shard_map/reduce_sum | solution.py:116
  62.3 5.4 %all-to-all-done = f32[8,136,512]{2,1,0:T(8,128)S(1)} async-done(((f32[8,136,512]{2,1,0:T(8,128)}), f32[8,136,512]{2,1,0:T(8,128)S(1)}, u32[]{:S(2)}, u32[]{:S(2)}) %all-to-all-start) | async-done | bytes 2228256 | tf_op jit(solution)/shard_map/all_to_all | solution.py:79
  68.2 3.0 %fusion.2 = f32[6,128,512]{2,1,0:T(8,128)S(1)} fusion(bf16[10,512,512]{2,1,0:T(8,128)(2,1)} %param.8, bf16[6,64,512]{2,1,0:T(8,128)(2,1)S(1)} %get-tuple-element.21, bf16[6,64,512]{2,1,0:T(8,128)(2,1)S(1)} %get-tuple-element.20), kind=kOutput, calls=%fused_computation.6 | convolution fusion | flops 404226048 | bytes 5505024 | tf_op jit(solution)/shard_map/dot_general | solution.py:21
  72.5 2.3 %reduce-precision_convert_fusion.2 = (bf16[4,64,512]{2,1,0:T(8,128)(2,1)}, f32[4,64,512]{2,1,0:T(8,128)S(1)}, f32[4,64,512]{2,1,0:T(8,128)S(1)}) fusion(f32[4,512]{1,0:T(4,128)S(1)} %multiply_add_fusion.1, f32[4,64,512]{2,1,0:T(8,128)S(1)} %multiply_reduce_fusion.1, f32[4,128,512]{2,1,0:T(8,128)S(1)} %copy-done.10, f32[]{:T(128)} %bitcast.2, ...), kind=kLoop, calls=%fused_computation.34 | loop fusion | flops 1179648 | bytes 3416072 | tf_op jit(solution)/shard_map/convert_element_type | solution.py:15
  77.6 4.5 %all-to-all-start.1 = ((f32[8,136,512]{2,1,0:T(8,128)}), f32[8,136,512]{2,1,0:T(8,128)}, u32[]{:S(2)}, u32[]{:S(2)}) async-start(f32[8,136,512]{2,1,0:T(8,128)} %bitcast.215), calls=%async_computation.1 | async-start | bytes 4456448 | tf_op jit(solution)/shard_map/all_to_all | solution.py:79
  82.4 3.5 %fusion.4 = f32[4,128,512]{2,1,0:T(8,128)} fusion(bf16[10,512,512]{2,1,0:T(8,128)(2,1)} %param.8, bf16[4,64,512]{2,1,0:T(8,128)(2,1)S(1)} %fusion.17, bf16[4,64,512]{2,1,0:T(8,128)(2,1)} %get-tuple-element.11), kind=kOutput, calls=%fused_computation.13 | convolution fusion | flops 269484032 | bytes 3670016 | tf_op jit(solution)/shard_map/dot_general | solution.py:21
  85.9 46.9 %all-to-all-done.1 = f32[8,136,512]{2,1,0:T(8,128)} async-done(((f32[8,136,512]{2,1,0:T(8,128)}), f32[8,136,512]{2,1,0:T(8,128)}, u32[]{:S(2)}, u32[]{:S(2)}) %all-to-all-start.1) | async-done | bytes 2228256 | tf_op jit(solution)/shard_map/all_to_all | solution.py:79
  133.9 1.8 %slice.216 = f32[8,128,512]{2,1,0:T(8,128)S(1)} slice(f32[8,136,512]{2,1,0:T(8,128)} %all-to-all-done.1), slice={[0:8], [0:128], [0:512]} | slice | bytes 4194304 | tf_op jit(solution)/shard_map/slice | solution.py:80
  136.0 3.0 %fusion = f32[6,128,512]{2,1,0:T(8,128)S(1)} fusion(bf16[10,512,512]{2,1,0:T(8,128)(2,1)} %param.8, bf16[6,64,512]{2,1,0:T(8,128)(2,1)S(1)} %get-tuple-element.19, bf16[6,64,512]{2,1,0:T(8,128)(2,1)S(1)} %get-tuple-element.18), kind=kOutput, calls=%fused_computation.4 | convolution fusion | flops 404226048 | bytes 5505024 | tf_op jit(solution)/shard_map/dot_general | solution.py:21
  140.9 1.8 %fusion.26 = (f32[4,64,512]{2,1,0:T(8,128)S(1)}, f32[4,64,512]{2,1,0:T(8,128)S(1)}) fusion(f32[4,64,512]{2,1,0:T(8,128)S(1)} %multiply_reduce_fusion, f32[4,128,512]{2,1,0:T(8,128)S(1)} %copy-done.13, f32[64]{0:T(128)S(1)} %get-tuple-element.34, f32[]{:T(128)} %bitcast.2, f32[]{:T(128)} %bitcast.1, f32[4,64,512]{2,1,0:T(8,128)S(1)} %copy-done.4, ...), kind=kLoop, calls=%fused_computation.49 | loop fusion | flops 1572864 | bytes 5251336 | tf_op jit(solution)/shard_map/add | solution.py:126
  146.0 3.6 %all-to-all-start.2 = ((f32[32,1,832]{2,1,0:T(1,128)}), f32[32,1,832]{2,1,0:T(1,128)S(1)}, u32[]{:S(2)}, u32[]{:S(2)}) async-start(f32[32,1,832]{2,1,0:T(1,128)} %reshape.236), calls=%async_computation.2 | async-start | bytes 229376 | tf_op jit(solution)/shard_map/all_to_all | solution.py:136
  149.6 8.0 %all-to-all-done.2 = f32[32,1,832]{2,1,0:T(1,128)S(1)} async-done(((f32[32,1,832]{2,1,0:T(1,128)}), f32[32,1,832]{2,1,0:T(1,128)S(1)}, u32[]{:S(2)}, u32[]{:S(2)}) %all-to-all-start.2) | async-done | bytes 106528 | tf_op jit(solution)/shard_map/all_to_all | solution.py:136
  (136 shorter events, 23.8 us)
Async XLA Ops:
  0.6 5.3 %copy-start = (f32[64,2048]{1,0:T(8,128)S(1)}, f32[64,2048]{1,0:T(8,128)}, u32[]{:S(2)}) copy-start(f32[64,2048]{1,0:T(8,128)} %param.6) | copy-start | bytes 1572868
  9.2 10.7 %copy-start.14 = (s32[10]{0:T(128)S(1)}, s32[10]{0:T(128)}, u32[]{:S(2)}) copy-start(s32[10]{0:T(128)} %param.10) | copy-start | bytes 124
  9.2 20.7 %copy-start.15 = (s32[10]{0:T(128)S(1)}, s32[10]{0:T(128)}, u32[]{:S(2)}) copy-start(s32[10]{0:T(128)} %param.9) | copy-start | bytes 124
  9.2 58.5 %all-to-all-start = ((f32[8,136,512]{2,1,0:T(8,128)}), f32[8,136,512]{2,1,0:T(8,128)S(1)}, u32[]{:S(2)}, u32[]{:S(2)}) async-start(f32[8,136,512]{2,1,0:T(8,128)} %pad_maximum_fusion), calls=%async_computation | async-start | bytes 4456448 | tf_op jit(solution)/shard_map/all_to_all | solution.py:79
  16.7 20.8 %collective-permute-start = (f32[64,2048]{1,0:T(8,128)S(1)}, f32[64,2048]{1,0:T(8,128)}, u32[]{:S(2)}, u32[]{:S(2)}) collective-permute-start(f32[64,2048]{1,0:T(8,128)S(1)} %copy-done), channel_id=1, source_target_pairs={{0,1},{1,2},{2,3},{3,0},{4,5},{5,6},{6,7},{7,4},{8,9},{9,10},{10,1... | collective-permute-start | bytes 1572872 | tf_op jit(solution)/shard_map/ppermute | solution.py:96
  16.7 20.8 %collective-permute-start.2 = (f32[64,2048]{1,0:T(8,128)S(1)}, f32[64,2048]{1,0:T(8,128)}, u32[]{:S(2)}, u32[]{:S(2)}) collective-permute-start(f32[64,2048]{1,0:T(8,128)S(1)} %copy-done), channel_id=1, source_target_pairs={{0,3},{1,0},{2,1},{3,2},{4,7},{5,4},{6,5},{7,6},{8,11},{9,8},{10,9... | collective-permute-start | bytes 1572872 | tf_op jit(solution)/shard_map/ppermute | solution.py:96
  18.4 23.8 %collective-permute-start.1 = (f32[64,2048]{1,0:T(8,128)S(1)}, f32[64,2048]{1,0:T(8,128)}, u32[]{:S(2)}, u32[]{:S(2)}) collective-permute-start(f32[64,2048]{1,0:T(8,128)S(1)} %copy-done), channel_id=1, source_target_pairs={{0,2},{1,3},{2,0},{3,1},{4,6},{5,7},{6,4},{7,5},{8,10},{9,11},{10,... | collective-permute-start | bytes 1572872 | tf_op jit(solution)/shard_map/ppermute | solution.py:96
  53.0 9.3 %copy-start.5 = (f32[64,4,512]{2,1,0:T(4,128)}, f32[64,4,512]{2,1,0:T(4,128)S(1)}, u32[]{:S(2)}) copy-start(f32[64,4,512]{2,1,0:T(4,128)S(1)} %reshape.209) | copy-start | bytes 1572868
  71.2 1.2 copy-start.10
  72.5 3.3 %copy-start.3 = (f32[4,64,512]{2,1,0:T(8,128)}, f32[4,64,512]{2,1,0:T(8,128)S(1)}, u32[]{:S(2)}) copy-start(f32[4,64,512]{2,1,0:T(8,128)S(1)} %multiply_reduce_fusion.1) | copy-start | bytes 1572868
  74.8 0.8 copy-start.1
  76.3 1.4 copy-start.12
  77.6 55.1 %all-to-all-start.1 = ((f32[8,136,512]{2,1,0:T(8,128)}), f32[8,136,512]{2,1,0:T(8,128)}, u32[]{:S(2)}, u32[]{:S(2)}) async-start(f32[8,136,512]{2,1,0:T(8,128)} %bitcast.215), calls=%async_computation.1 | async-start | bytes 4456448 | tf_op jit(solution)/shard_map/all_to_all | solution.py:79
  139.0 1.0 copy-start.2
  139.0 1.2 copy-start.4
  139.0 1.5 copy-start.11
  139.0 1.8 %copy-start.13 = (f32[4,128,512]{2,1,0:T(8,128)S(1)}, f32[4,128,512]{2,1,0:T(8,128)}, u32[]{:S(2)}) copy-start(f32[4,128,512]{2,1,0:T(8,128)} %fusion.4) | copy-start | bytes 3145732
  142.7 1.0 copy-start.6
  142.7 1.2 copy-start.7
  142.8 1.3 copy-start.8
  142.8 1.5 copy-start.9
  146.0 11.6 %all-to-all-start.2 = ((f32[32,1,832]{2,1,0:T(1,128)}), f32[32,1,832]{2,1,0:T(1,128)S(1)}, u32[]{:S(2)}, u32[]{:S(2)}) async-start(f32[32,1,832]{2,1,0:T(1,128)} %reshape.236), calls=%async_computation.2 | async-start | bytes 229376 | tf_op jit(solution)/shard_map/all_to_all | solution.py:136

commit v17 on v16

--- a/solution.py
+++ b/solution.py
@@ -62,6 +62,12 @@
 
     def exchange(x, extra, by_concat=False):
         width = x.shape[1]
+        if extra is None:
+            rolled = jnp.stack([jnp.roll(x, -t, axis=0) for t in range(NEED)], axis=1)
+            rolled = rolled.reshape(row_tiles, NEED * width, tile_size)
+            pieces = jnp.tile(rolled, (peers // row_tiles, 1, 1))
+            arrived = lax.all_to_all(pieces, "ind", split_axis=0, concat_axis=0, tiled=True)
+            return arrived.reshape(peers * NEED, width, tile_size), None
         flat = extra.reshape(-1)
         flat = jnp.pad(flat, (0, PAD_ROWS * tile_size - flat.shape[0]))
         if by_concat:
@@ -81,10 +87,13 @@
         sums = jnp.sum(arrived[:, NEED * width:].reshape(peers, -1)[:, :extra.size], axis=0)
         return tiles_in, sums.reshape(extra.shape)
 
-    def kprod(x, arrived):
+    def kprod(x, arrived, gather=False):
         width = x.shape[1]
-        picked = jnp.stack([lax.dynamic_index_in_dim(arrived, position[s], 0, keepdims=False)
-                            for s in range(off_count)])
+        if gather:
+            picked = jnp.take(arrived, position, axis=0, mode="clip")
+        else:
+            picked = jnp.stack([lax.dynamic_index_in_dim(arrived, position[s], 0, keepdims=False)
+                                for s in range(off_count)])
         near = batched_tile_dot(x, grm_tiles[:row_tiles])
         far = batched_tile_dot(picked, grm_tiles[row_tiles:])
         return near + jnp.sum(weight[:, :, None, None] * far[:, None], axis=0)
@@ -108,16 +117,16 @@
 
     def chunk(g, geno_sub):
         z0 = g / precond
-        tiles0, sums0 = exchange(z0, colsum(g * z0)[None])
-        rz0 = sums0[0]
-        kz0 = kprod(z0, tiles0)
+        tiles0, _ = exchange(z0, None)
+        kz0 = kprod(z0, tiles0, gather=True)
         image0 = tau0 * z0 + tau1 * kz0
         w = image0 / precond
         p0_local = jnp.sum(geno_sub * z0[None], axis=(1, 3))
-        extra1 = jnp.concatenate([colsum(z0 * image0)[None], p0_local], axis=0)
+        extra1 = jnp.concatenate([colsum(g * z0)[None], colsum(z0 * image0)[None], p0_local], axis=0)
         tiles1, sums1 = exchange(w, extra1, by_concat=True)
-        dad0 = sums1[0]
-        p0 = sums1[1:]
+        rz0 = sums1[0]
+        dad0 = sums1[1]
+        p0 = sums1[2:]
         alpha0 = rz0 / dad0
         resid1 = g - alpha0[None, :, None] * image0
         z1 = resid1 / precond

time: 162 us -> 157 us (0.969)
  waiting for transfers between devices: 65.1 us -> 73 us
  local copies, waits for them, and re-layouts: 30.6 us -> 24.2 us
  other arithmetic: 20.3 us -> 14.6 us
    ppermute x3, waiting for transfers between devices: 4.8 us -> 17.4 us  [local(): lax.ppermute(genotypes, 'var', [(j, (j + k) % nvar) for j in range(nvar)])]
    all_to_all x2, waiting for transfers between devices: 52.3 us -> 47.6 us  [exchange(): lax.all_to_all(pieces, 'ind', split_axis=0, concat_axis=0, tiled=True)]
    reshape x4, local copies, waits for them, and re-layouts: 8.25 us -> 4.96 us  [to_tiles(): return jnp.transpose(x.reshape(cols_here, row_tiles, tile_size), (1, 0, 2))]
    gather x0 -> x1, local copies, waits for them, and re-layouts: none -> 2.19 us  [kprod(): picked = jnp.take(arrived, position, axis=0, mode='clip')]
    slice x2 -> x1, local copies, waits for them, and re-layouts: 1.96 us -> 0.21 us  [exchange(): tiles_in = arrived[:, :NEED * width].reshape(peers * NEED, width, tile_size)]
    concatenate x2 -> x1, other arithmetic: 1.67 us -> 0.01 us  [chunk(): jnp.concatenate([colsum(g * z0)[None], colsum(z0 * image0)[None], p0_loca...]
    unnamed x71 -> x72, local copies, waits for them, and re-layouts: 7.52 us -> 6.39 us
  transfers between devices with their start and end apart: 6 -> 6, of which waited for: 4 -> 6; matrix products, arithmetic and copies ran while one was open for 18% -> 12% of each run, Pallas kernels for 0% -> 0%
where the time goes in v17:
time: 157 us; the launch traced here: 156 us
  waiting for transfers between devices  73 us (46%)
  local copies, waits for them, and re-layouts  24.2 us (15%)
  starting transfers between devices  18.1 us (12%)
  other arithmetic  14.6 us (9%)
  between operations  13.3 us (8%)
  matrix products  12.9 us (8%)
    all_to_all x2, waiting for transfers between devices, exchange(): lax.all_to_all(pieces, 'ind', split_axis=0, concat_axis=0, tiled=True)  47.6 us
    ppermute x3, waiting for transfers between devices, local(): lax.ppermute(genotypes, 'var', [(j, (j + k) % nvar) for j in range(nvar)])  17.4 us
    dot_general x4, matrix products, batched_tile_dot(): lax.dot_general(parts, tiles, (((2,), (2,)), ((0,), (0,))), preferred_ele...  12.9 us
    all_to_all x2, starting transfers between devices, exchange(): lax.all_to_all(pieces, 'ind', split_axis=0, concat_axis=0, tiled=True)  11.2 us
    all_to_all x1, waiting for transfers between devices, chunk(): lax.all_to_all(spread, ('ind', 'var'), split_axis=0, concat_axis=0, tiled...  7.98 us
    unnamed x72, local copies, waits for them, and re-layouts  6.39 us
    reshape x4, local copies, waits for them, and re-layouts, to_tiles(): return jnp.transpose(x.reshape(cols_here, row_tiles, tile_size), (1, 0, 2))  4.96 us
    all_to_all x1, starting transfers between devices, chunk(): lax.all_to_all(spread, ('ind', 'var'), split_axis=0, concat_axis=0, tiled...  3.62 us
  transfers between devices with their start and end apart: 6, of which 6 were waited for; matrix products, arithmetic and copies ran while one was open for 12% of the time, Pallas kernels for 0%

profile of v17, /device:TPU:0, one launch (start us, length us, event | category | flops | bytes accessed | tf_op | source)
XLA Modules:
  0.0 156.1 jit_solution(7267352174444894340)
XLA Ops:
  2.1 2.4 %select_reduce_fusion = f32[4,512]{1,0:T(4,128)S(1)} fusion(pred[512,512]{1,0:T(8,128)(4,1)S(1)} %iota_compare_fusion, bf16[10,512,512]{2,1,0:T(8,128)(2,1)} %param.8), kind=kLoop, calls=%fused_computation.2 | loop fusion | flops 3143680 | bytes 2367488 | tf_op jit(solution)/shard_map/reduce_sum | solution.py:45
  6.9 1.6 %tile.11 = f32[2,4,128,512]{3,2,1,0:T(8,128)} broadcast(f32[4,128,512]{2,1,0:T(8,128)S(1)} %bitcast.199), dimensions={1,2,3} | broadcast | bytes 3145728 | tf_op jit(solution)/shard_map/tile | solution.py:68
  8.5 7.4 %all-to-all-start = ((f32[8,128,512]{2,1,0:T(8,128)}), f32[8,128,512]{2,1,0:T(8,128)}, u32[]{:S(2)}, u32[]{:S(2)}) async-start(f32[8,128,512]{2,1,0:T(8,128)} %bitcast.7), calls=%async_computation | async-start | bytes 4194304 | tf_op jit(solution)/shard_map/all_to_all | solution.py:69
  15.9 1.7 %collective-permute-start.2 = (f32[64,2048]{1,0:T(8,128)S(1)}, f32[64,2048]{1,0:T(8,128)S(1)}, u32[]{:S(2)}, u32[]{:S(2)}) collective-permute-start(f32[64,2048]{1,0:T(8,128)S(1)} %copy-done), channel_id=1, source_target_pairs={{0,3},{1,0},{2,1},{3,2},{4,7},{5,4},{6,5},{7,6},{8,11},{9,8},{10,9... | collective-permute-start | bytes 1572872 | tf_op jit(solution)/shard_map/ppermute | solution.py:105
  17.7 1.5 collective-permute-start.1
  20.5 3.5 %fusion.6 = f32[4,128,512]{2,1,0:T(8,128)} fusion(bf16[10,512,512]{2,1,0:T(8,128)(2,1)} %param.8, bf16[4,64,512]{2,1,0:T(8,128)(2,1)} %get-tuple-element.25, bf16[4,64,512]{2,1,0:T(8,128)(2,1)S(1)} %get-tuple-element.24), kind=kOutput, calls=%fused_computation.15 | convolution fusion | flops 269484032 | bytes 3670016 | tf_op jit(solution)/shard_map/dot_general | solution.py:21
  24.0 4.4 %collective-permute-done = f32[64,2048]{1,0:T(8,128)S(1)} collective-permute-done((f32[64,2048]{1,0:T(8,128)S(1)}, f32[64,2048]{1,0:T(8,128)S(1)}, u32[]{:S(2)}, u32[]{:S(2)}) %collective-permute-start) | collective-permute-done | bytes 524320 | tf_op jit(solution)/shard_map/ppermute | solution.py:105
  28.3 1.7 %collective-permute-done.2 = f32[64,2048]{1,0:T(8,128)S(1)} collective-permute-done((f32[64,2048]{1,0:T(8,128)S(1)}, f32[64,2048]{1,0:T(8,128)S(1)}, u32[]{:S(2)}, u32[]{:S(2)}) %collective-permute-start.2) | collective-permute-done | bytes 524320 | tf_op jit(solution)/shard_map/ppermute | solution.py:105
  30.0 11.4 %collective-permute-done.1 = f32[64,2048]{1,0:T(8,128)S(1)} collective-permute-done((f32[64,2048]{1,0:T(8,128)S(1)}, f32[64,2048]{1,0:T(8,128)S(1)}, u32[]{:S(2)}, u32[]{:S(2)}) %collective-permute-start.1) | collective-permute-done | bytes 524320 | tf_op jit(solution)/shard_map/ppermute | solution.py:105
  41.4 1.5 pad_maximum_fusion
  42.9 2.3 %gather_fusion.1 = f32[4,64,2048]{2,1,0:T(8,128)S(1)} fusion(f32[4,64,2048]{2,1,0:T(8,128)} %pad_maximum_fusion, s32[1024]{0:T(1024)S(1)} %pad_clamp_fusion), kind=kCustom, calls=%fused_computation.1 | custom fusion | bytes 4194320 | tf_op jit(solution)/shard_map/jit(_take)/gather | solution.py:109
  48.0 1.6 %reshape.199 = f32[64,4,512]{2,1,0:T(4,128)S(1)} reshape(f32[64,2048]{1,0:T(8,128)} %get-tuple-element.17) | data formatting | bytes 1048576 | tf_op jit(solution)/shard_map/reshape | solution.py:58
  49.9 1.6 %reshape.197 = f32[64,4,512]{2,1,0:T(4,128)S(1)} reshape(f32[64,2048]{1,0:T(8,128)} %get-tuple-element.19) | data formatting | bytes 1048576 | tf_op jit(solution)/shard_map/reshape | solution.py:58
  52.5 11.8 %all-to-all-done = f32[8,128,512]{2,1,0:T(8,128)} async-done(((f32[8,128,512]{2,1,0:T(8,128)}), f32[8,128,512]{2,1,0:T(8,128)}, u32[]{:S(2)}, u32[]{:S(2)}) %all-to-all-start) | async-done | bytes 2097184 | tf_op jit(solution)/shard_map/all_to_all | solution.py:69
  64.3 2.2 %gather_fusion = f32[6,64,512]{2,1,0:T(8,128)S(1)} fusion(f32[16,64,512]{2,1,0:T(8,128)} %bitcast.8, s32[1024]{0:T(1024)S(1)} %pad_clamp_fusion.1), kind=kCustom, calls=%fused_computation | custom fusion | bytes 1572888 | tf_op jit(solution)/shard_map/jit(_take)/gather | solution.py:93
  66.6 3.0 %fusion.2 = f32[6,128,512]{2,1,0:T(8,128)S(1)} fusion(bf16[10,512,512]{2,1,0:T(8,128)(2,1)} %param.8, bf16[6,64,512]{2,1,0:T(8,128)(2,1)S(1)} %get-tuple-element.23, bf16[6,64,512]{2,1,0:T(8,128)(2,1)S(1)} %get-tuple-element.22), kind=kOutput, calls=%fused_computation.7 | convolution fusion | flops 404226048 | bytes 5505024 | tf_op jit(solution)/shard_map/dot_general | solution.py:21
  70.9 1.5 reduce-precision_convert_fusion.2
  75.3 3.8 %all-to-all-start.1 = ((f32[8,136,512]{2,1,0:T(8,128)}), f32[8,136,512]{2,1,0:T(8,128)S(1)}, u32[]{:S(2)}, u32[]{:S(2)}) async-start(f32[8,136,512]{2,1,0:T(8,128)} %bitcast.206), calls=%async_computation.1 | async-start | bytes 4456448 | tf_op jit(solution)/shard_map/all_to_all | solution.py:85
  91.0 3.4 %fusion.4 = f32[4,128,512]{2,1,0:T(8,128)} fusion(bf16[10,512,512]{2,1,0:T(8,128)(2,1)} %param.8, bf16[4,64,512]{2,1,0:T(8,128)(2,1)S(1)} %fusion.17, bf16[4,64,512]{2,1,0:T(8,128)(2,1)S(1)} %get-tuple-element.13), kind=kOutput, calls=%fused_computation.13 | convolution fusion | flops 269484032 | bytes 3670016 | tf_op jit(solution)/shard_map/dot_general | solution.py:21
  94.4 35.8 %all-to-all-done.1 = f32[8,136,512]{2,1,0:T(8,128)S(1)} async-done(((f32[8,136,512]{2,1,0:T(8,128)}), f32[8,136,512]{2,1,0:T(8,128)S(1)}, u32[]{:S(2)}, u32[]{:S(2)}) %all-to-all-start.1) | async-done | bytes 2228256 | tf_op jit(solution)/shard_map/all_to_all | solution.py:85
  131.0 3.0 %fusion = f32[6,128,512]{2,1,0:T(8,128)S(1)} fusion(bf16[10,512,512]{2,1,0:T(8,128)(2,1)} %param.8, bf16[6,64,512]{2,1,0:T(8,128)(2,1)S(1)} %get-tuple-element.21, bf16[6,64,512]{2,1,0:T(8,128)(2,1)S(1)} %get-tuple-element.20), kind=kOutput, calls=%fused_computation.5 | convolution fusion | flops 404226048 | bytes 5505024 | tf_op jit(solution)/shard_map/dot_general | solution.py:21
  135.9 1.8 %fusion.26 = (f32[4,64,512]{2,1,0:T(8,128)S(1)}, f32[4,64,512]{2,1,0:T(8,128)S(1)}) fusion(f32[4,64,512]{2,1,0:T(8,128)S(1)} %multiply_reduce_fusion, f32[4,128,512]{2,1,0:T(8,128)S(1)} %copy-done.17, f32[64]{0:T(128)S(1)} %get-tuple-element.35, f32[]{:T(128)} %bitcast.2, f32[]{:T(128)} %bitcast, f32[4,64,512]{2,1,0:T(8,128)S(1)} %copy-done.4, ...), kind=kLoop, calls=%fused_computation.49 | loop fusion | flops 1572864 | bytes 5251336 | tf_op jit(solution)/shard_map/add | solution.py:135
  141.0 3.6 %all-to-all-start.2 = ((f32[32,1,832]{2,1,0:T(1,128)}), f32[32,1,832]{2,1,0:T(1,128)S(1)}, u32[]{:S(2)}, u32[]{:S(2)}) async-start(f32[32,1,832]{2,1,0:T(1,128)} %reshape.232), calls=%async_computation.2 | async-start | bytes 229376 | tf_op jit(solution)/shard_map/all_to_all | solution.py:145
  144.6 8.0 %all-to-all-done.2 = f32[32,1,832]{2,1,0:T(1,128)S(1)} async-done(((f32[32,1,832]{2,1,0:T(1,128)}), f32[32,1,832]{2,1,0:T(1,128)S(1)}, u32[]{:S(2)}, u32[]{:S(2)}) %all-to-all-start.2) | async-done | bytes 106528 | tf_op jit(solution)/shard_map/all_to_all | solution.py:145
  (132 shorter events, 22.5 us)
Async XLA Ops:
  0.6 5.1 %copy-start = (f32[64,2048]{1,0:T(8,128)S(1)}, f32[64,2048]{1,0:T(8,128)}, u32[]{:S(2)}) copy-start(f32[64,2048]{1,0:T(8,128)} %param.6) | copy-start | bytes 1572868
  8.5 11.7 %copy-start.18 = (s32[10]{0:T(128)S(1)}, s32[10]{0:T(128)}, u32[]{:S(2)}) copy-start(s32[10]{0:T(128)} %param.9) | copy-start | bytes 124
  8.5 11.8 %copy-start.19 = (s32[10]{0:T(128)S(1)}, s32[10]{0:T(128)}, u32[]{:S(2)}) copy-start(s32[10]{0:T(128)} %param.10) | copy-start | bytes 124
  8.5 55.8 %all-to-all-start = ((f32[8,128,512]{2,1,0:T(8,128)}), f32[8,128,512]{2,1,0:T(8,128)}, u32[]{:S(2)}, u32[]{:S(2)}) async-start(f32[8,128,512]{2,1,0:T(8,128)} %bitcast.7), calls=%async_computation | async-start | bytes 4194304 | tf_op jit(solution)/shard_map/all_to_all | solution.py:69
  15.9 12.4 %collective-permute-start = (f32[64,2048]{1,0:T(8,128)S(1)}, f32[64,2048]{1,0:T(8,128)S(1)}, u32[]{:S(2)}, u32[]{:S(2)}) collective-permute-start(f32[64,2048]{1,0:T(8,128)S(1)} %copy-done), channel_id=1, source_target_pairs={{0,1},{1,2},{2,3},{3,0},{4,5},{5,6},{6,7},{7,4},{8,9},{9,10},{10,1... | collective-permute-start | bytes 1572872 | tf_op jit(solution)/shard_map/ppermute | solution.py:105
  15.9 14.1 %collective-permute-start.2 = (f32[64,2048]{1,0:T(8,128)S(1)}, f32[64,2048]{1,0:T(8,128)S(1)}, u32[]{:S(2)}, u32[]{:S(2)}) collective-permute-start(f32[64,2048]{1,0:T(8,128)S(1)} %copy-done), channel_id=1, source_target_pairs={{0,3},{1,0},{2,1},{3,2},{4,7},{5,4},{6,5},{7,6},{8,11},{9,8},{10,9... | collective-permute-start | bytes 1572872 | tf_op jit(solution)/shard_map/ppermute | solution.py:105
  17.7 23.7 %collective-permute-start.1 = (f32[64,2048]{1,0:T(8,128)S(1)}, f32[64,2048]{1,0:T(8,128)S(1)}, u32[]{:S(2)}, u32[]{:S(2)}) collective-permute-start(f32[64,2048]{1,0:T(8,128)S(1)} %copy-done), channel_id=1, source_target_pairs={{0,2},{1,3},{2,0},{3,1},{4,6},{5,7},{6,4},{7,5},{8,10},{9,11},{10,... | collective-permute-start | bytes 1572872 | tf_op jit(solution)/shard_map/ppermute | solution.py:105
  46.5 3.1 %copy-start.16 = (f32[64,2048]{1,0:T(8,128)S(1)}, f32[64,2048]{1,0:T(8,128)}, u32[]{:S(2)}) copy-start(f32[64,2048]{1,0:T(8,128)} %get-tuple-element.18) | copy-start | bytes 1572868
  48.0 4.5 %copy-start.5 = (f32[64,4,512]{2,1,0:T(4,128)}, f32[64,4,512]{2,1,0:T(4,128)S(1)}, u32[]{:S(2)}) copy-start(f32[64,4,512]{2,1,0:T(4,128)S(1)} %reshape.196) | copy-start | bytes 1572868
  49.6 2.9 %copy-start.7 = (f32[64,4,512]{2,1,0:T(4,128)}, f32[64,4,512]{2,1,0:T(4,128)S(1)}, u32[]{:S(2)}) copy-start(f32[64,4,512]{2,1,0:T(4,128)S(1)} %reshape.199) | copy-start | bytes 1572868
  49.9 16.5 %copy-start.9 = (f32[64,4,512]{2,1,0:T(4,128)}, f32[64,4,512]{2,1,0:T(4,128)S(1)}, u32[]{:S(2)}) copy-start(f32[64,4,512]{2,1,0:T(4,128)S(1)} %reshape.198) | copy-start | bytes 1572868
  51.5 15.1 %copy-start.11 = (f32[64,4,512]{2,1,0:T(4,128)}, f32[64,4,512]{2,1,0:T(4,128)S(1)}, u32[]{:S(2)}) copy-start(f32[64,4,512]{2,1,0:T(4,128)S(1)} %reshape.197) | copy-start | bytes 1572868
  69.6 1.2 copy-start.13
  70.9 2.5 %copy-start.3 = (f32[4,64,512]{2,1,0:T(8,128)}, f32[4,64,512]{2,1,0:T(8,128)S(1)}, u32[]{:S(2)}) copy-start(f32[4,64,512]{2,1,0:T(8,128)S(1)} %multiply_reduce_fusion.1) | copy-start | bytes 1572868
  73.9 1.4 copy-start.15
  75.3 54.9 %all-to-all-start.1 = ((f32[8,136,512]{2,1,0:T(8,128)}), f32[8,136,512]{2,1,0:T(8,128)S(1)}, u32[]{:S(2)}, u32[]{:S(2)}) async-start(f32[8,136,512]{2,1,0:T(8,128)} %bitcast.206), calls=%async_computation.1 | async-start | bytes 4456448 | tf_op jit(solution)/shard_map/all_to_all | solution.py:85
  134.1 1.2 copy-start.4
  134.1 1.5 copy-start.14
  134.1 1.8 %copy-start.17 = (f32[4,128,512]{2,1,0:T(8,128)S(1)}, f32[4,128,512]{2,1,0:T(8,128)}, u32[]{:S(2)}) copy-start(f32[4,128,512]{2,1,0:T(8,128)} %fusion.4) | copy-start | bytes 3145732
  137.7 1.0 copy-start.6
  137.7 1.2 copy-start.8
  137.7 1.3 copy-start.10
  137.7 1.5 copy-start.12
  141.0 11.6 %all-to-all-start.2 = ((f32[32,1,832]{2,1,0:T(1,128)}), f32[32,1,832]{2,1,0:T(1,128)S(1)}, u32[]{:S(2)}, u32[]{:S(2)}) async-start(f32[32,1,832]{2,1,0:T(1,128)} %reshape.232), calls=%async_computation.2 | async-start | bytes 229376 | tf_op jit(solution)/shard_map/all_to_all | solution.py:145
  (2 other events, 1.8 us)

commit v18 on v17

--- a/solution.py
+++ b/solution.py
@@ -90,7 +90,9 @@
     def kprod(x, arrived, gather=False):
         width = x.shape[1]
         if gather:
-            picked = jnp.take(arrived, position, axis=0, mode="clip")
+            pick = (position[:, None] == jnp.arange(arrived.shape[0], dtype=jnp.int32)[None, :])
+            picked = jnp.einsum("sk,kct->sct", pick.astype(jnp.float32), arrived,
+                                precision=lax.Precision.HIGHEST)
         else:
             picked = jnp.stack([lax.dynamic_index_in_dim(arrived, position[s], 0, keepdims=False)
                                 for s in range(off_count)])

time: 157 us -> 158 us (level)
  waiting for transfers between devices: 73 us -> 63.2 us
  local copies, waits for them, and re-layouts: 24.2 us -> 28.9 us
  other arithmetic: 14.6 us -> 18.5 us
  matrix products: 12.9 us -> 15.4 us
    all_to_all x2, waiting for transfers between devices: 47.6 us -> 38.6 us  [exchange(): lax.all_to_all(pieces, 'ind', split_axis=0, concat_axis=0, tiled=True)]
    reshape x4, local copies, waits for them, and re-layouts: 4.96 us -> 8.13 us  [to_tiles(): return jnp.transpose(x.reshape(cols_here, row_tiles, tile_size), (1, 0, 2))]
    gather x1 -> x0, local copies, waits for them, and re-layouts: 2.19 us -> none  [kprod(): picked = jnp.take(arrived, position, axis=0, mode='clip')]
    dot_general x0 -> x1, matrix products: none -> 2.14 us  [kprod(): jnp.einsum('sk,kct->sct', pick.astype(jnp.float32), arrived, precision=la...]
    convert_element_type x5 -> x4, other arithmetic: 2.71 us -> 3.42 us  [split2(): return (hi.astype(jnp.bfloat16), lo.astype(jnp.bfloat16))]
    unnamed x72 -> x64, local copies, waits for them, and re-layouts: 6.39 us -> 6.41 us
  transfers between devices with their start and end apart: 6 -> 6, of which waited for: 6 -> 6; matrix products, arithmetic and copies ran while one was open for 12% -> 19% of each run, Pallas kernels for 0% -> 0%
where the time goes in v18:
time: 158 us; the launch traced here: 157 us
  waiting for transfers between devices  63.2 us (40%)
  local copies, waits for them, and re-layouts  28.9 us (18%)
  other arithmetic  18.5 us (12%)
  starting transfers between devices  18.1 us (11%)
  matrix products  15.4 us (10%)
  between operations  13 us (8%)
    all_to_all x2, waiting for transfers between devices, exchange(): lax.all_to_all(pieces, 'ind', split_axis=0, concat_axis=0, tiled=True)  38.6 us
    ppermute x3, waiting for transfers between devices, local(): lax.ppermute(genotypes, 'var', [(j, (j + k) % nvar) for j in range(nvar)])  16.6 us
    dot_general x4, matrix products, batched_tile_dot(): lax.dot_general(parts, tiles, (((2,), (2,)), ((0,), (0,))), preferred_ele...  13.2 us
    all_to_all x2, starting transfers between devices, exchange(): lax.all_to_all(pieces, 'ind', split_axis=0, concat_axis=0, tiled=True)  11.2 us
    reshape x4, local copies, waits for them, and re-layouts, to_tiles(): return jnp.transpose(x.reshape(cols_here, row_tiles, tile_size), (1, 0, 2))  8.13 us
    all_to_all x1, waiting for transfers between devices, chunk(): lax.all_to_all(spread, ('ind', 'var'), split_axis=0, concat_axis=0, tiled...  7.98 us
    unnamed x64, local copies, waits for them, and re-layouts  6.41 us
    all_to_all x1, starting transfers between devices, chunk(): lax.all_to_all(spread, ('ind', 'var'), split_axis=0, concat_axis=0, tiled...  3.63 us
  transfers between devices with their start and end apart: 6, of which 6 were waited for; matrix products, arithmetic and copies ran while one was open for 19% of the time, Pallas kernels for 0%

profile of v18, /device:TPU:0, one launch (start us, length us, event | category | flops | bytes accessed | tf_op | source)
XLA Modules:
  0.0 157.0 jit_solution(8423348058511005344)
XLA Ops:
  2.1 2.4 %select_reduce_fusion = f32[4,512]{1,0:T(4,128)S(1)} fusion(pred[512,512]{1,0:T(8,128)(4,1)S(1)} %iota_compare_fusion, bf16[10,512,512]{2,1,0:T(8,128)(2,1)} %param.8), kind=kLoop, calls=%fused_computation.1 | loop fusion | flops 3143680 | bytes 2367488 | tf_op jit(solution)/shard_map/reduce_sum | solution.py:45
  8.7 7.4 %all-to-all-start = ((f32[8,128,512]{2,1,0:T(8,128)}), f32[8,128,512]{2,1,0:T(8,128)S(1)}, u32[]{:S(2)}, u32[]{:S(2)}) async-start(f32[8,128,512]{2,1,0:T(8,128)} %bitcast.196), calls=%async_computation | async-start | bytes 4194304 | tf_op jit(solution)/shard_map/all_to_all | solution.py:69
  16.1 1.7 %collective-permute-start.2 = (f32[64,2048]{1,0:T(8,128)S(1)}, f32[64,2048]{1,0:T(8,128)}, u32[]{:S(2)}, u32[]{:S(2)}) collective-permute-start(f32[64,2048]{1,0:T(8,128)S(1)} %copy-done), channel_id=1, source_target_pairs={{0,3},{1,0},{2,1},{3,2},{4,7},{5,4},{6,5},{7,6},{8,11},{9,8},{10,9... | collective-permute-start | bytes 1572872 | tf_op jit(solution)/shard_map/ppermute | solution.py:107
  21.5 3.6 %fusion.8 = f32[4,128,512]{2,1,0:T(8,128)} fusion(bf16[10,512,512]{2,1,0:T(8,128)(2,1)} %param.8, bf16[4,64,512]{2,1,0:T(8,128)(2,1)} %get-tuple-element.25, bf16[4,64,512]{2,1,0:T(8,128)(2,1)} %get-tuple-element.24), kind=kOutput, calls=%fused_computation.16 | convolution fusion | flops 269484032 | bytes 3670016 | tf_op jit(solution)/shard_map/dot_general | solution.py:21
  25.0 3.6 %collective-permute-done = f32[64,2048]{1,0:T(8,128)} collective-permute-done((f32[64,2048]{1,0:T(8,128)S(1)}, f32[64,2048]{1,0:T(8,128)}, u32[]{:S(2)}, u32[]{:S(2)}) %collective-permute-start) | collective-permute-done | bytes 524320 | tf_op jit(solution)/shard_map/ppermute | solution.py:107
  30.2 11.5 %collective-permute-done.1 = f32[64,2048]{1,0:T(8,128)} collective-permute-done((f32[64,2048]{1,0:T(8,128)S(1)}, f32[64,2048]{1,0:T(8,128)}, u32[]{:S(2)}, u32[]{:S(2)}) %collective-permute-start.1) | collective-permute-done | bytes 524320 | tf_op jit(solution)/shard_map/ppermute | solution.py:107
  41.7 2.9 %pad_maximum_fusion = f32[4,64,2048]{2,1,0:T(8,128)} fusion(f32[1,64,2048]{2,1,0:T(8,128)} %bitcast.17, f32[1,64,2048]{2,1,0:T(8,128)} %bitcast.16, f32[1,64,2048]{2,1,0:T(8,128)} %bitcast.15, f32[1,64,2048]{2,1,0:T(8,128)S(1)} %bitcast.189), kind=kLoop, calls=%fused_computation.8 | loop fusion | flops 1572864 | bytes 4194304 | tf_op jit(solution)/shard_map/stack | solution.py:109
  44.6 3.6 %gather_fusion = f32[4,64,2048]{2,1,0:T(8,128)} fusion(f32[4,64,2048]{2,1,0:T(8,128)} %pad_maximum_fusion, s32[1024]{0:T(1024)S(1)} %pad_clamp_fusion), kind=kCustom, calls=%fused_computation | custom fusion | bytes 4194320 | tf_op jit(solution)/shard_map/jit(_take)/gather | solution.py:111
  48.2 2.9 %constant_dynamic-slice_fusion.6 = (f32[64,2048]{1,0:T(8,128)}, f32[64,2048]{1,0:T(8,128)}, f32[64,2048]{1,0:T(8,128)}, f32[64,2048]{1,0:T(8,128)}) fusion(f32[256,2048]{1,0:T(8,128)} %bitcast.197, s32[]{:T(128)S(6)} %select_n.90, s32[]{:T(128)S(6)} %select_n.93, s32[]{:T(128)S(6)} %select_n.92, s32[]{:T(128)S(6)} %select_n.91), kind=kLoop, calls=%fused_computation.120 | loop fusion | bytes 4194320 | tf_op jit(solution)/shard_map/dynamic_slice | solution.py:116
  52.5 2.4 %reshape.200 = f32[64,4,512]{2,1,0:T(4,128)} reshape(f32[64,2048]{1,0:T(8,128)} %get-tuple-element.17) | data formatting | bytes 1048576 | tf_op jit(solution)/shard_map/reshape | solution.py:58
  54.8 2.2 %reshape.199 = f32[64,4,512]{2,1,0:T(4,128)} reshape(f32[64,2048]{1,0:T(8,128)} %get-tuple-element.18) | data formatting | bytes 1048576 | tf_op jit(solution)/shard_map/reshape | solution.py:58
  57.0 2.2 %reshape.198 = f32[64,4,512]{2,1,0:T(4,128)} reshape(f32[64,2048]{1,0:T(8,128)} %get-tuple-element.19) | data formatting | bytes 1048576 | tf_op jit(solution)/shard_map/reshape | solution.py:58
  59.2 2.4 %multiply_reduce_fusion.3 = f32[4,64]{1,0:T(4,128)S(1)} fusion(f32[4,64,512]{2,0,1:T(4,128)} %copy.46, f32[1,4,64,512]{3,1,2,0:T(4,128)} %bitcast.200, f32[1,4,64,512]{3,1,2,0:T(4,128)} %bitcast.202, f32[1,4,64,512]{3,1,2,0:T(4,128)} %bitcast.204, f32[1,4,64,512]{3,1,2,0:T(4,128)S(1)} %bitcast.198), kind=kLoop, calls=%fused_computation.13 | loop fusion | flops 2621184 | bytes 2622464 | tf_op jit(solution)/shard_map/reduce_sum | solution.py:126
  61.6 2.7 %all-to-all-done = f32[8,128,512]{2,1,0:T(8,128)S(1)} async-done(((f32[8,128,512]{2,1,0:T(8,128)}), f32[8,128,512]{2,1,0:T(8,128)S(1)}, u32[]{:S(2)}, u32[]{:S(2)}) %all-to-all-start) | async-done | bytes 2097184 | tf_op jit(solution)/shard_map/all_to_all | solution.py:69
  64.4 2.1 %reduce-precision_convert_fusion = (bf16[6,64,512]{2,0,1:T(8,128)(2,1)S(1)}, bf16[6,64,512]{2,0,1:T(8,128)(2,1)S(1)}) fusion(f32[16,64,512]{2,1,0:T(8,128)S(1)} %bitcast.195, s32[6]{0:T(128)S(1)} %fusion.66), kind=kOutput, calls=%fused_computation.19 | convolution fusion | flops 38535264 | bytes 2883608 | tf_op jit(solution)/shard_map/sk,kct->sct/dot_general | solution.py:94
  66.7 3.1 %fusion.2 = f32[6,128,512]{2,1,0:T(8,128)S(1)} fusion(bf16[10,512,512]{2,1,0:T(8,128)(2,1)} %param.8, bf16[6,128,512]{2,0,1:T(8,128)(2,1)S(1)} %pad_maximum_fusion.3), kind=kOutput, calls=%fused_computation.6 | convolution fusion | flops 402653184 | bytes 5505024 | tf_op jit(solution)/shard_map/dot_general | solution.py:21
  71.1 2.2 %reduce-precision_convert_fusion.2 = (bf16[4,64,512]{2,1,0:T(8,128)(2,1)}, f32[4,64,512]{2,1,0:T(8,128)S(1)}, f32[4,64,512]{2,1,0:T(8,128)S(1)}) fusion(f32[4,512]{1,0:T(4,128)S(1)} %multiply_add_fusion.1, f32[4,64,512]{2,1,0:T(8,128)S(1)} %multiply_reduce_fusion.1, f32[4,128,512]{2,1,0:T(8,128)S(1)} %copy-done.10, f32[]{:T(128)} %bitcast.2, ...), kind=kLoop, calls=%fused_computation.34 | loop fusion | flops 1179648 | bytes 3416072 | tf_op jit(solution)/shard_map/convert_element_type | solution.py:15
  76.2 3.8 %all-to-all-start.1 = ((f32[8,136,512]{2,1,0:T(8,128)}), f32[8,136,512]{2,1,0:T(8,128)S(1)}, u32[]{:S(2)}, u32[]{:S(2)}) async-start(f32[8,136,512]{2,1,0:T(8,128)} %bitcast.213), calls=%async_computation.1 | async-start | bytes 4456448 | tf_op jit(solution)/shard_map/all_to_all | solution.py:85
  91.8 3.5 %fusion.6 = f32[4,128,512]{2,1,0:T(8,128)} fusion(bf16[10,512,512]{2,1,0:T(8,128)(2,1)} %param.8, bf16[4,64,512]{2,1,0:T(8,128)(2,1)S(1)} %fusion.17, bf16[4,64,512]{2,1,0:T(8,128)(2,1)} %get-tuple-element.13), kind=kOutput, calls=%fused_computation.14 | convolution fusion | flops 269484032 | bytes 3670016 | tf_op jit(solution)/shard_map/dot_general | solution.py:21
  95.3 35.9 %all-to-all-done.1 = f32[8,136,512]{2,1,0:T(8,128)S(1)} async-done(((f32[8,136,512]{2,1,0:T(8,128)}), f32[8,136,512]{2,1,0:T(8,128)S(1)}, u32[]{:S(2)}, u32[]{:S(2)}) %all-to-all-start.1) | async-done | bytes 2228256 | tf_op jit(solution)/shard_map/all_to_all | solution.py:85
  131.9 3.0 %fusion = f32[6,128,512]{2,1,0:T(8,128)S(1)} fusion(bf16[10,512,512]{2,1,0:T(8,128)(2,1)} %param.8, bf16[6,64,512]{2,1,0:T(8,128)(2,1)S(1)} %get-tuple-element.23, bf16[6,64,512]{2,1,0:T(8,128)(2,1)S(1)} %get-tuple-element.22), kind=kOutput, calls=%fused_computation.4 | convolution fusion | flops 404226048 | bytes 5505024 | tf_op jit(solution)/shard_map/dot_general | solution.py:21
  136.8 1.8 %fusion.26 = (f32[4,64,512]{2,1,0:T(8,128)S(1)}, f32[4,64,512]{2,1,0:T(8,128)S(1)}) fusion(f32[4,64,512]{2,1,0:T(8,128)S(1)} %multiply_reduce_fusion, f32[4,128,512]{2,1,0:T(8,128)S(1)} %copy-done.13, f32[64]{0:T(128)S(1)} %get-tuple-element.35, f32[]{:T(128)} %bitcast.2, f32[]{:T(128)} %bitcast, f32[4,64,512]{2,1,0:T(8,128)S(1)} %copy-done.4, ...), kind=kLoop, calls=%fused_computation.49 | loop fusion | flops 1572864 | bytes 5251336 | tf_op jit(solution)/shard_map/add | solution.py:137
  141.9 3.6 %all-to-all-start.2 = ((f32[32,1,832]{2,1,0:T(1,128)}), f32[32,1,832]{2,1,0:T(1,128)S(1)}, u32[]{:S(2)}, u32[]{:S(2)}) async-start(f32[32,1,832]{2,1,0:T(1,128)} %reshape.225), calls=%async_computation.2 | async-start | bytes 229376 | tf_op jit(solution)/shard_map/all_to_all | solution.py:147
  145.6 8.0 %all-to-all-done.2 = f32[32,1,832]{2,1,0:T(1,128)S(1)} async-done(((f32[32,1,832]{2,1,0:T(1,128)}), f32[32,1,832]{2,1,0:T(1,128)S(1)}, u32[]{:S(2)}, u32[]{:S(2)}) %all-to-all-start.2) | async-done | bytes 106528 | tf_op jit(solution)/shard_map/all_to_all | solution.py:147
  (123 shorter events, 25.5 us)
Async XLA Ops:
  0.6 5.2 %copy-start = (f32[64,2048]{1,0:T(8,128)S(1)}, f32[64,2048]{1,0:T(8,128)}, u32[]{:S(2)}) copy-start(f32[64,2048]{1,0:T(8,128)} %param.6) | copy-start | bytes 1572868
  8.7 12.5 %copy-start.14 = (s32[10]{0:T(128)S(1)}, s32[10]{0:T(128)}, u32[]{:S(2)}) copy-start(s32[10]{0:T(128)} %param.9) | copy-start | bytes 124
  8.7 12.7 %copy-start.15 = (s32[10]{0:T(128)S(1)}, s32[10]{0:T(128)}, u32[]{:S(2)}) copy-start(s32[10]{0:T(128)} %param.10) | copy-start | bytes 124
  8.7 55.7 %all-to-all-start = ((f32[8,128,512]{2,1,0:T(8,128)}), f32[8,128,512]{2,1,0:T(8,128)S(1)}, u32[]{:S(2)}, u32[]{:S(2)}) async-start(f32[8,128,512]{2,1,0:T(8,128)} %bitcast.196), calls=%async_computation | async-start | bytes 4194304 | tf_op jit(solution)/shard_map/all_to_all | solution.py:69
  16.1 12.5 %collective-permute-start = (f32[64,2048]{1,0:T(8,128)S(1)}, f32[64,2048]{1,0:T(8,128)}, u32[]{:S(2)}, u32[]{:S(2)}) collective-permute-start(f32[64,2048]{1,0:T(8,128)S(1)} %copy-done), channel_id=1, source_target_pairs={{0,1},{1,2},{2,3},{3,0},{4,5},{5,6},{6,7},{7,4},{8,9},{9,10},{10,1... | collective-permute-start | bytes 1572872 | tf_op jit(solution)/shard_map/ppermute | solution.py:107
  16.1 14.1 %collective-permute-start.2 = (f32[64,2048]{1,0:T(8,128)S(1)}, f32[64,2048]{1,0:T(8,128)}, u32[]{:S(2)}, u32[]{:S(2)}) collective-permute-start(f32[64,2048]{1,0:T(8,128)S(1)} %copy-done), channel_id=1, source_target_pairs={{0,3},{1,0},{2,1},{3,2},{4,7},{5,4},{6,5},{7,6},{8,11},{9,8},{10,9... | collective-permute-start | bytes 1572872 | tf_op jit(solution)/shard_map/ppermute | solution.py:107
  17.9 23.8 %collective-permute-start.1 = (f32[64,2048]{1,0:T(8,128)S(1)}, f32[64,2048]{1,0:T(8,128)}, u32[]{:S(2)}, u32[]{:S(2)}) collective-permute-start(f32[64,2048]{1,0:T(8,128)S(1)} %copy-done), channel_id=1, source_target_pairs={{0,2},{1,3},{2,0},{3,1},{4,6},{5,7},{6,4},{7,5},{8,10},{9,11},{10,... | collective-permute-start | bytes 1572872 | tf_op jit(solution)/shard_map/ppermute | solution.py:107
  52.5 9.2 %copy-start.5 = (f32[64,4,512]{2,1,0:T(4,128)}, f32[64,4,512]{2,1,0:T(4,128)S(1)}, u32[]{:S(2)}) copy-start(f32[64,4,512]{2,1,0:T(4,128)S(1)} %reshape.197) | copy-start | bytes 1572868
  69.8 1.2 copy-start.10
  71.1 3.2 %copy-start.3 = (f32[4,64,512]{2,1,0:T(8,128)}, f32[4,64,512]{2,1,0:T(8,128)S(1)}, u32[]{:S(2)}) copy-start(f32[4,64,512]{2,1,0:T(8,128)S(1)} %multiply_reduce_fusion.1) | copy-start | bytes 1572868
  73.3 0.8 copy-start.1
  74.8 1.4 copy-start.12
  76.2 54.9 %all-to-all-start.1 = ((f32[8,136,512]{2,1,0:T(8,128)}), f32[8,136,512]{2,1,0:T(8,128)S(1)}, u32[]{:S(2)}, u32[]{:S(2)}) async-start(f32[8,136,512]{2,1,0:T(8,128)} %bitcast.213), calls=%async_computation.1 | async-start | bytes 4456448 | tf_op jit(solution)/shard_map/all_to_all | solution.py:85
  135.0 1.0 copy-start.2
  135.0 1.2 copy-start.4
  135.0 1.5 copy-start.11
  135.0 1.8 %copy-start.13 = (f32[4,128,512]{2,1,0:T(8,128)S(1)}, f32[4,128,512]{2,1,0:T(8,128)}, u32[]{:S(2)}) copy-start(f32[4,128,512]{2,1,0:T(8,128)} %fusion.6) | copy-start | bytes 3145732
  138.6 1.0 copy-start.6
  138.6 1.2 copy-start.7
  138.7 1.3 copy-start.8
  138.7 1.5 copy-start.9
  141.9 11.6 %all-to-all-start.2 = ((f32[32,1,832]{2,1,0:T(1,128)}), f32[32,1,832]{2,1,0:T(1,128)S(1)}, u32[]{:S(2)}, u32[]{:S(2)}) async-start(f32[32,1,832]{2,1,0:T(1,128)} %reshape.225), calls=%async_computation.2 | async-start | bytes 229376 | tf_op jit(solution)/shard_map/all_to_all | solution.py:147
